TPU v7x, 128 devices: a whole 4x4x4 slice. The times are simulated.
128 devices in a mesh: sect: 4 (over y), blk: 32 (over x, z, core).
Axes of the slice: x: 4, y: 4, z: 4, core: 2. Of those that a mesh axis runs over, the one named last changes fastest.
Arguments:
- theta: bfloat16 [4, 4096, 2048], P('sect', 'blk'), may hold values from -6 to 6
- left_env: bfloat16 [4, 8, 4096, 4096], P('sect', None, 'blk'), may hold values from -0.125 to 0.125
- sector_ids: int32 [4, 4096], P('sect'), may hold values from 0 to 15, never falling along the last dimension, each value on 1 to 2560 neighbouring positions
- local_ops: float32 [4, 8, 16, 16], P('sect'), may hold values from -0.5 to 0.5
- edge_env: float32 [128, 128], replicated, may hold values from -0.5 to 0.5
Outputs:
- updated: bfloat16 [4, 4096, 2048], P('sect', 'blk')
- outgoing: float32 [4, 128, 128], P('sect')
Inputs may be any that keep to these rules, and one draw needn't show every extreme that they name: `sector_ids`: within each section the sector numbers never fall along the rows; each sector holds 1 to 2560 rows and one holds exactly 2560.
All inputs are finite; a program needn't handle non-finite values.
Results may differ from a plain program's by a relative error of at most 0.00165.
Values may be sent and summed in bfloat16 or wider, within the bound.
No kernel may reach another device: no remote copies, remote signals or barrier semaphores. Data moves between devices by JAX's collectives and lax.ppermute only.
A program may use at most 128 MiB of HBM per device.

v0:
```python
import jax
import jax.numpy as jnp
from jax import lax
from jax.sharding import PartitionSpec as P


def shifted(array, axis, by):
    peers = lax.axis_size(axis)
    pairs = [(i, i + by) for i in range(peers) if 0 <= i + by < peers]
    return lax.ppermute(array, axis, pairs)


def matprod(first, second):
    return jnp.dot(first, second, precision=lax.Precision.HIGHEST)


def per_device(theta, left_env, sector_ids, local_ops, edge_env):
    rows_dev = theta.shape[1]
    width = theta.shape[2]
    chain_w = left_env.shape[1]
    phys = local_ops.shape[2]
    cols = width // phys
    theta_loc = theta[0]
    env_loc = left_env[0]
    sec_all = sector_ids[0]
    ops_loc = local_ops[0]
    my_block = lax.axis_index("blk")
    row_start = my_block * rows_dev
    my_sec = lax.dynamic_slice_in_dim(sec_all, row_start, rows_dev, 0)
    same = my_sec[:, None] == sec_all[None, :]
    masked = jnp.where(same[None, :, :], env_loc, jnp.zeros_like(env_loc))
    applied = jnp.einsum(
        "wij,jx->wix",
        masked,
        lax.all_gather(theta_loc, "blk", axis=0, tiled=True),
        preferred_element_type=jnp.float32,
    )
    applied = applied.reshape(chain_w, rows_dev, phys, cols)
    acted = jnp.einsum("wpq,wiqc->ipc", ops_loc, applied, precision=lax.Precision.HIGHEST)
    theta_f = theta_loc.astype(jnp.float32).reshape(rows_dev, phys, cols)
    partial_intersection = jnp.einsum(
        "ipc,ipd->cd", theta_f, acted, precision=lax.Precision.HIGHEST
    )
    intersection = lax.psum(partial_intersection, "blk")
    transfer = (
        intersection
        * jnp.sqrt(jnp.float32(cols))
        / jnp.sqrt(jnp.sum(intersection * intersection) + 1e-06)
    )
    sect_no = lax.axis_index("sect")
    incoming = edge_env
    for step_no in range(lax.axis_size("sect") - 1):
        leaving = matprod(incoming, transfer)
        passed = shifted(leaving, "sect", 1)
        incoming = jnp.where(sect_no == 0, edge_env, passed)
    outgoing = matprod(incoming, transfer)
    result = jnp.einsum("ipc,cd->ipd", acted, incoming, precision=lax.Precision.HIGHEST)
    updated = result.reshape(1, rows_dev, width).astype(jnp.bfloat16)
    return (updated, outgoing[None])


def solution(mesh):
    placed = (
        P("sect", "blk", None),
        P("sect", None, "blk", None),
        P("sect", None),
        P("sect", None, None, None),
        P(),
    )
    return jax.shard_map(
        per_device,
        mesh=mesh,
        in_specs=placed,
        out_specs=(P("sect", "blk", None), P("sect", None, None)),
        check_vma=False,
    )
```

profile of v0, /device:TPU:0, one launch (start us, length us, event | category | flops | bytes accessed | tf_op | source)
XLA Modules:
  0.0 270.4 jit_solution(17785318184022447140)
XLA Ops:
  7.2 0.7 all-gather.3.cloned.1.call-update
  7.9 0.0 all-reduce.2.cloned.1.call-start
  8.0 1.1 copy.21
  9.1 0.7 dynamic-slice_bitcast_fusion
  9.8 1.1 broadcast_compare_fusion
  10.9 74.6 %all-gather.3.cloned.1.call-done = bf16[1,4096,2048]{2,1,0:T(8,128)(2,1)} async-done(((bf16[1,128,2048]{2,1,0:T(8,128)(2,1)}), bf16[1,4096,2048]{2,1,0:T(8,128)(2,1)}) %all-gather.3.cloned.1.call-update) | async-done | bytes 16777232 | tf_op jit(solution)/shard_map/all_gather | solution.py:35
  85.4 15.1 %copy.20 = bf16[512,8,16,128]{3,2,1,0:T(8,128)(2,1)} copy(bf16[512,8,16,128]{3,1,2,0:T(8,128)(2,1)} %bitcast.44) | data formatting | bytes 33554432
  100.5 25.4 %fusion = f32[8,128,16,128]{3,1,2,0:T(8,128)} fusion(bf16[16,128,4096,1]{1,0,2,3:T(8,128)(2,1)} %bitcast.45, bf16[1,8,128,4096]{3,2,1,0:T(8,128)(2,1)} %param.6, pred[128,4096]{1,0:T(8,128)(4,1)S(1)} %broadcast_compare_fusion), kind=kOutput, calls=%fused_computation | convolution fusion | flops 17184063488 | bytes 34078720 | tf_op jit(solution)/shard_map/wij,jx->wix/dot_general | solution.py:32
  126.0 12.4 %fusion.8 = f32[128,16,128]{2,1,0:T(8,128)S(1)} fusion(f32[8,128,16,128]{3,1,2,0:T(8,128)} %fusion, f32[1,8,16,16]{3,2,1,0:T(8,128)S(1)} %copy-done), kind=kOutput, calls=%fused_computation.8 | convolution fusion | flops 402653184 | bytes 9445376 | tf_op jit(solution)/shard_map/wpq,wiqc->ipc/dot_general | solution.py:39
  138.4 1.6 convolution_bitcast_fusion
  140.0 96.2 %all-reduce.2.cloned.1.call-done = f32[128,128]{0,1:T(8,128)} async-done(((f32[128,128]{0,1:T(8,128)}), f32[128,128]{0,1:T(8,128)}) %all-reduce.2.cloned.1.call-update) | async-done | bytes 65552 | tf_op jit(solution)/shard_map/psum | solution.py:44
  236.2 1.5 multiply_reduce_fusion
  238.4 1.1 convolution_bitcast_fusion.2
  239.5 3.4 %collective-permute-start = (f32[128,128]{1,0:T(8,128)S(1)}, f32[128,128]{1,0:T(8,128)S(1)}, u32[]{:S(2)}, u32[]{:S(2)}) collective-permute-start(f32[128,128]{1,0:T(8,128)S(1)} %convolution_bitcast_fusion.2), channel_id=1, source_target_pairs={{0,32},{32,64},{64,96},{1,33},{33,65},{65,97},{2,34},{34,66},{66,9... | collective-permute-start | bytes 196616 | tf_op jit(solution)/shard_map/ppermute | solution.py:10
  242.9 1.9 collective-permute-done
  244.8 1.1 fusion.16
  245.9 4.3 %collective-permute-start.1 = (f32[128,128]{1,0:T(8,128)S(1)}, f32[128,128]{1,0:T(8,128)S(1)}, u32[]{:S(2)}, u32[]{:S(2)}) collective-permute-start(f32[128,128]{1,0:T(8,128)S(1)} %fusion.16), channel_id=1, source_target_pairs={{0,32},{32,64},{64,96},{1,33},{33,65},{65,97},{2,34},{34,66},{66,9... | collective-permute-start | bytes 196616 | tf_op jit(solution)/shard_map/ppermute | solution.py:10
  250.3 1.9 collective-permute-done.1
  252.1 1.1 fusion.14
  253.3 4.3 %collective-permute-start.2 = (f32[128,128]{1,0:T(8,128)S(1)}, f32[128,128]{1,0:T(8,128)S(1)}, u32[]{:S(2)}, u32[]{:S(2)}) collective-permute-start(f32[128,128]{1,0:T(8,128)S(1)} %fusion.14), channel_id=1, source_target_pairs={{0,32},{32,64},{64,96},{1,33},{33,65},{65,97},{2,34},{34,66},{66,9... | collective-permute-start | bytes 196616 | tf_op jit(solution)/shard_map/ppermute | solution.py:10
  257.5 1.9 collective-permute-done.2
  259.4 1.4 convolution_convert_fusion
  260.8 1.0 copy.11
  261.8 1.7 convolution_bitcast_fusion.1
  (6 shorter events, 0.1 us)
Async XLA Ops:
  7.2 118.8 %copy-start = (f32[1,8,16,16]{3,2,1,0:T(8,128)S(1)}, f32[1,8,16,16]{3,2,1,0:T(8,128)}, u32[]{:S(2)}) copy-start(f32[1,8,16,16]{3,2,1,0:T(8,128)} %param.8) | copy-start | bytes 24580
  7.2 78.3 %all-gather.3.cloned.1.call-start = ((), (), s32[]{:S(2)}) async-start(), calls=%async_computation.1 | async-start | bytes 17301504 | tf_op jit(solution)/shard_map/all_gather | solution.py:35
  7.9 228.3 %all-reduce.2.cloned.1.call-start = ((), (), s32[]{:S(2)}) async-start(), calls=%async_computation | async-start | bytes 131072 | tf_op jit(solution)/shard_map/psum | solution.py:44
  126.0 112.4 %copy-start.1 = (f32[128,128]{1,0:T(8,128)S(1)}, f32[128,128]{1,0:T(8,128)}, u32[]{:S(2)}) copy-start(f32[128,128]{1,0:T(8,128)} %param.9) | copy-start | bytes 196612
  239.5 5.3 %collective-permute-start = (f32[128,128]{1,0:T(8,128)S(1)}, f32[128,128]{1,0:T(8,128)S(1)}, u32[]{:S(2)}, u32[]{:S(2)}) collective-permute-start(f32[128,128]{1,0:T(8,128)S(1)} %convolution_bitcast_fusion.2), channel_id=1, source_target_pairs={{0,32},{32,64},{64,96},{1,33},{33,65},{65,97},{2,34},{34,66},{66,9... | collective-permute-start | bytes 196616 | tf_op jit(solution)/shard_map/ppermute | solution.py:10
  245.9 6.2 %collective-permute-start.1 = (f32[128,128]{1,0:T(8,128)S(1)}, f32[128,128]{1,0:T(8,128)S(1)}, u32[]{:S(2)}, u32[]{:S(2)}) collective-permute-start(f32[128,128]{1,0:T(8,128)S(1)} %fusion.16), channel_id=1, source_target_pairs={{0,32},{32,64},{64,96},{1,33},{33,65},{65,97},{2,34},{34,66},{66,9... | collective-permute-start | bytes 196616 | tf_op jit(solution)/shard_map/ppermute | solution.py:10
  253.3 6.2 %collective-permute-start.2 = (f32[128,128]{1,0:T(8,128)S(1)}, f32[128,128]{1,0:T(8,128)S(1)}, u32[]{:S(2)}, u32[]{:S(2)}) collective-permute-start(f32[128,128]{1,0:T(8,128)S(1)} %fusion.14), channel_id=1, source_target_pairs={{0,32},{32,64},{64,96},{1,33},{33,65},{65,97},{2,34},{34,66},{66,9... | collective-permute-start | bytes 196616 | tf_op jit(solution)/shard_map/ppermute | solution.py:10
Sparse Core Ops, SparseCore 0:
  10.2 75.1 all-gather.2
  140.1 96.0 all-reduce.1
where the time goes:
time: 272 us; the launch traced here: 270 us
  waiting for transfers between devices  177 us (65%)
  matrix products  45.9 us (17%)
  local copies, waits for them, and re-layouts  17.9 us (7%)
  between operations  14.8 us (5%)
  starting transfers between devices  12.1 us (4%)
    psum x1, waiting for transfers between devices, per_device(): intersection = lax.psum(partial_intersection, 'blk')  96.2 us
    all_gather x1, waiting for transfers between devices, per_device(): lax.all_gather(theta_loc, 'blk', axis=0, tiled=True)  74.6 us
    dot_general x1, matrix products, per_device(): jnp.einsum('wij,jx->wix', masked, lax.all_gather(theta_loc, 'blk', axis=0...  25.4 us
    unnamed x7, local copies, waits for them, and re-layouts  17.2 us
    dot_general x1, matrix products, per_device(): jnp.einsum('wpq,wiqc->ipc', ops_loc, applied, precision=lax.Precision.HIG...  12.4 us
    ppermute x3, starting transfers between devices, shifted(): return lax.ppermute(array, axis, pairs)  12 us
    ppermute x3, waiting for transfers between devices, shifted(): return lax.ppermute(array, axis, pairs)  5.65 us
  transfers between devices with their start and end apart: 5, of which 5 were waited for; matrix products, arithmetic and copies ran while one was open for 1% of the time, Pallas kernels for 0%

commit v1 on v0

--- a/solution.py
+++ b/solution.py
@@ -4,14 +4,30 @@
 from jax.sharding import PartitionSpec as P
 
 
-def shifted(array, axis, by):
-    peers = lax.axis_size(axis)
-    pairs = [(i, i + by) for i in range(peers) if 0 <= i + by < peers]
-    return lax.ppermute(array, axis, pairs)
+def matprod(first, second):
+    return jnp.dot(first, second, precision=lax.Precision.HIGHEST)
 
 
-def matprod(first, second):
-    return jnp.dot(first, second, precision=lax.Precision.HIGHEST)
+def butterfly_sum(value, axis):
+    peers = lax.axis_size(axis)
+    step = 1
+    while step < peers:
+        pairs = [(i, i ^ step) for i in range(peers)]
+        value = value + lax.ppermute(value, axis, pairs)
+        step *= 2
+    return value
+
+
+def gather_all(value, axis):
+    peers = lax.axis_size(axis)
+    me = lax.axis_index(axis)
+    parts = [value]
+    for shift in range(1, peers):
+        pairs = [(i, (i + shift) % peers) for i in range(peers)]
+        parts.append(lax.ppermute(value, axis, pairs))
+    stacked = jnp.stack(parts)
+    order = (me - jnp.arange(peers)) % peers
+    return jnp.zeros_like(stacked).at[order].set(stacked)
 
 
 def per_device(theta, left_env, sector_ids, local_ops, edge_env):
@@ -41,19 +57,20 @@
     partial_intersection = jnp.einsum(
         "ipc,ipd->cd", theta_f, acted, precision=lax.Precision.HIGHEST
     )
-    intersection = lax.psum(partial_intersection, "blk")
+    intersection = butterfly_sum(partial_intersection, "blk")
     transfer = (
         intersection
         * jnp.sqrt(jnp.float32(cols))
         / jnp.sqrt(jnp.sum(intersection * intersection) + 1e-06)
     )
+    transfers = gather_all(transfer, "sect")
     sect_no = lax.axis_index("sect")
-    incoming = edge_env
-    for step_no in range(lax.axis_size("sect") - 1):
-        leaving = matprod(incoming, transfer)
-        passed = shifted(leaving, "sect", 1)
-        incoming = jnp.where(sect_no == 0, edge_env, passed)
-    outgoing = matprod(incoming, transfer)
+    prefix = [edge_env]
+    for step_no in range(lax.axis_size("sect")):
+        prefix.append(matprod(prefix[-1], transfers[step_no]))
+    prefix = jnp.stack(prefix)
+    incoming = prefix[sect_no]
+    outgoing = prefix[sect_no + 1]
     result = jnp.einsum("ipc,cd->ipd", acted, incoming, precision=lax.Precision.HIGHEST)
     updated = result.reshape(1, rows_dev, width).astype(jnp.bfloat16)
     return (updated, outgoing[None])

time: 272 us -> 184 us (0.68)
  waiting for transfers between devices: 177 us -> 93.1 us
  matrix products: 45.9 us -> 41.3 us
    psum x1 -> x0, waiting for transfers between devices: 96.2 us -> none  [per_device(): intersection = lax.psum(partial_intersection, 'blk')]
    ppermute x3 -> x8, waiting for transfers between devices: 5.65 us -> 17.8 us  [the longest x5 13 us: butterfly_sum(): value = value + lax.ppermute(value, axis, pairs)]
    dot_general x4, matrix products: 5.07 us -> 1.06 us  [matprod(): return jnp.dot(first, second, precision=lax.Precision.HIGHEST)]
    ppermute x3 -> x8, starting transfers between devices: 12 us -> 13.1 us  [the longest x5 8.58 us: butterfly_sum(): value = value + lax.ppermute(value, axis, pairs)]
    unnamed x7 -> x12, local copies, waits for them, and re-layouts: 17.2 us -> 18.1 us
  transfers between devices with their start and end apart: 5 -> 9, of which waited for: 5 -> 9; matrix products, arithmetic and copies ran while one was open for 1% -> 2% of each run, Pallas kernels for 0% -> 0%
where the time goes in v1:
time: 184 us
  waiting for transfers between devices  93.1 us (51%)
  matrix products  41.3 us (22%)
  local copies, waits for them, and re-layouts  19.7 us (11%)
  between operations  14.9 us (8%)
  starting transfers between devices  13.1 us (7%)
    all_gather x1, waiting for transfers between devices, per_device(): lax.all_gather(theta_loc, 'blk', axis=0, tiled=True)  74.6 us
    dot_general x1, matrix products, per_device(): jnp.einsum('wij,jx->wix', masked, lax.all_gather(theta_loc, 'blk', axis=0...  25.5 us
    unnamed x12, local copies, waits for them, and re-layouts  18.1 us
    ppermute x5, waiting for transfers between devices, butterfly_sum(): value = value + lax.ppermute(value, axis, pairs)  13 us
    dot_general x1, matrix products, per_device(): jnp.einsum('wpq,wiqc->ipc', ops_loc, applied, precision=lax.Precision.HIG...  12.4 us
    ppermute x5, starting transfers between devices, butterfly_sum(): value = value + lax.ppermute(value, axis, pairs)  8.58 us
    ppermute x3, waiting for transfers between devices, gather_all(): parts.append(lax.ppermute(value, axis, pairs))  4.77 us
    ppermute x3, starting transfers between devices, gather_all(): parts.append(lax.ppermute(value, axis, pairs))  4.5 us
  transfers between devices with their start and end apart: 9, of which 9 were waited for; matrix products, arithmetic and copies ran while one was open for 2% of the time, Pallas kernels for 0%

profile of v1, /device:TPU:0, one launch (start us, length us, event | category | flops | bytes accessed | tf_op | source)
XLA Modules:
  0.0 183.9 jit_solution(11128533183710162262)
XLA Ops:
  7.9 1.1 copy.34
  9.7 1.1 broadcast_compare_fusion
  10.8 74.6 %all-gather.3.cloned.1.call-done = bf16[1,4096,2048]{2,1,0:T(8,128)(2,1)} async-done(((bf16[1,128,2048]{2,1,0:T(8,128)(2,1)}), bf16[1,4096,2048]{2,1,0:T(8,128)(2,1)}) %all-gather.3.cloned.1.call-update) | async-done | bytes 16777232 | tf_op jit(solution)/shard_map/all_gather | solution.py:51
  85.4 15.1 %copy.33 = bf16[512,8,16,128]{3,2,1,0:T(8,128)(2,1)} copy(bf16[512,8,16,128]{3,1,2,0:T(8,128)(2,1)} %bitcast.78) | data formatting | bytes 33554432
  100.5 25.5 %fusion = f32[8,128,16,128]{3,1,2,0:T(8,128)} fusion(bf16[16,128,4096,1]{1,0,2,3:T(8,128)(2,1)} %bitcast.79, bf16[1,8,128,4096]{3,2,1,0:T(8,128)(2,1)} %param.6, pred[128,4096]{1,0:T(8,128)(4,1)S(1)} %broadcast_compare_fusion), kind=kOutput, calls=%fused_computation.1 | convolution fusion | flops 17184063488 | bytes 34078720 | tf_op jit(solution)/shard_map/wij,jx->wix/dot_general | solution.py:48
  126.0 12.4 %fusion.8 = f32[128,16,128]{2,1,0:T(8,128)S(1)} fusion(f32[8,128,16,128]{3,1,2,0:T(8,128)} %fusion, f32[1,8,16,16]{3,2,1,0:T(8,128)S(1)} %copy-done), kind=kOutput, calls=%fused_computation.9 | convolution fusion | flops 402653184 | bytes 9445376 | tf_op jit(solution)/shard_map/wpq,wiqc->ipc/dot_general | solution.py:55
  138.4 1.0 convolution_bitcast_fusion
  139.7 1.0 collective-permute-done
  140.7 1.0 collective-permute-start.1
  141.7 3.3 %collective-permute-done.1 = f32[128,128]{0,1:T(8,128)S(1)} collective-permute-done((f32[128,128]{0,1:T(8,128)S(1)}, f32[128,128]{0,1:T(8,128)S(1)}, u32[]{:S(2)}, u32[]{:S(2)}) %collective-permute-start.1) | collective-permute-done | bytes 65568 | tf_op jit(solution)/shard_map/ppermute | solution.py:16
  145.1 2.6 %collective-permute-start.2 = (f32[128,128]{0,1:T(8,128)S(1)}, f32[128,128]{0,1:T(8,128)S(1)}, u32[]{:S(2)}, u32[]{:S(2)}) collective-permute-start(f32[128,128]{0,1:T(8,128)S(1)} %add.59), channel_id=1, source_target_pairs={{0,4},{1,5},{2,6},{3,7},{4,0},{5,1},{6,2},{7,3},{8,12},{9,13},{10,... | collective-permute-start | bytes 196616 | tf_op jit(solution)/shard_map/ppermute | solution.py:16
  147.7 3.2 %collective-permute-done.2 = f32[128,128]{0,1:T(8,128)S(1)} collective-permute-done((f32[128,128]{0,1:T(8,128)S(1)}, f32[128,128]{0,1:T(8,128)S(1)}, u32[]{:S(2)}, u32[]{:S(2)}) %collective-permute-start.2) | collective-permute-done | bytes 65568 | tf_op jit(solution)/shard_map/ppermute | solution.py:16
  150.9 1.6 collective-permute-start.3
  152.6 2.7 %collective-permute-done.3 = f32[128,128]{0,1:T(8,128)S(1)} collective-permute-done((f32[128,128]{0,1:T(8,128)S(1)}, f32[128,128]{0,1:T(8,128)S(1)}, u32[]{:S(2)}, u32[]{:S(2)}) %collective-permute-start.3) | collective-permute-done | bytes 65568 | tf_op jit(solution)/shard_map/ppermute | solution.py:16
  155.3 3.1 %collective-permute-start.4 = (f32[128,128]{0,1:T(8,128)S(1)}, f32[128,128]{0,1:T(8,128)S(1)}, u32[]{:S(2)}, u32[]{:S(2)}) collective-permute-start(f32[128,128]{0,1:T(8,128)S(1)} %add.61), channel_id=1, source_target_pairs={{0,16},{1,17},{2,18},{3,19},{4,20},{5,21},{6,22},{7,23},{8,24},{9,... | collective-permute-start | bytes 196616 | tf_op jit(solution)/shard_map/ppermute | solution.py:16
  158.4 2.8 %collective-permute-done.4 = f32[128,128]{0,1:T(8,128)S(1)} collective-permute-done((f32[128,128]{0,1:T(8,128)S(1)}, f32[128,128]{0,1:T(8,128)S(1)}, u32[]{:S(2)}, u32[]{:S(2)}) %collective-permute-start.4) | collective-permute-done | bytes 65568 | tf_op jit(solution)/shard_map/ppermute | solution.py:16
  162.5 2.8 %collective-permute-start.7 = (f32[128,128]{0,1:T(8,128)S(1)}, f32[128,128]{0,1:T(8,128)S(1)}, u32[]{:S(2)}, u32[]{:S(2)}) collective-permute-start(f32[128,128]{0,1:T(8,128)S(1)} %multiply_divide_fusion), channel_id=1, source_target_pairs={{0,96},{32,0},{64,32},{96,64},{1,97},{33,1},{65,33},{97,65},{2,98}... | collective-permute-start | bytes 196616 | tf_op jit(solution)/shard_map/ppermute | solution.py:27
  165.3 0.8 collective-permute-start.6
  166.1 0.9 collective-permute-start.5
  167.2 3.9 %collective-permute-done.6 = f32[128,128]{0,1:T(8,128)S(1)} collective-permute-done((f32[128,128]{0,1:T(8,128)S(1)}, f32[128,128]{0,1:T(8,128)S(1)}, u32[]{:S(2)}, u32[]{:S(2)}) %collective-permute-start.6) | collective-permute-done | bytes 65568 | tf_op jit(solution)/shard_map/ppermute | solution.py:27
  171.1 0.7 collective-permute-done.5
  173.9 1.4 convolution_convert_fusion
  175.3 1.0 copy.24
  176.3 0.7 copy.25
  (31 shorter events, 4.8 us)
Async XLA Ops:
  7.2 118.8 %copy-start = (f32[1,8,16,16]{3,2,1,0:T(8,128)S(1)}, f32[1,8,16,16]{3,2,1,0:T(8,128)}, u32[]{:S(2)}) copy-start(f32[1,8,16,16]{3,2,1,0:T(8,128)} %param.8) | copy-start | bytes 24580
  7.2 78.3 %all-gather.3.cloned.1.call-start = ((), (), s32[]{:S(2)}) async-start(), calls=%async_computation | async-start | bytes 17301504 | tf_op jit(solution)/shard_map/all_gather | solution.py:51
  126.0 26.5 %copy-start.1 = (f32[128,128]{1,0:T(8,128)S(1)}, f32[128,128]{1,0:T(8,128)}, u32[]{:S(2)}) copy-start(f32[128,128]{1,0:T(8,128)} %param.9) | copy-start | bytes 196612
  139.4 1.3 collective-permute-start
  140.7 4.3 %collective-permute-start.1 = (f32[128,128]{0,1:T(8,128)S(1)}, f32[128,128]{0,1:T(8,128)S(1)}, u32[]{:S(2)}, u32[]{:S(2)}) collective-permute-start(f32[128,128]{0,1:T(8,128)S(1)} %add.58), channel_id=1, source_target_pairs={{0,2},{1,3},{2,0},{3,1},{4,6},{5,7},{6,4},{7,5},{8,10},{9,11},{10,... | collective-permute-start | bytes 196616 | tf_op jit(solution)/shard_map/ppermute | solution.py:16
  145.1 5.8 %collective-permute-start.2 = (f32[128,128]{0,1:T(8,128)S(1)}, f32[128,128]{0,1:T(8,128)S(1)}, u32[]{:S(2)}, u32[]{:S(2)}) collective-permute-start(f32[128,128]{0,1:T(8,128)S(1)} %add.59), channel_id=1, source_target_pairs={{0,4},{1,5},{2,6},{3,7},{4,0},{5,1},{6,2},{7,3},{8,12},{9,13},{10,... | collective-permute-start | bytes 196616 | tf_op jit(solution)/shard_map/ppermute | solution.py:16
  150.9 4.3 %collective-permute-start.3 = (f32[128,128]{0,1:T(8,128)S(1)}, f32[128,128]{0,1:T(8,128)S(1)}, u32[]{:S(2)}, u32[]{:S(2)}) collective-permute-start(f32[128,128]{0,1:T(8,128)S(1)} %add.60), channel_id=1, source_target_pairs={{0,8},{1,9},{2,10},{3,11},{4,12},{5,13},{6,14},{7,15},{8,0},{9,1},... | collective-permute-start | bytes 196616 | tf_op jit(solution)/shard_map/ppermute | solution.py:16
  155.3 5.8 %collective-permute-start.4 = (f32[128,128]{0,1:T(8,128)S(1)}, f32[128,128]{0,1:T(8,128)S(1)}, u32[]{:S(2)}, u32[]{:S(2)}) collective-permute-start(f32[128,128]{0,1:T(8,128)S(1)} %add.61), channel_id=1, source_target_pairs={{0,16},{1,17},{2,18},{3,19},{4,20},{5,21},{6,22},{7,23},{8,24},{9,... | collective-permute-start | bytes 196616 | tf_op jit(solution)/shard_map/ppermute | solution.py:16
  162.5 4.7 %collective-permute-start.7 = (f32[128,128]{0,1:T(8,128)S(1)}, f32[128,128]{0,1:T(8,128)S(1)}, u32[]{:S(2)}, u32[]{:S(2)}) collective-permute-start(f32[128,128]{0,1:T(8,128)S(1)} %multiply_divide_fusion), channel_id=1, source_target_pairs={{0,96},{32,0},{64,32},{96,64},{1,97},{33,1},{65,33},{97,65},{2,98}... | collective-permute-start | bytes 196616 | tf_op jit(solution)/shard_map/ppermute | solution.py:27
  165.3 5.8 %collective-permute-start.6 = (f32[128,128]{0,1:T(8,128)S(1)}, f32[128,128]{0,1:T(8,128)S(1)}, u32[]{:S(2)}, u32[]{:S(2)}) collective-permute-start(f32[128,128]{0,1:T(8,128)S(1)} %multiply_divide_fusion), channel_id=1, source_target_pairs={{0,64},{32,96},{64,0},{96,32},{1,65},{33,97},{65,1},{97,33},{2,66}... | collective-permute-start | bytes 196616 | tf_op jit(solution)/shard_map/ppermute | solution.py:27
  166.1 5.7 %collective-permute-start.5 = (f32[128,128]{0,1:T(8,128)S(1)}, f32[128,128]{0,1:T(8,128)S(1)}, u32[]{:S(2)}, u32[]{:S(2)}) collective-permute-start(f32[128,128]{0,1:T(8,128)S(1)} %multiply_divide_fusion), channel_id=1, source_target_pairs={{0,32},{32,64},{64,96},{96,0},{1,33},{33,65},{65,97},{97,1},{2,34}... | collective-permute-start | bytes 196616 | tf_op jit(solution)/shard_map/ppermute | solution.py:27
Sparse Core Ops, SparseCore 0:
  10.2 75.1 all-gather.2

commit v2 on v1

--- a/solution.py
+++ b/solution.py
@@ -1,7 +1,13 @@
+import functools
+
 import jax
 import jax.numpy as jnp
 from jax import lax
+from jax.experimental import pallas as pl
+from jax.experimental.pallas import tpu as pltpu
 from jax.sharding import PartitionSpec as P
+
+K_TILE = 512
 
 
 def matprod(first, second):
@@ -30,6 +36,54 @@
     return jnp.zeros_like(stacked).at[order].set(stacked)
 
 
+def masked_apply_kernel(span_ref, env_ref, theta_ref, sec_j_ref, sec_i_ref, out_ref):
+    step = pl.program_id(0)
+
+    @pl.when(step == 0)
+    def _():
+        out_ref[...] = jnp.zeros_like(out_ref)
+
+    @pl.when(span_ref[0] + step <= span_ref[1])
+    def _():
+        same = sec_i_ref[...] == sec_j_ref[...]
+        block = theta_ref[...]
+        for w in range(out_ref.shape[0]):
+            env_w = jnp.where(same, env_ref[w], jnp.zeros_like(env_ref[w]))
+            out_ref[w] += jnp.dot(env_w, block, preferred_element_type=jnp.float32)
+
+
+def masked_apply(env_loc, theta_all, sec_all, my_sec):
+    chain_w, rows_dev, depth = env_loc.shape
+    width = theta_all.shape[1]
+    tiles = depth // K_TILE
+    first = jnp.sum((sec_all < my_sec[0]).astype(jnp.int32))
+    last = jnp.sum((sec_all <= my_sec[-1]).astype(jnp.int32)) - 1
+    span = jnp.stack([first // K_TILE, last // K_TILE]).astype(jnp.int32)
+
+    def tile_of(step, span_ref):
+        return jnp.minimum(span_ref[0] + step, span_ref[1])
+
+    grid_spec = pltpu.PrefetchScalarGridSpec(
+        num_scalar_prefetch=1,
+        grid=(tiles,),
+        in_specs=[
+            pl.BlockSpec((chain_w, rows_dev, K_TILE), lambda k, s: (0, 0, tile_of(k, s))),
+            pl.BlockSpec((K_TILE, width), lambda k, s: (tile_of(k, s), 0)),
+            pl.BlockSpec((1, K_TILE), lambda k, s: (0, tile_of(k, s))),
+            pl.BlockSpec((rows_dev, 1), lambda k, s: (0, 0)),
+        ],
+        out_specs=pl.BlockSpec((chain_w, rows_dev, width), lambda k, s: (0, 0, 0)),
+    )
+    return pl.pallas_call(
+        masked_apply_kernel,
+        grid_spec=grid_spec,
+        out_shape=jax.ShapeDtypeStruct((chain_w, rows_dev, width), jnp.float32),
+        compiler_params=pltpu.CompilerParams(
+            dimension_semantics=("arbitrary",), vmem_limit_bytes=48 * 1024 * 1024
+        ),
+    )(span, env_loc, theta_all, sec_all.reshape(1, depth), my_sec.reshape(rows_dev, 1))
+
+
 def per_device(theta, left_env, sector_ids, local_ops, edge_env):
     rows_dev = theta.shape[1]
     width = theta.shape[2]
@@ -43,19 +97,13 @@
     my_block = lax.axis_index("blk")
     row_start = my_block * rows_dev
     my_sec = lax.dynamic_slice_in_dim(sec_all, row_start, rows_dev, 0)
-    same = my_sec[:, None] == sec_all[None, :]
-    masked = jnp.where(same[None, :, :], env_loc, jnp.zeros_like(env_loc))
-    applied = jnp.einsum(
-        "wij,jx->wix",
-        masked,
-        lax.all_gather(theta_loc, "blk", axis=0, tiled=True),
-        preferred_element_type=jnp.float32,
-    )
+    theta_all = lax.all_gather(theta_loc, "blk", axis=0, tiled=True)
+    applied = masked_apply(env_loc, theta_all, sec_all, my_sec)
     applied = applied.reshape(chain_w, rows_dev, phys, cols)
-    acted = jnp.einsum("wpq,wiqc->ipc", ops_loc, applied, precision=lax.Precision.HIGHEST)
+    acted = jnp.einsum("wpq,wiqc->ipc", ops_loc, applied, precision=lax.Precision.HIGH)
     theta_f = theta_loc.astype(jnp.float32).reshape(rows_dev, phys, cols)
     partial_intersection = jnp.einsum(
-        "ipc,ipd->cd", theta_f, acted, precision=lax.Precision.HIGHEST
+        "ipc,ipd->cd", theta_f, acted, precision=lax.Precision.HIGH
     )
     intersection = butterfly_sum(partial_intersection, "blk")
     transfer = (
@@ -71,7 +119,7 @@
     prefix = jnp.stack(prefix)
     incoming = prefix[sect_no]
     outgoing = prefix[sect_no + 1]
-    result = jnp.einsum("ipc,cd->ipd", acted, incoming, precision=lax.Precision.HIGHEST)
+    result = jnp.einsum("ipc,cd->ipd", acted, incoming, precision=lax.Precision.HIGH)
     updated = result.reshape(1, rows_dev, width).astype(jnp.bfloat16)
     return (updated, outgoing[None])
 

time: 184 us -> 161 us (0.88)
  matrix products: 41.3 us -> 5.27 us
  starting transfers between devices: 13.1 us -> 31.5 us
  waiting for transfers between devices: 93.1 us -> 81.3 us
  Pallas kernels: 0 us -> 9.04 us
  local copies, waits for them, and re-layouts: 19.7 us -> 12.1 us
  between operations: 14.9 us -> 17.9 us
    dot_general x4 -> x3, matrix products: 40.2 us -> 4.21 us  [the longest x1 2.63 us: per_device(): jnp.einsum('wpq,wiqc->ipc', ops_loc, applied, precision=lax.Precision.HIGH)]
    ppermute x5, starting transfers between devices: 8.58 us -> 21.1 us  [butterfly_sum(): value = value + lax.ppermute(value, axis, pairs)]
    pallas_call x0 -> x1, Pallas kernels: none -> 9.04 us  [masked_apply(): pl.pallas_call(masked_apply_kernel, grid_spec=grid_spec, out_shape=jax.Sh...]
    unnamed x12 -> x14, local copies, waits for them, and re-layouts: 18.1 us -> 9.1 us
    all_gather x1, waiting for transfers between devices: 74.6 us -> 68.5 us  [per_device(): theta_all = lax.all_gather(theta_loc, 'blk', axis=0, tiled=True)]
    ppermute x3, starting transfers between devices: 4.5 us -> 10.3 us  [gather_all(): parts.append(lax.ppermute(value, axis, pairs))]
    ppermute x3, waiting for transfers between devices: 4.77 us -> 1.89 us  [gather_all(): parts.append(lax.ppermute(value, axis, pairs))]
    ppermute x5, waiting for transfers between devices: 13 us -> 10.2 us  [butterfly_sum(): value = value + lax.ppermute(value, axis, pairs)]
  transfers between devices with their start and end apart: 9 -> 9, of which waited for: 9 -> 8; matrix products, arithmetic and copies ran while one was open for 2% -> 4% of each run, Pallas kernels for 0% -> 0%
where the time goes in v2:
time: 161 us
  waiting for transfers between devices  81.3 us (50%)
  starting transfers between devices  31.5 us (20%)
  between operations  17.9 us (11%)
  local copies, waits for them, and re-layouts  12.1 us (8%)
  Pallas kernels  9.04 us (6%)
  matrix products  5.27 us (3%)
  other arithmetic  3.53 us (2%)
    all_gather x1, waiting for transfers between devices, per_device(): theta_all = lax.all_gather(theta_loc, 'blk', axis=0, tiled=True)  68.5 us
    ppermute x5, starting transfers between devices, butterfly_sum(): value = value + lax.ppermute(value, axis, pairs)  21.1 us
    ppermute x3, starting transfers between devices, gather_all(): parts.append(lax.ppermute(value, axis, pairs))  10.3 us
    ppermute x5, waiting for transfers between devices, butterfly_sum(): value = value + lax.ppermute(value, axis, pairs)  10.2 us
    unnamed x14, local copies, waits for them, and re-layouts  9.1 us
    pallas_call x1, Pallas kernels, masked_apply(): pl.pallas_call(masked_apply_kernel, grid_spec=grid_spec, out_shape=jax.Sh...  9.04 us
  transfers between devices with their start and end apart: 9, of which 8 were waited for; matrix products, arithmetic and copies ran while one was open for 4% of the time, Pallas kernels for 0%

profile of v2, /device:TPU:0, one launch (start us, length us, event | category | flops | bytes accessed | tf_op | source)
XLA Modules:
  0.0 160.7 jit_solution(13281296146807924559)
XLA Ops:
  9.2 2.8 %fusion.13 = (s32[]{:T(128)}, s32[]{:T(128)}) fusion(s32[1,4096]{1,0:T(1,128)} %sec_j_ref.1, s32[]{:T(128)} %bitcast, s32[]{:T(128)} %bitcast.2), kind=kLoop, calls=%fused_computation.28 | loop fusion | flops 24574 | bytes 16400 | tf_op jit(solution)/shard_map/reduce_sum | solution.py:59
  15.7 1.1 copy.36
  16.9 68.5 %all-gather.3.cloned.1.call-done = bf16[1,4096,2048]{2,1,0:T(8,128)(2,1)} async-done(((bf16[1,128,2048]{2,1,0:T(8,128)(2,1)}), bf16[1,4096,2048]{2,1,0:T(8,128)(2,1)}) %all-gather.3.cloned.1.call-update) | async-done | bytes 16777232 | tf_op jit(solution)/shard_map/all_gather | solution.py:100
  85.4 0.7 copy-done.1
  86.2 9.0 %shard_map.68 = f32[8,128,2048]{2,1,0:T(8,128)} custom-call(s32[2]{0:T(128)S(1)} %pad_add_fusion.span_ref, bf16[8,128,4096]{2,1,0:T(8,128)(2,1)} %bitcast.83, bf16[4096,2048]{1,0:T(8,128)(2,1)} %bitcast.82, s32[1,4096]{1,0:T(1,128)S(1)} %copy-done.1, s32[128,1]{1,0:T(8,128)S(1)} %copy.18.sec_i_ref), custom_call_target="tpu_custom_call" | custom-call | tf_op jit(solution)/shard_map/pallas_call | solution.py:77
  95.2 5.4 %copy.35 = f32[128,8,16,128]{3,2,1,0:T(8,128)S(1)} copy(f32[128,8,16,128]{3,1,2,0:T(8,128)} %bitcast.81) | data formatting | bytes 16777216
  100.6 2.6 %fusion.2 = f32[128,16,128]{2,1,0:T(8,128)S(1)} fusion(f32[1,8,16,16]{3,2,1,0:T(8,128)S(1)} %copy-done, f32[8,128,16,128]{3,2,1,0:T(8,128)S(1)} %bitcast.80), kind=kOutput, calls=%fused_computation.3 | convolution fusion | flops 201326592 | bytes 9445376 | tf_op jit(solution)/shard_map/wpq,wiqc->ipc/dot_general | solution.py:103
  103.2 0.7 convolution_bitcast_fusion
  104.3 1.0 collective-permute-done
  105.3 3.4 %collective-permute-start.1 = (f32[128,128]{0,1:T(8,128)S(1)}, f32[128,128]{0,1:T(8,128)S(1)}, u32[]{:S(2)}, u32[]{:S(2)}) collective-permute-start(f32[128,128]{0,1:T(8,128)S(1)} %add.61), channel_id=1, source_target_pairs={{0,2},{1,3},{2,0},{3,1},{4,6},{5,7},{6,4},{7,5},{8,10},{9,11},{10,... | collective-permute-start | bytes 196616 | tf_op jit(solution)/shard_map/ppermute | solution.py:22
  108.7 2.6 %collective-permute-done.1 = f32[128,128]{0,1:T(8,128)S(1)} collective-permute-done((f32[128,128]{0,1:T(8,128)S(1)}, f32[128,128]{0,1:T(8,128)S(1)}, u32[]{:S(2)}, u32[]{:S(2)}) %collective-permute-start.1) | collective-permute-done | bytes 65568 | tf_op jit(solution)/shard_map/ppermute | solution.py:22
  111.3 5.9 %collective-permute-start.2 = (f32[128,128]{0,1:T(8,128)S(1)}, f32[128,128]{0,1:T(8,128)S(1)}, u32[]{:S(2)}, u32[]{:S(2)}) collective-permute-start(f32[128,128]{0,1:T(8,128)S(1)} %add.62), channel_id=1, source_target_pairs={{0,4},{1,5},{2,6},{3,7},{4,0},{5,1},{6,2},{7,3},{8,12},{9,13},{10,... | collective-permute-start | bytes 196616 | tf_op jit(solution)/shard_map/ppermute | solution.py:22
  117.2 2.2 %collective-permute-done.2 = f32[128,128]{0,1:T(8,128)S(1)} collective-permute-done((f32[128,128]{0,1:T(8,128)S(1)}, f32[128,128]{0,1:T(8,128)S(1)}, u32[]{:S(2)}, u32[]{:S(2)}) %collective-permute-start.2) | collective-permute-done | bytes 65568 | tf_op jit(solution)/shard_map/ppermute | solution.py:22
  119.5 5.3 %collective-permute-start.3 = (f32[128,128]{0,1:T(8,128)S(1)}, f32[128,128]{0,1:T(8,128)S(1)}, u32[]{:S(2)}, u32[]{:S(2)}) collective-permute-start(f32[128,128]{0,1:T(8,128)S(1)} %add.63), channel_id=1, source_target_pairs={{0,8},{1,9},{2,10},{3,11},{4,12},{5,13},{6,14},{7,15},{8,0},{9,1},... | collective-permute-start | bytes 196616 | tf_op jit(solution)/shard_map/ppermute | solution.py:22
  124.9 2.1 %collective-permute-done.3 = f32[128,128]{0,1:T(8,128)S(1)} collective-permute-done((f32[128,128]{0,1:T(8,128)S(1)}, f32[128,128]{0,1:T(8,128)S(1)}, u32[]{:S(2)}, u32[]{:S(2)}) %collective-permute-start.3) | collective-permute-done | bytes 65568 | tf_op jit(solution)/shard_map/ppermute | solution.py:22
  127.0 6.2 %collective-permute-start.4 = (f32[128,128]{0,1:T(8,128)S(1)}, f32[128,128]{0,1:T(8,128)S(1)}, u32[]{:S(2)}, u32[]{:S(2)}) collective-permute-start(f32[128,128]{0,1:T(8,128)S(1)} %add.64), channel_id=1, source_target_pairs={{0,16},{1,17},{2,18},{3,19},{4,20},{5,21},{6,22},{7,23},{8,24},{9,... | collective-permute-start | bytes 196616 | tf_op jit(solution)/shard_map/ppermute | solution.py:22
  133.2 2.2 %collective-permute-done.4 = f32[128,128]{0,1:T(8,128)S(1)} collective-permute-done((f32[128,128]{0,1:T(8,128)S(1)}, f32[128,128]{0,1:T(8,128)S(1)}, u32[]{:S(2)}, u32[]{:S(2)}) %collective-permute-start.4) | collective-permute-done | bytes 65568 | tf_op jit(solution)/shard_map/ppermute | solution.py:22
  136.8 3.7 %collective-permute-start.5 = (f32[128,128]{0,1:T(8,128)S(1)}, f32[128,128]{0,1:T(8,128)S(1)}, u32[]{:S(2)}, u32[]{:S(2)}) collective-permute-start(f32[128,128]{0,1:T(8,128)S(1)} %multiply_divide_fusion), channel_id=1, source_target_pairs={{0,32},{32,64},{64,96},{96,0},{1,33},{33,65},{65,97},{97,1},{2,34}... | collective-permute-start | bytes 196616 | tf_op jit(solution)/shard_map/ppermute | solution.py:33
  140.5 4.1 %collective-permute-start.6 = (f32[128,128]{0,1:T(8,128)S(1)}, f32[128,128]{0,1:T(8,128)S(1)}, u32[]{:S(2)}, u32[]{:S(2)}) collective-permute-start(f32[128,128]{0,1:T(8,128)S(1)} %multiply_divide_fusion), channel_id=1, source_target_pairs={{0,64},{32,96},{64,0},{96,32},{1,65},{33,97},{65,1},{97,33},{2,66}... | collective-permute-start | bytes 196616 | tf_op jit(solution)/shard_map/ppermute | solution.py:33
  144.6 2.5 %collective-permute-start.7 = (f32[128,128]{0,1:T(8,128)S(1)}, f32[128,128]{0,1:T(8,128)S(1)}, u32[]{:S(2)}, u32[]{:S(2)}) collective-permute-start(f32[128,128]{0,1:T(8,128)S(1)} %multiply_divide_fusion), channel_id=1, source_target_pairs={{0,96},{32,0},{64,32},{96,64},{1,97},{33,1},{65,33},{97,65},{2,98}... | collective-permute-start | bytes 196616 | tf_op jit(solution)/shard_map/ppermute | solution.py:33
  147.4 1.6 collective-permute-done.7
  151.2 0.9 convolution_convert_fusion
  152.1 1.0 copy.28
  153.1 0.7 copy.29
  (37 shorter events, 6.3 us)
Async XLA Ops:
  7.2 93.4 %copy-start = (f32[1,8,16,16]{3,2,1,0:T(8,128)S(1)}, f32[1,8,16,16]{3,2,1,0:T(8,128)}, u32[]{:S(2)}) copy-start(f32[1,8,16,16]{3,2,1,0:T(8,128)} %param.8) | copy-start | bytes 24580
  7.2 78.3 %all-gather.3.cloned.1.call-start = ((), (), s32[]{:S(2)}) async-start(), calls=%async_computation | async-start | bytes 17301504 | tf_op jit(solution)/shard_map/all_gather | solution.py:100
  85.4 0.7 copy-start.1
  100.6 24.2 %copy-start.2 = (f32[128,128]{1,0:T(8,128)S(1)}, f32[128,128]{1,0:T(8,128)}, u32[]{:S(2)}) copy-start(f32[128,128]{1,0:T(8,128)} %param.9) | copy-start | bytes 196612
  104.0 1.3 collective-permute-start
  105.3 6.0 %collective-permute-start.1 = (f32[128,128]{0,1:T(8,128)S(1)}, f32[128,128]{0,1:T(8,128)S(1)}, u32[]{:S(2)}, u32[]{:S(2)}) collective-permute-start(f32[128,128]{0,1:T(8,128)S(1)} %add.61), channel_id=1, source_target_pairs={{0,2},{1,3},{2,0},{3,1},{4,6},{5,7},{6,4},{7,5},{8,10},{9,11},{10,... | collective-permute-start | bytes 196616 | tf_op jit(solution)/shard_map/ppermute | solution.py:22
  111.3 8.1 %collective-permute-start.2 = (f32[128,128]{0,1:T(8,128)S(1)}, f32[128,128]{0,1:T(8,128)S(1)}, u32[]{:S(2)}, u32[]{:S(2)}) collective-permute-start(f32[128,128]{0,1:T(8,128)S(1)} %add.62), channel_id=1, source_target_pairs={{0,4},{1,5},{2,6},{3,7},{4,0},{5,1},{6,2},{7,3},{8,12},{9,13},{10,... | collective-permute-start | bytes 196616 | tf_op jit(solution)/shard_map/ppermute | solution.py:22
  119.5 7.5 %collective-permute-start.3 = (f32[128,128]{0,1:T(8,128)S(1)}, f32[128,128]{0,1:T(8,128)S(1)}, u32[]{:S(2)}, u32[]{:S(2)}) collective-permute-start(f32[128,128]{0,1:T(8,128)S(1)} %add.63), channel_id=1, source_target_pairs={{0,8},{1,9},{2,10},{3,11},{4,12},{5,13},{6,14},{7,15},{8,0},{9,1},... | collective-permute-start | bytes 196616 | tf_op jit(solution)/shard_map/ppermute | solution.py:22
  127.0 8.4 %collective-permute-start.4 = (f32[128,128]{0,1:T(8,128)S(1)}, f32[128,128]{0,1:T(8,128)S(1)}, u32[]{:S(2)}, u32[]{:S(2)}) collective-permute-start(f32[128,128]{0,1:T(8,128)S(1)} %add.64), channel_id=1, source_target_pairs={{0,16},{1,17},{2,18},{3,19},{4,20},{5,21},{6,22},{7,23},{8,24},{9,... | collective-permute-start | bytes 196616 | tf_op jit(solution)/shard_map/ppermute | solution.py:22
  136.8 10.4 %collective-permute-start.5 = (f32[128,128]{0,1:T(8,128)S(1)}, f32[128,128]{0,1:T(8,128)S(1)}, u32[]{:S(2)}, u32[]{:S(2)}) collective-permute-start(f32[128,128]{0,1:T(8,128)S(1)} %multiply_divide_fusion), channel_id=1, source_target_pairs={{0,32},{32,64},{64,96},{96,0},{1,33},{33,65},{65,97},{97,1},{2,34}... | collective-permute-start | bytes 196616 | tf_op jit(solution)/shard_map/ppermute | solution.py:33
  140.5 7.0 %collective-permute-start.6 = (f32[128,128]{0,1:T(8,128)S(1)}, f32[128,128]{0,1:T(8,128)S(1)}, u32[]{:S(2)}, u32[]{:S(2)}) collective-permute-start(f32[128,128]{0,1:T(8,128)S(1)} %multiply_divide_fusion), channel_id=1, source_target_pairs={{0,64},{32,96},{64,0},{96,32},{1,65},{33,97},{65,1},{97,33},{2,66}... | collective-permute-start | bytes 196616 | tf_op jit(solution)/shard_map/ppermute | solution.py:33
  144.6 4.4 %collective-permute-start.7 = (f32[128,128]{0,1:T(8,128)S(1)}, f32[128,128]{0,1:T(8,128)S(1)}, u32[]{:S(2)}, u32[]{:S(2)}) collective-permute-start(f32[128,128]{0,1:T(8,128)S(1)} %multiply_divide_fusion), channel_id=1, source_target_pairs={{0,96},{32,0},{64,32},{96,64},{1,97},{33,1},{65,33},{97,65},{2,98}... | collective-permute-start | bytes 196616 | tf_op jit(solution)/shard_map/ppermute | solution.py:33
Sparse Core Ops, SparseCore 0:
  10.2 75.1 all-gather.2

commit v3 on v2

--- a/solution.py
+++ b/solution.py
@@ -47,12 +47,16 @@
     def _():
         same = sec_i_ref[...] == sec_j_ref[...]
         block = theta_ref[...]
-        for w in range(out_ref.shape[0]):
+        cols = out_ref.shape[2]
+        phys = block.shape[1] // cols
+        for w in range(env_ref.shape[0]):
             env_w = jnp.where(same, env_ref[w], jnp.zeros_like(env_ref[w]))
-            out_ref[w] += jnp.dot(env_w, block, preferred_element_type=jnp.float32)
+            part = jnp.dot(env_w, block, preferred_element_type=jnp.float32)
+            for q in range(phys):
+                out_ref[w * phys + q] += part[:, q * cols:(q + 1) * cols]
 
 
-def masked_apply(env_loc, theta_all, sec_all, my_sec):
+def masked_apply(env_loc, theta_all, sec_all, my_sec, phys):
     chain_w, rows_dev, depth = env_loc.shape
     width = theta_all.shape[1]
     tiles = depth // K_TILE
@@ -72,12 +76,12 @@
             pl.BlockSpec((1, K_TILE), lambda k, s: (0, tile_of(k, s))),
             pl.BlockSpec((rows_dev, 1), lambda k, s: (0, 0)),
         ],
-        out_specs=pl.BlockSpec((chain_w, rows_dev, width), lambda k, s: (0, 0, 0)),
+        out_specs=pl.BlockSpec((chain_w * phys, rows_dev, width // phys), lambda k, s: (0, 0, 0)),
     )
     return pl.pallas_call(
         masked_apply_kernel,
         grid_spec=grid_spec,
-        out_shape=jax.ShapeDtypeStruct((chain_w, rows_dev, width), jnp.float32),
+        out_shape=jax.ShapeDtypeStruct((chain_w * phys, rows_dev, width // phys), jnp.float32),
         compiler_params=pltpu.CompilerParams(
             dimension_semantics=("arbitrary",), vmem_limit_bytes=48 * 1024 * 1024
         ),
@@ -98,9 +102,9 @@
     row_start = my_block * rows_dev
     my_sec = lax.dynamic_slice_in_dim(sec_all, row_start, rows_dev, 0)
     theta_all = lax.all_gather(theta_loc, "blk", axis=0, tiled=True)
-    applied = masked_apply(env_loc, theta_all, sec_all, my_sec)
-    applied = applied.reshape(chain_w, rows_dev, phys, cols)
-    acted = jnp.einsum("wpq,wiqc->ipc", ops_loc, applied, precision=lax.Precision.HIGH)
+    applied = masked_apply(env_loc, theta_all, sec_all, my_sec, phys)
+    applied = applied.reshape(chain_w, phys, rows_dev, cols)
+    acted = jnp.einsum("wpq,wqic->ipc", ops_loc, applied, precision=lax.Precision.HIGH)
     theta_f = theta_loc.astype(jnp.float32).reshape(rows_dev, phys, cols)
     partial_intersection = jnp.einsum(
         "ipc,ipd->cd", theta_f, acted, precision=lax.Precision.HIGH

time: 161 us -> 163 us (1.012)
  matrix products: 5.27 us -> 12.7 us
  local copies, waits for them, and re-layouts: 12.1 us -> 6.74 us
  waiting for transfers between devices: 81.3 us -> 84.3 us
  starting transfers between devices: 31.5 us -> 29.4 us
    dot_general x1, matrix products: 2.63 us -> 10.1 us  [per_device(): jnp.einsum('wpq,wqic->ipc', ops_loc, applied, precision=lax.Precision.HIGH)]
    unnamed x14 -> x13, local copies, waits for them, and re-layouts: 9.1 us -> 3.72 us
    ppermute x3, starting transfers between devices: 10.3 us -> 6.76 us  [gather_all(): parts.append(lax.ppermute(value, axis, pairs))]
    ppermute x3, waiting for transfers between devices: 1.89 us -> 4.25 us  [gather_all(): parts.append(lax.ppermute(value, axis, pairs))]
  transfers between devices with their start and end apart: 9 -> 9, of which waited for: 8 -> 9; matrix products, arithmetic and copies ran while one was open for 4% -> 4% of each run, Pallas kernels for 0% -> 0%
where the time goes in v3:
time: 163 us; the launch traced here: 164 us
  waiting for transfers between devices  84.3 us (52%)
  starting transfers between devices  29.4 us (18%)
  between operations  17.9 us (11%)
  matrix products  12.7 us (8%)
  Pallas kernels  9.04 us (6%)
  local copies, waits for them, and re-layouts  6.74 us (4%)
  other arithmetic  3.53 us (2%)
    all_gather x1, waiting for transfers between devices, per_device(): theta_all = lax.all_gather(theta_loc, 'blk', axis=0, tiled=True)  68.5 us
    ppermute x5, starting transfers between devices, butterfly_sum(): value = value + lax.ppermute(value, axis, pairs)  22.6 us
    ppermute x5, waiting for transfers between devices, butterfly_sum(): value = value + lax.ppermute(value, axis, pairs)  10.8 us
    dot_general x1, matrix products, per_device(): jnp.einsum('wpq,wqic->ipc', ops_loc, applied, precision=lax.Precision.HIGH)  10.1 us
    pallas_call x1, Pallas kernels, masked_apply(): pl.pallas_call(masked_apply_kernel, grid_spec=grid_spec, out_shape=jax.Sh...  9.04 us
    ppermute x3, starting transfers between devices, gather_all(): parts.append(lax.ppermute(value, axis, pairs))  6.76 us
    ppermute x3, waiting for transfers between devices, gather_all(): parts.append(lax.ppermute(value, axis, pairs))  4.25 us
    unnamed x13, local copies, waits for them, and re-layouts  3.72 us
  transfers between devices with their start and end apart: 9, of which 9 were waited for; matrix products, arithmetic and copies ran while one was open for 4% of the time, Pallas kernels for 0%

profile of v3, /device:TPU:0, one launch (start us, length us, event | category | flops | bytes accessed | tf_op | source)
XLA Modules:
  0.0 163.6 jit_solution(4165113793277685798)
XLA Ops:
  9.2 2.8 %fusion.13 = (s32[]{:T(128)}, s32[]{:T(128)}) fusion(s32[1,4096]{1,0:T(1,128)} %sec_j_ref.1, s32[]{:T(128)} %bitcast, s32[]{:T(128)} %bitcast.2), kind=kLoop, calls=%fused_computation.28 | loop fusion | flops 24574 | bytes 16400 | tf_op jit(solution)/shard_map/reduce_sum | solution.py:63
  15.7 1.1 copy.34
  16.9 68.5 %all-gather.3.cloned.1.call-done = bf16[1,4096,2048]{2,1,0:T(8,128)(2,1)} async-done(((bf16[1,128,2048]{2,1,0:T(8,128)(2,1)}), bf16[1,4096,2048]{2,1,0:T(8,128)(2,1)}) %all-gather.3.cloned.1.call-update) | async-done | bytes 16777232 | tf_op jit(solution)/shard_map/all_gather | solution.py:104
  86.2 9.0 %shard_map.68 = f32[128,128,128]{2,1,0:T(8,128)} custom-call(s32[2]{0:T(128)S(1)} %pad_add_fusion.span_ref, bf16[8,128,4096]{2,1,0:T(8,128)(2,1)} %bitcast.72, bf16[4096,2048]{1,0:T(8,128)(2,1)} %bitcast.71, s32[1,4096]{1,0:T(1,128)S(1)} %copy-done.1, s32[128,1]{1,0:T(8,128)S(1)} %copy.18.sec_i_ref), custom_call_target="tpu_custom_call" | custom-call | tf_op jit(solution)/shard_map/pallas_call | solution.py:81
  95.2 10.1 %fusion.2 = f32[128,16,128]{2,1,0:T(8,128)S(1)} fusion(f32[8,16,128,128]{3,2,1,0:T(8,128)} %bitcast.70, f32[1,8,16,16]{3,2,1,0:T(8,128)S(1)} %copy-done), kind=kOutput, calls=%fused_computation.3 | convolution fusion | flops 201326592 | bytes 9445376 | tf_op jit(solution)/shard_map/wpq,wqic->ipc/dot_general | solution.py:107
  105.3 0.7 convolution_bitcast_fusion
  106.0 2.8 %collective-permute-start = (f32[128,128]{0,1:T(8,128)S(1)}, f32[128,128]{0,1:T(8,128)S(1)}, u32[]{:S(2)}, u32[]{:S(2)}) collective-permute-start(f32[128,128]{0,1:T(8,128)S(1)} %convolution_bitcast_fusion), channel_id=1, source_target_pairs={{0,1},{1,0},{2,3},{3,2},{4,5},{5,4},{6,7},{7,6},{8,9},{9,8},{10,11... | collective-permute-start | bytes 196616 | tf_op jit(solution)/shard_map/ppermute | solution.py:22
  108.8 0.9 collective-permute-done
  109.7 1.1 collective-permute-start.1
  110.9 3.3 %collective-permute-done.1 = f32[128,128]{0,1:T(8,128)S(1)} collective-permute-done((f32[128,128]{0,1:T(8,128)S(1)}, f32[128,128]{0,1:T(8,128)S(1)}, u32[]{:S(2)}, u32[]{:S(2)}) %collective-permute-start.1) | collective-permute-done | bytes 65568 | tf_op jit(solution)/shard_map/ppermute | solution.py:22
  114.2 12.5 %collective-permute-start.2 = (f32[128,128]{0,1:T(8,128)S(1)}, f32[128,128]{0,1:T(8,128)S(1)}, u32[]{:S(2)}, u32[]{:S(2)}) collective-permute-start(f32[128,128]{0,1:T(8,128)S(1)} %add.62), channel_id=1, source_target_pairs={{0,4},{1,5},{2,6},{3,7},{4,0},{5,1},{6,2},{7,3},{8,12},{9,13},{10,... | collective-permute-start | bytes 196616 | tf_op jit(solution)/shard_map/ppermute | solution.py:22
  126.7 2.2 %collective-permute-done.2 = f32[128,128]{0,1:T(8,128)S(1)} collective-permute-done((f32[128,128]{0,1:T(8,128)S(1)}, f32[128,128]{0,1:T(8,128)S(1)}, u32[]{:S(2)}, u32[]{:S(2)}) %collective-permute-start.2) | collective-permute-done | bytes 65568 | tf_op jit(solution)/shard_map/ppermute | solution.py:22
  129.0 2.6 %collective-permute-start.3 = (f32[128,128]{0,1:T(8,128)S(1)}, f32[128,128]{0,1:T(8,128)S(1)}, u32[]{:S(2)}, u32[]{:S(2)}) collective-permute-start(f32[128,128]{0,1:T(8,128)S(1)} %add.63), channel_id=1, source_target_pairs={{0,8},{1,9},{2,10},{3,11},{4,12},{5,13},{6,14},{7,15},{8,0},{9,1},... | collective-permute-start | bytes 196616 | tf_op jit(solution)/shard_map/ppermute | solution.py:22
  131.6 2.1 %collective-permute-done.3 = f32[128,128]{0,1:T(8,128)S(1)} collective-permute-done((f32[128,128]{0,1:T(8,128)S(1)}, f32[128,128]{0,1:T(8,128)S(1)}, u32[]{:S(2)}, u32[]{:S(2)}) %collective-permute-start.3) | collective-permute-done | bytes 65568 | tf_op jit(solution)/shard_map/ppermute | solution.py:22
  133.8 3.6 %collective-permute-start.4 = (f32[128,128]{0,1:T(8,128)S(1)}, f32[128,128]{0,1:T(8,128)S(1)}, u32[]{:S(2)}, u32[]{:S(2)}) collective-permute-start(f32[128,128]{0,1:T(8,128)S(1)} %add.64), channel_id=1, source_target_pairs={{0,16},{1,17},{2,18},{3,19},{4,20},{5,21},{6,22},{7,23},{8,24},{9,... | collective-permute-start | bytes 196616 | tf_op jit(solution)/shard_map/ppermute | solution.py:22
  137.4 2.2 %collective-permute-done.4 = f32[128,128]{0,1:T(8,128)S(1)} collective-permute-done((f32[128,128]{0,1:T(8,128)S(1)}, f32[128,128]{0,1:T(8,128)S(1)}, u32[]{:S(2)}, u32[]{:S(2)}) %collective-permute-start.4) | collective-permute-done | bytes 65568 | tf_op jit(solution)/shard_map/ppermute | solution.py:22
  141.0 1.9 %collective-permute-start.5 = (f32[128,128]{0,1:T(8,128)S(1)}, f32[128,128]{0,1:T(8,128)S(1)}, u32[]{:S(2)}, u32[]{:S(2)}) collective-permute-start(f32[128,128]{0,1:T(8,128)S(1)} %multiply_divide_fusion), channel_id=1, source_target_pairs={{0,32},{32,64},{64,96},{96,0},{1,33},{33,65},{65,97},{97,1},{2,34}... | collective-permute-start | bytes 196616 | tf_op jit(solution)/shard_map/ppermute | solution.py:33
  142.9 4.8 %collective-permute-start.6 = (f32[128,128]{0,1:T(8,128)S(1)}, f32[128,128]{0,1:T(8,128)S(1)}, u32[]{:S(2)}, u32[]{:S(2)}) collective-permute-start(f32[128,128]{0,1:T(8,128)S(1)} %multiply_divide_fusion), channel_id=1, source_target_pairs={{0,64},{32,96},{64,0},{96,32},{1,65},{33,97},{65,1},{97,33},{2,66}... | collective-permute-start | bytes 196616 | tf_op jit(solution)/shard_map/ppermute | solution.py:33
  147.8 0.8 collective-permute-done.5
  148.5 2.2 %collective-permute-done.6 = f32[128,128]{0,1:T(8,128)S(1)} collective-permute-done((f32[128,128]{0,1:T(8,128)S(1)}, f32[128,128]{0,1:T(8,128)S(1)}, u32[]{:S(2)}, u32[]{:S(2)}) %collective-permute-start.6) | collective-permute-done | bytes 65568 | tf_op jit(solution)/shard_map/ppermute | solution.py:33
  150.7 1.3 collective-permute-done.7
  154.2 0.9 convolution_convert_fusion
  155.1 1.0 copy.28
  156.1 0.7 copy.29
  (36 shorter events, 6.4 us)
Async XLA Ops:
  7.2 88.0 %copy-start = (f32[1,8,16,16]{3,2,1,0:T(8,128)S(1)}, f32[1,8,16,16]{3,2,1,0:T(8,128)}, u32[]{:S(2)}) copy-start(f32[1,8,16,16]{3,2,1,0:T(8,128)} %param.8) | copy-start | bytes 24580
  7.2 78.3 %all-gather.3.cloned.1.call-start = ((), (), s32[]{:S(2)}) async-start(), calls=%async_computation | async-start | bytes 17301504 | tf_op jit(solution)/shard_map/all_gather | solution.py:104
  85.4 0.7 copy-start.1
  95.2 36.3 %copy-start.2 = (f32[128,128]{1,0:T(8,128)S(1)}, f32[128,128]{1,0:T(8,128)}, u32[]{:S(2)}) copy-start(f32[128,128]{1,0:T(8,128)} %param.9) | copy-start | bytes 196612
  106.0 3.7 %collective-permute-start = (f32[128,128]{0,1:T(8,128)S(1)}, f32[128,128]{0,1:T(8,128)S(1)}, u32[]{:S(2)}, u32[]{:S(2)}) collective-permute-start(f32[128,128]{0,1:T(8,128)S(1)} %convolution_bitcast_fusion), channel_id=1, source_target_pairs={{0,1},{1,0},{2,3},{3,2},{4,5},{5,4},{6,7},{7,6},{8,9},{9,8},{10,11... | collective-permute-start | bytes 196616 | tf_op jit(solution)/shard_map/ppermute | solution.py:22
  109.7 4.4 %collective-permute-start.1 = (f32[128,128]{0,1:T(8,128)S(1)}, f32[128,128]{0,1:T(8,128)S(1)}, u32[]{:S(2)}, u32[]{:S(2)}) collective-permute-start(f32[128,128]{0,1:T(8,128)S(1)} %add.61), channel_id=1, source_target_pairs={{0,2},{1,3},{2,0},{3,1},{4,6},{5,7},{6,4},{7,5},{8,10},{9,11},{10,... | collective-permute-start | bytes 196616 | tf_op jit(solution)/shard_map/ppermute | solution.py:22
  114.2 14.8 %collective-permute-start.2 = (f32[128,128]{0,1:T(8,128)S(1)}, f32[128,128]{0,1:T(8,128)S(1)}, u32[]{:S(2)}, u32[]{:S(2)}) collective-permute-start(f32[128,128]{0,1:T(8,128)S(1)} %add.62), channel_id=1, source_target_pairs={{0,4},{1,5},{2,6},{3,7},{4,0},{5,1},{6,2},{7,3},{8,12},{9,13},{10,... | collective-permute-start | bytes 196616 | tf_op jit(solution)/shard_map/ppermute | solution.py:22
  129.0 4.8 %collective-permute-start.3 = (f32[128,128]{0,1:T(8,128)S(1)}, f32[128,128]{0,1:T(8,128)S(1)}, u32[]{:S(2)}, u32[]{:S(2)}) collective-permute-start(f32[128,128]{0,1:T(8,128)S(1)} %add.63), channel_id=1, source_target_pairs={{0,8},{1,9},{2,10},{3,11},{4,12},{5,13},{6,14},{7,15},{8,0},{9,1},... | collective-permute-start | bytes 196616 | tf_op jit(solution)/shard_map/ppermute | solution.py:22
  133.8 5.9 %collective-permute-start.4 = (f32[128,128]{0,1:T(8,128)S(1)}, f32[128,128]{0,1:T(8,128)S(1)}, u32[]{:S(2)}, u32[]{:S(2)}) collective-permute-start(f32[128,128]{0,1:T(8,128)S(1)} %add.64), channel_id=1, source_target_pairs={{0,16},{1,17},{2,18},{3,19},{4,20},{5,21},{6,22},{7,23},{8,24},{9,... | collective-permute-start | bytes 196616 | tf_op jit(solution)/shard_map/ppermute | solution.py:22
  141.0 7.5 %collective-permute-start.5 = (f32[128,128]{0,1:T(8,128)S(1)}, f32[128,128]{0,1:T(8,128)S(1)}, u32[]{:S(2)}, u32[]{:S(2)}) collective-permute-start(f32[128,128]{0,1:T(8,128)S(1)} %multiply_divide_fusion), channel_id=1, source_target_pairs={{0,32},{32,64},{64,96},{96,0},{1,33},{33,65},{65,97},{97,1},{2,34}... | collective-permute-start | bytes 196616 | tf_op jit(solution)/shard_map/ppermute | solution.py:33
  142.9 7.8 %collective-permute-start.6 = (f32[128,128]{0,1:T(8,128)S(1)}, f32[128,128]{0,1:T(8,128)S(1)}, u32[]{:S(2)}, u32[]{:S(2)}) collective-permute-start(f32[128,128]{0,1:T(8,128)S(1)} %multiply_divide_fusion), channel_id=1, source_target_pairs={{0,64},{32,96},{64,0},{96,32},{1,65},{33,97},{65,1},{97,33},{2,66}... | collective-permute-start | bytes 196616 | tf_op jit(solution)/shard_map/ppermute | solution.py:33
  147.8 4.3 %collective-permute-start.7 = (f32[128,128]{0,1:T(8,128)S(1)}, f32[128,128]{0,1:T(8,128)S(1)}, u32[]{:S(2)}, u32[]{:S(2)}) collective-permute-start(f32[128,128]{0,1:T(8,128)S(1)} %multiply_divide_fusion), channel_id=1, source_target_pairs={{0,96},{32,0},{64,32},{96,64},{1,97},{33,1},{65,33},{97,65},{2,98}... | collective-permute-start | bytes 196616 | tf_op jit(solution)/shard_map/ppermute | solution.py:33
Sparse Core Ops, SparseCore 0:
  10.2 75.1 all-gather.2

commit v4 on v2

--- a/solution.py
+++ b/solution.py
@@ -7,7 +7,7 @@
 from jax.experimental.pallas import tpu as pltpu
 from jax.sharding import PartitionSpec as P
 
-K_TILE = 512
+K_TILE = 256
 
 
 def matprod(first, second):

time: 161 us -> 162 us (level)
  waiting for transfers between devices: 81.3 us -> 89.3 us
  starting transfers between devices: 31.5 us -> 24.2 us
    ppermute x3, starting transfers between devices: 10.3 us -> 3.3 us  [gather_all(): parts.append(lax.ppermute(value, axis, pairs))]
    ppermute x5, waiting for transfers between devices: 10.2 us -> 16.4 us  [butterfly_sum(): value = value + lax.ppermute(value, axis, pairs)]
    ppermute x3, waiting for transfers between devices: 1.89 us -> 3.78 us  [gather_all(): parts.append(lax.ppermute(value, axis, pairs))]
where the time goes in v4:
time: 162 us; the launch traced here: 160 us
  waiting for transfers between devices  89.3 us (55%)
  starting transfers between devices  24.2 us (15%)
  between operations  17.9 us (11%)
  local copies, waits for them, and re-layouts  12.1 us (7%)
  Pallas kernels  7.71 us (5%)
  matrix products  5.27 us (3%)
  other arithmetic  3.53 us (2%)
    all_gather x1, waiting for transfers between devices, per_device(): theta_all = lax.all_gather(theta_loc, 'blk', axis=0, tiled=True)  68.5 us
    ppermute x5, starting transfers between devices, butterfly_sum(): value = value + lax.ppermute(value, axis, pairs)  20.9 us
    ppermute x5, waiting for transfers between devices, butterfly_sum(): value = value + lax.ppermute(value, axis, pairs)  16.4 us
    unnamed x14, local copies, waits for them, and re-layouts  9.11 us
    pallas_call x1, Pallas kernels, masked_apply(): pl.pallas_call(masked_apply_kernel, grid_spec=grid_spec, out_shape=jax.Sh...  7.71 us
    ppermute x3, waiting for transfers between devices, gather_all(): parts.append(lax.ppermute(value, axis, pairs))  3.78 us
    ppermute x3, starting transfers between devices, gather_all(): parts.append(lax.ppermute(value, axis, pairs))  3.3 us
  transfers between devices with their start and end apart: 9, of which 8 were waited for; matrix products, arithmetic and copies ran while one was open for 4% of the time, Pallas kernels for 0%

profile of v4, /device:TPU:0, one launch (start us, length us, event | category | flops | bytes accessed | tf_op | source)
XLA Modules:
  0.0 160.1 jit_solution(12428439437588457918)
XLA Ops:
  9.2 2.8 %fusion.13 = (s32[]{:T(128)}, s32[]{:T(128)}) fusion(s32[1,4096]{1,0:T(1,128)} %sec_j_ref.1, s32[]{:T(128)} %bitcast, s32[]{:T(128)} %bitcast.2), kind=kLoop, calls=%fused_computation.28 | loop fusion | flops 24574 | bytes 16400 | tf_op jit(solution)/shard_map/reduce_sum | solution.py:59
  15.7 1.1 copy.36
  16.9 68.5 %all-gather.3.cloned.1.call-done = bf16[1,4096,2048]{2,1,0:T(8,128)(2,1)} async-done(((bf16[1,128,2048]{2,1,0:T(8,128)(2,1)}), bf16[1,4096,2048]{2,1,0:T(8,128)(2,1)}) %all-gather.3.cloned.1.call-update) | async-done | bytes 16777232 | tf_op jit(solution)/shard_map/all_gather | solution.py:100
  85.4 0.7 copy-done.1
  86.2 7.7 %shard_map.68 = f32[8,128,2048]{2,1,0:T(8,128)} custom-call(s32[2]{0:T(128)S(1)} %pad_add_fusion.span_ref, bf16[8,128,4096]{2,1,0:T(8,128)(2,1)} %bitcast.83, bf16[4096,2048]{1,0:T(8,128)(2,1)} %bitcast.82, s32[1,4096]{1,0:T(1,128)S(1)} %copy-done.1, s32[128,1]{1,0:T(8,128)S(1)} %copy.18.sec_i_ref), custom_call_target="tpu_custom_call" | custom-call | tf_op jit(solution)/shard_map/pallas_call | solution.py:77
  93.9 5.4 %copy.35 = f32[128,8,16,128]{3,2,1,0:T(8,128)S(1)} copy(f32[128,8,16,128]{3,1,2,0:T(8,128)} %bitcast.81) | data formatting | bytes 16777216
  99.3 2.6 %fusion.2 = f32[128,16,128]{2,1,0:T(8,128)S(1)} fusion(f32[1,8,16,16]{3,2,1,0:T(8,128)S(1)} %copy-done, f32[8,128,16,128]{3,2,1,0:T(8,128)S(1)} %bitcast.80), kind=kOutput, calls=%fused_computation.3 | convolution fusion | flops 201326592 | bytes 9445376 | tf_op jit(solution)/shard_map/wpq,wiqc->ipc/dot_general | solution.py:103
  101.9 0.7 convolution_bitcast_fusion
  102.6 3.0 %collective-permute-start = (f32[128,128]{0,1:T(8,128)S(1)}, f32[128,128]{0,1:T(8,128)S(1)}, u32[]{:S(2)}, u32[]{:S(2)}) collective-permute-start(f32[128,128]{0,1:T(8,128)S(1)} %convolution_bitcast_fusion), channel_id=1, source_target_pairs={{0,1},{1,0},{2,3},{3,2},{4,5},{5,4},{6,7},{7,6},{8,9},{9,8},{10,11... | collective-permute-start | bytes 196616 | tf_op jit(solution)/shard_map/ppermute | solution.py:22
  105.6 0.9 collective-permute-done
  106.6 1.1 collective-permute-start.1
  107.7 3.3 %collective-permute-done.1 = f32[128,128]{0,1:T(8,128)S(1)} collective-permute-done((f32[128,128]{0,1:T(8,128)S(1)}, f32[128,128]{0,1:T(8,128)S(1)}, u32[]{:S(2)}, u32[]{:S(2)}) %collective-permute-start.1) | collective-permute-done | bytes 65568 | tf_op jit(solution)/shard_map/ppermute | solution.py:22
  111.0 15.9 %collective-permute-start.2 = (f32[128,128]{0,1:T(8,128)S(1)}, f32[128,128]{0,1:T(8,128)S(1)}, u32[]{:S(2)}, u32[]{:S(2)}) collective-permute-start(f32[128,128]{0,1:T(8,128)S(1)} %add.62), channel_id=1, source_target_pairs={{0,4},{1,5},{2,6},{3,7},{4,0},{5,1},{6,2},{7,3},{8,12},{9,13},{10,... | collective-permute-start | bytes 196616 | tf_op jit(solution)/shard_map/ppermute | solution.py:22
  126.9 2.2 %collective-permute-done.2 = f32[128,128]{0,1:T(8,128)S(1)} collective-permute-done((f32[128,128]{0,1:T(8,128)S(1)}, f32[128,128]{0,1:T(8,128)S(1)}, u32[]{:S(2)}, u32[]{:S(2)}) %collective-permute-start.2) | collective-permute-done | bytes 65568 | tf_op jit(solution)/shard_map/ppermute | solution.py:22
  129.4 4.8 %collective-permute-done.3 = f32[128,128]{0,1:T(8,128)S(1)} collective-permute-done((f32[128,128]{0,1:T(8,128)S(1)}, f32[128,128]{0,1:T(8,128)S(1)}, u32[]{:S(2)}, u32[]{:S(2)}) %collective-permute-start.3) | collective-permute-done | bytes 65568 | tf_op jit(solution)/shard_map/ppermute | solution.py:22
  134.2 0.7 collective-permute-start.4
  135.0 5.1 %collective-permute-done.4 = f32[128,128]{0,1:T(8,128)S(1)} collective-permute-done((f32[128,128]{0,1:T(8,128)S(1)}, f32[128,128]{0,1:T(8,128)S(1)}, u32[]{:S(2)}, u32[]{:S(2)}) %collective-permute-start.4) | collective-permute-done | bytes 65568 | tf_op jit(solution)/shard_map/ppermute | solution.py:22
  141.5 1.3 collective-permute-start.6
  142.8 1.9 %collective-permute-start.7 = (f32[128,128]{0,1:T(8,128)S(1)}, f32[128,128]{0,1:T(8,128)S(1)}, u32[]{:S(2)}, u32[]{:S(2)}) collective-permute-start(f32[128,128]{0,1:T(8,128)S(1)} %multiply_divide_fusion), channel_id=1, source_target_pairs={{0,96},{32,0},{64,32},{96,64},{1,97},{33,1},{65,33},{97,65},{2,98}... | collective-permute-start | bytes 196616 | tf_op jit(solution)/shard_map/ppermute | solution.py:33
  144.7 2.9 %collective-permute-done.5 = f32[128,128]{0,1:T(8,128)S(1)} collective-permute-done((f32[128,128]{0,1:T(8,128)S(1)}, f32[128,128]{0,1:T(8,128)S(1)}, u32[]{:S(2)}, u32[]{:S(2)}) %collective-permute-start.5) | collective-permute-done | bytes 65568 | tf_op jit(solution)/shard_map/ppermute | solution.py:33
  147.6 0.9 collective-permute-done.7
  150.7 0.9 convolution_convert_fusion
  151.5 1.0 copy.28
  152.5 0.7 copy.29
  (37 shorter events, 5.9 us)
Async XLA Ops:
  7.2 92.1 %copy-start = (f32[1,8,16,16]{3,2,1,0:T(8,128)S(1)}, f32[1,8,16,16]{3,2,1,0:T(8,128)}, u32[]{:S(2)}) copy-start(f32[1,8,16,16]{3,2,1,0:T(8,128)} %param.8) | copy-start | bytes 24580
  7.2 78.3 %all-gather.3.cloned.1.call-start = ((), (), s32[]{:S(2)}) async-start(), calls=%async_computation | async-start | bytes 17301504 | tf_op jit(solution)/shard_map/all_gather | solution.py:100
  85.4 0.7 copy-start.1
  99.3 30.0 %copy-start.2 = (f32[128,128]{1,0:T(8,128)S(1)}, f32[128,128]{1,0:T(8,128)}, u32[]{:S(2)}) copy-start(f32[128,128]{1,0:T(8,128)} %param.9) | copy-start | bytes 196612
  102.6 3.9 %collective-permute-start = (f32[128,128]{0,1:T(8,128)S(1)}, f32[128,128]{0,1:T(8,128)S(1)}, u32[]{:S(2)}, u32[]{:S(2)}) collective-permute-start(f32[128,128]{0,1:T(8,128)S(1)} %convolution_bitcast_fusion), channel_id=1, source_target_pairs={{0,1},{1,0},{2,3},{3,2},{4,5},{5,4},{6,7},{7,6},{8,9},{9,8},{10,11... | collective-permute-start | bytes 196616 | tf_op jit(solution)/shard_map/ppermute | solution.py:22
  106.6 4.4 %collective-permute-start.1 = (f32[128,128]{0,1:T(8,128)S(1)}, f32[128,128]{0,1:T(8,128)S(1)}, u32[]{:S(2)}, u32[]{:S(2)}) collective-permute-start(f32[128,128]{0,1:T(8,128)S(1)} %add.61), channel_id=1, source_target_pairs={{0,2},{1,3},{2,0},{3,1},{4,6},{5,7},{6,4},{7,5},{8,10},{9,11},{10,... | collective-permute-start | bytes 196616 | tf_op jit(solution)/shard_map/ppermute | solution.py:22
  111.0 18.2 %collective-permute-start.2 = (f32[128,128]{0,1:T(8,128)S(1)}, f32[128,128]{0,1:T(8,128)S(1)}, u32[]{:S(2)}, u32[]{:S(2)}) collective-permute-start(f32[128,128]{0,1:T(8,128)S(1)} %add.62), channel_id=1, source_target_pairs={{0,4},{1,5},{2,6},{3,7},{4,0},{5,1},{6,2},{7,3},{8,12},{9,13},{10,... | collective-permute-start | bytes 196616 | tf_op jit(solution)/shard_map/ppermute | solution.py:22
  129.2 5.0 %collective-permute-start.3 = (f32[128,128]{0,1:T(8,128)S(1)}, f32[128,128]{0,1:T(8,128)S(1)}, u32[]{:S(2)}, u32[]{:S(2)}) collective-permute-start(f32[128,128]{0,1:T(8,128)S(1)} %add.63), channel_id=1, source_target_pairs={{0,8},{1,9},{2,10},{3,11},{4,12},{5,13},{6,14},{7,15},{8,0},{9,1},... | collective-permute-start | bytes 196616 | tf_op jit(solution)/shard_map/ppermute | solution.py:22
  134.2 5.8 %collective-permute-start.4 = (f32[128,128]{0,1:T(8,128)S(1)}, f32[128,128]{0,1:T(8,128)S(1)}, u32[]{:S(2)}, u32[]{:S(2)}) collective-permute-start(f32[128,128]{0,1:T(8,128)S(1)} %add.64), channel_id=1, source_target_pairs={{0,16},{1,17},{2,18},{3,19},{4,20},{5,21},{6,22},{7,23},{8,24},{9,... | collective-permute-start | bytes 196616 | tf_op jit(solution)/shard_map/ppermute | solution.py:22
  141.4 6.2 %collective-permute-start.5 = (f32[128,128]{0,1:T(8,128)S(1)}, f32[128,128]{0,1:T(8,128)S(1)}, u32[]{:S(2)}, u32[]{:S(2)}) collective-permute-start(f32[128,128]{0,1:T(8,128)S(1)} %multiply_divide_fusion), channel_id=1, source_target_pairs={{0,32},{32,64},{64,96},{96,0},{1,33},{33,65},{65,97},{97,1},{2,34}... | collective-permute-start | bytes 196616 | tf_op jit(solution)/shard_map/ppermute | solution.py:33
  141.5 6.2 %collective-permute-start.6 = (f32[128,128]{0,1:T(8,128)S(1)}, f32[128,128]{0,1:T(8,128)S(1)}, u32[]{:S(2)}, u32[]{:S(2)}) collective-permute-start(f32[128,128]{0,1:T(8,128)S(1)} %multiply_divide_fusion), channel_id=1, source_target_pairs={{0,64},{32,96},{64,0},{96,32},{1,65},{33,97},{65,1},{97,33},{2,66}... | collective-permute-start | bytes 196616 | tf_op jit(solution)/shard_map/ppermute | solution.py:33
  142.8 5.7 %collective-permute-start.7 = (f32[128,128]{0,1:T(8,128)S(1)}, f32[128,128]{0,1:T(8,128)S(1)}, u32[]{:S(2)}, u32[]{:S(2)}) collective-permute-start(f32[128,128]{0,1:T(8,128)S(1)} %multiply_divide_fusion), channel_id=1, source_target_pairs={{0,96},{32,0},{64,32},{96,64},{1,97},{33,1},{65,33},{97,65},{2,98}... | collective-permute-start | bytes 196616 | tf_op jit(solution)/shard_map/ppermute | solution.py:33
Sparse Core Ops, SparseCore 0:
  10.2 75.1 all-gather.2

commit v5 on v3

--- a/solution.py
+++ b/solution.py
@@ -7,7 +7,7 @@
 from jax.experimental.pallas import tpu as pltpu
 from jax.sharding import PartitionSpec as P
 
-K_TILE = 512
+K_TILE = 256
 
 
 def matprod(first, second):
@@ -104,11 +104,12 @@
     theta_all = lax.all_gather(theta_loc, "blk", axis=0, tiled=True)
     applied = masked_apply(env_loc, theta_all, sec_all, my_sec, phys)
     applied = applied.reshape(chain_w, phys, rows_dev, cols)
+    theta_f = theta_loc.astype(jnp.float32).reshape(rows_dev, phys, cols)
+    theta_ops = jnp.einsum("wpq,ipc->wqic", ops_loc, theta_f, precision=lax.Precision.HIGH)
+    partial_intersection = jnp.einsum(
+        "wqic,wqid->cd", theta_ops, applied, precision=lax.Precision.HIGH
+    )
     acted = jnp.einsum("wpq,wqic->ipc", ops_loc, applied, precision=lax.Precision.HIGH)
-    theta_f = theta_loc.astype(jnp.float32).reshape(rows_dev, phys, cols)
-    partial_intersection = jnp.einsum(
-        "ipc,ipd->cd", theta_f, acted, precision=lax.Precision.HIGH
-    )
     intersection = butterfly_sum(partial_intersection, "blk")
     transfer = (
         intersection

time: 163 us -> 172 us (1.055); the launches traced: 164 us -> 171 us
  matrix products: 12.7 us -> 30.7 us
  starting transfers between devices: 29.4 us -> 15.1 us
  Pallas kernels: 9.04 us -> 19.9 us
  waiting for transfers between devices: 84.3 us -> 77.4 us
    dot_general x1 -> x2, matrix products: 0.72 us -> 18.8 us  [the longest x1 14.2 us: per_device(): jnp.einsum('wqic,wqid->cd', theta_ops, applied, precision=lax.Precision.H...]
    ppermute x5, starting transfers between devices: 22.6 us -> 8.53 us  [butterfly_sum(): value = value + lax.ppermute(value, axis, pairs)]
    pallas_call x1, Pallas kernels: 9.04 us -> 19.9 us  [masked_apply(): pl.pallas_call(masked_apply_kernel, grid_spec=grid_spec, out_shape=jax.Sh...]
    all_gather x1, waiting for transfers between devices: 68.5 us -> 63.6 us  [per_device(): theta_all = lax.all_gather(theta_loc, 'blk', axis=0, tiled=True)]
    ppermute x3, waiting for transfers between devices: 4.25 us -> 0.01 us  [gather_all(): parts.append(lax.ppermute(value, axis, pairs))]
    ppermute x5, waiting for transfers between devices: 10.8 us -> 13.1 us  [butterfly_sum(): value = value + lax.ppermute(value, axis, pairs)]
    unnamed x13 -> x15, local copies, waits for them, and re-layouts: 3.72 us -> 3.01 us
  transfers between devices with their start and end apart: 9 -> 9, of which waited for: 9 -> 6; matrix products, arithmetic and copies ran while one was open for 4% -> 12% of each run, Pallas kernels for 0% -> 0%
where the time goes in v5:
time: 172 us; the launch traced here: 171 us
  waiting for transfers between devices  77.4 us (45%)
  matrix products  30.7 us (18%)
  Pallas kernels  19.9 us (12%)
  between operations  18.3 us (11%)
  starting transfers between devices  15.1 us (9%)
  local copies, waits for them, and re-layouts  5.9 us (3%)
  other arithmetic  3.53 us (2%)
    all_gather x1, waiting for transfers between devices, per_device(): theta_all = lax.all_gather(theta_loc, 'blk', axis=0, tiled=True)  63.6 us
    pallas_call x1, Pallas kernels, masked_apply(): pl.pallas_call(masked_apply_kernel, grid_spec=grid_spec, out_shape=jax.Sh...  19.9 us
    dot_general x1, matrix products, per_device(): jnp.einsum('wqic,wqid->cd', theta_ops, applied, precision=lax.Precision.H...  14.2 us
    ppermute x5, waiting for transfers between devices, butterfly_sum(): value = value + lax.ppermute(value, axis, pairs)  13.1 us
    dot_general x1, matrix products, per_device(): jnp.einsum('wpq,wqic->ipc', ops_loc, applied, precision=lax.Precision.HIGH)  10 us
    ppermute x5, starting transfers between devices, butterfly_sum(): value = value + lax.ppermute(value, axis, pairs)  8.53 us
    ppermute x3, starting transfers between devices, gather_all(): parts.append(lax.ppermute(value, axis, pairs))  6.49 us
    dot_general x1, matrix products, per_device(): jnp.einsum('wpq,ipc->wqic', ops_loc, theta_f, precision=lax.Precision.HIGH)  4.58 us
  transfers between devices with their start and end apart: 9, of which 6 were waited for; matrix products, arithmetic and copies ran while one was open for 12% of the time, Pallas kernels for 0%

profile of v5, /device:TPU:0, one launch (start us, length us, event | category | flops | bytes accessed | tf_op | source)
XLA Modules:
  0.0 170.8 jit_solution(14831488690323779368)
XLA Ops:
  7.2 0.7 all-gather.3.cloned.1.call-update
  9.2 2.8 %fusion.21 = (s32[]{:T(128)}, s32[]{:T(128)}) fusion(s32[1,4096]{1,0:T(1,128)} %sec_j_ref.1, s32[]{:T(128)} %bitcast, s32[]{:T(128)} %bitcast.2), kind=kLoop, calls=%fused_computation.33 | loop fusion | flops 24574 | bytes 16400 | tf_op jit(solution)/shard_map/reduce_sum | solution.py:63
  15.3 0.7 fusion.32
  16.0 1.1 copy.25
  17.3 4.6 %fusion.16 = f32[8,16,128,128]{3,1,2,0:T(8,128)} fusion(bf16[128,16,128,1]{2,1,0,3:T(8,128)(2,1)S(1)} %bitcast.79, f32[1,8,16,16]{3,2,1,0:T(8,128)S(1)} %copy-done), kind=kOutput, calls=%fused_computation.21 | convolution fusion | flops 201326592 | bytes 8921088 | tf_op jit(solution)/shard_map/wpq,ipc->wqic/dot_general | solution.py:108
  21.9 63.6 %all-gather.3.cloned.1.call-done = bf16[1,4096,2048]{2,1,0:T(8,128)(2,1)} async-done(((bf16[1,128,2048]{2,1,0:T(8,128)(2,1)}), bf16[1,4096,2048]{2,1,0:T(8,128)(2,1)}) %all-gather.3.cloned.1.call-update) | async-done | bytes 16777232 | tf_op jit(solution)/shard_map/all_gather | solution.py:104
  85.5 19.9 %shard_map.68 = f32[128,128,128]{2,1,0:T(8,128)} custom-call(s32[2]{0:T(128)S(1)} %pad_add_fusion.span_ref, bf16[8,128,4096]{2,1,0:T(8,128)(2,1)} %bitcast.78, bf16[4096,2048]{1,0:T(8,128)(2,1)} %bitcast.77, s32[1,4096]{1,0:T(1,128)S(1)} %copy-done.1, s32[128,1]{1,0:T(8,128)S(1)} %copy.7.sec_i_ref), custom_call_target="tpu_custom_call" | custom-call | tf_op jit(solution)/shard_map/pallas_call | solution.py:81
  105.4 14.2 %fusion.5 = f32[128,128]{1,0:T(8,128)S(1)} fusion(f32[8,16,128,128]{3,2,1,0:T(8,128)} %bitcast.75, f32[8,16,128,128]{3,1,2,0:T(8,128)S(1)} %copy-done.2), kind=kOutput, calls=%fused_computation.7 | convolution fusion | flops 1610612736 | bytes 16842752 | tf_op jit(solution)/shard_map/wqic,wqid->cd/dot_general | solution.py:109
  119.9 1.0 collective-permute-done
  121.0 1.0 collective-permute-start.1
  122.0 3.3 %collective-permute-done.1 = f32[128,128]{1,0:T(8,128)S(1)} collective-permute-done((f32[128,128]{1,0:T(8,128)S(1)}, f32[128,128]{1,0:T(8,128)S(1)}, u32[]{:S(2)}, u32[]{:S(2)}) %collective-permute-start.1) | collective-permute-done | bytes 65568 | tf_op jit(solution)/shard_map/ppermute | solution.py:22
  125.3 2.6 %collective-permute-start.2 = (f32[128,128]{1,0:T(8,128)S(1)}, f32[128,128]{1,0:T(8,128)S(1)}, u32[]{:S(2)}, u32[]{:S(2)}) collective-permute-start(f32[128,128]{1,0:T(8,128)S(1)} %add.62), channel_id=1, source_target_pairs={{0,4},{1,5},{2,6},{3,7},{4,0},{5,1},{6,2},{7,3},{8,12},{9,13},{10,... | collective-permute-start | bytes 196616 | tf_op jit(solution)/shard_map/ppermute | solution.py:22
  128.0 3.1 %collective-permute-done.2 = f32[128,128]{1,0:T(8,128)S(1)} collective-permute-done((f32[128,128]{1,0:T(8,128)S(1)}, f32[128,128]{1,0:T(8,128)S(1)}, u32[]{:S(2)}, u32[]{:S(2)}) %collective-permute-start.2) | collective-permute-done | bytes 65568 | tf_op jit(solution)/shard_map/ppermute | solution.py:22
  131.2 1.5 collective-permute-start.3
  132.7 2.8 %collective-permute-done.3 = f32[128,128]{1,0:T(8,128)S(1)} collective-permute-done((f32[128,128]{1,0:T(8,128)S(1)}, f32[128,128]{1,0:T(8,128)S(1)}, u32[]{:S(2)}, u32[]{:S(2)}) %collective-permute-start.3) | collective-permute-done | bytes 65568 | tf_op jit(solution)/shard_map/ppermute | solution.py:22
  135.5 3.0 %collective-permute-start.4 = (f32[128,128]{1,0:T(8,128)S(1)}, f32[128,128]{1,0:T(8,128)S(1)}, u32[]{:S(2)}, u32[]{:S(2)}) collective-permute-start(f32[128,128]{1,0:T(8,128)S(1)} %add.64), channel_id=1, source_target_pairs={{0,16},{1,17},{2,18},{3,19},{4,20},{5,21},{6,22},{7,23},{8,24},{9,... | collective-permute-start | bytes 196616 | tf_op jit(solution)/shard_map/ppermute | solution.py:22
  138.6 2.8 %collective-permute-done.4 = f32[128,128]{1,0:T(8,128)S(1)} collective-permute-done((f32[128,128]{1,0:T(8,128)S(1)}, f32[128,128]{1,0:T(8,128)S(1)}, u32[]{:S(2)}, u32[]{:S(2)}) %collective-permute-start.4) | collective-permute-done | bytes 65568 | tf_op jit(solution)/shard_map/ppermute | solution.py:22
  142.7 3.2 %collective-permute-start.5 = (f32[128,128]{1,0:T(8,128)S(1)}, f32[128,128]{1,0:T(8,128)S(1)}, u32[]{:S(2)}, u32[]{:S(2)}) collective-permute-start(f32[128,128]{1,0:T(8,128)S(1)} %multiply_divide_fusion), channel_id=1, source_target_pairs={{0,32},{32,64},{64,96},{96,0},{1,33},{33,65},{65,97},{97,1},{2,34}... | collective-permute-start | bytes 196616 | tf_op jit(solution)/shard_map/ppermute | solution.py:33
  145.9 2.2 %collective-permute-start.6 = (f32[128,128]{1,0:T(8,128)S(1)}, f32[128,128]{1,0:T(8,128)S(1)}, u32[]{:S(2)}, u32[]{:S(2)}) collective-permute-start(f32[128,128]{1,0:T(8,128)S(1)} %multiply_divide_fusion), channel_id=1, source_target_pairs={{0,64},{32,96},{64,0},{96,32},{1,65},{33,97},{65,1},{97,33},{2,66}... | collective-permute-start | bytes 196616 | tf_op jit(solution)/shard_map/ppermute | solution.py:33
  148.2 1.0 collective-permute-start.7
  149.2 10.0 %fusion.3 = f32[128,128,16,1]{1,2,3,0:T(8,128)S(1)} fusion(f32[8,16,128,128]{3,2,1,0:T(8,128)} %bitcast.76, f32[1,8,16,16]{3,2,1,0:T(8,128)S(1)} %copy-done), kind=kOutput, calls=%fused_computation.4 | convolution fusion | flops 201326592 | bytes 9445376 | tf_op jit(solution)/shard_map/wpq,wqic->ipc/dot_general | solution.py:112
  161.3 0.9 convolution_convert_fusion
  162.2 1.0 copy.13
  163.2 0.7 copy.14
  (38 shorter events, 4.5 us)
Async XLA Ops:
  7.2 10.1 %copy-start = (f32[1,8,16,16]{3,2,1,0:T(8,128)S(1)}, f32[1,8,16,16]{3,2,1,0:T(8,128)}, u32[]{:S(2)}) copy-start(f32[1,8,16,16]{3,2,1,0:T(8,128)} %param.8) | copy-start | bytes 24580
  7.2 78.3 %copy-start.1 = (s32[1,4096]{1,0:T(1,128)S(1)}, s32[1,4096]{1,0:T(1,128)}, u32[]{:S(2)}) copy-start(s32[1,4096]{1,0:T(1,128)} %sec_j_ref.1) | copy-start | bytes 49156
  7.2 78.3 %all-gather.3.cloned.1.call-start = ((), (), s32[]{:S(2)}) async-start(), calls=%async_computation | async-start | bytes 17301504 | tf_op jit(solution)/shard_map/all_gather | solution.py:104
  85.5 19.9 %copy-start.2 = (f32[8,16,128,128]{3,1,2,0:T(8,128)S(1)}, f32[8,16,128,128]{3,1,2,0:T(8,128)}, u32[]{:S(2)}) copy-start(f32[8,16,128,128]{3,1,2,0:T(8,128)} %fusion.16) | copy-start | bytes 25165828
  105.4 22.5 %copy-start.3 = (f32[128,128]{1,0:T(8,128)S(1)}, f32[128,128]{1,0:T(8,128)}, u32[]{:S(2)}) copy-start(f32[128,128]{1,0:T(8,128)} %param.9) | copy-start | bytes 196612
  119.6 1.3 collective-permute-start
  121.0 4.3 %collective-permute-start.1 = (f32[128,128]{1,0:T(8,128)S(1)}, f32[128,128]{1,0:T(8,128)S(1)}, u32[]{:S(2)}, u32[]{:S(2)}) collective-permute-start(f32[128,128]{1,0:T(8,128)S(1)} %add.61), channel_id=1, source_target_pairs={{0,2},{1,3},{2,0},{3,1},{4,6},{5,7},{6,4},{7,5},{8,10},{9,11},{10,... | collective-permute-start | bytes 196616 | tf_op jit(solution)/shard_map/ppermute | solution.py:22
  125.3 5.8 %collective-permute-start.2 = (f32[128,128]{1,0:T(8,128)S(1)}, f32[128,128]{1,0:T(8,128)S(1)}, u32[]{:S(2)}, u32[]{:S(2)}) collective-permute-start(f32[128,128]{1,0:T(8,128)S(1)} %add.62), channel_id=1, source_target_pairs={{0,4},{1,5},{2,6},{3,7},{4,0},{5,1},{6,2},{7,3},{8,12},{9,13},{10,... | collective-permute-start | bytes 196616 | tf_op jit(solution)/shard_map/ppermute | solution.py:22
  131.2 4.3 %collective-permute-start.3 = (f32[128,128]{1,0:T(8,128)S(1)}, f32[128,128]{1,0:T(8,128)S(1)}, u32[]{:S(2)}, u32[]{:S(2)}) collective-permute-start(f32[128,128]{1,0:T(8,128)S(1)} %add.63), channel_id=1, source_target_pairs={{0,8},{1,9},{2,10},{3,11},{4,12},{5,13},{6,14},{7,15},{8,0},{9,1},... | collective-permute-start | bytes 196616 | tf_op jit(solution)/shard_map/ppermute | solution.py:22
  135.5 5.8 %collective-permute-start.4 = (f32[128,128]{1,0:T(8,128)S(1)}, f32[128,128]{1,0:T(8,128)S(1)}, u32[]{:S(2)}, u32[]{:S(2)}) collective-permute-start(f32[128,128]{1,0:T(8,128)S(1)} %add.64), channel_id=1, source_target_pairs={{0,16},{1,17},{2,18},{3,19},{4,20},{5,21},{6,22},{7,23},{8,24},{9,... | collective-permute-start | bytes 196616 | tf_op jit(solution)/shard_map/ppermute | solution.py:22
  142.7 16.5 %collective-permute-start.5 = (f32[128,128]{1,0:T(8,128)S(1)}, f32[128,128]{1,0:T(8,128)S(1)}, u32[]{:S(2)}, u32[]{:S(2)}) collective-permute-start(f32[128,128]{1,0:T(8,128)S(1)} %multiply_divide_fusion), channel_id=1, source_target_pairs={{0,32},{32,64},{64,96},{96,0},{1,33},{33,65},{65,97},{97,1},{2,34}... | collective-permute-start | bytes 196616 | tf_op jit(solution)/shard_map/ppermute | solution.py:33
  145.9 13.3 %collective-permute-start.6 = (f32[128,128]{1,0:T(8,128)S(1)}, f32[128,128]{1,0:T(8,128)S(1)}, u32[]{:S(2)}, u32[]{:S(2)}) collective-permute-start(f32[128,128]{1,0:T(8,128)S(1)} %multiply_divide_fusion), channel_id=1, source_target_pairs={{0,64},{32,96},{64,0},{96,32},{1,65},{33,97},{65,1},{97,33},{2,66}... | collective-permute-start | bytes 196616 | tf_op jit(solution)/shard_map/ppermute | solution.py:33
  148.2 11.1 %collective-permute-start.7 = (f32[128,128]{1,0:T(8,128)S(1)}, f32[128,128]{1,0:T(8,128)S(1)}, u32[]{:S(2)}, u32[]{:S(2)}) collective-permute-start(f32[128,128]{1,0:T(8,128)S(1)} %multiply_divide_fusion), channel_id=1, source_target_pairs={{0,96},{32,0},{64,32},{96,64},{1,97},{33,1},{65,33},{97,65},{2,98}... | collective-permute-start | bytes 196616 | tf_op jit(solution)/shard_map/ppermute | solution.py:33
Sparse Core Ops, SparseCore 0:
  10.3 75.1 all-gather.2

commit v6 on v4

--- a/solution.py
+++ b/solution.py
@@ -36,7 +36,7 @@
     return jnp.zeros_like(stacked).at[order].set(stacked)
 
 
-def masked_apply_kernel(span_ref, env_ref, theta_ref, sec_j_ref, sec_i_ref, out_ref):
+def masked_apply_kernel(span_ref, env_ref, theta_ref, sec_j_ref, sec_i_ref, to_ref, out_ref, inter_ref):
     step = pl.program_id(0)
 
     @pl.when(step == 0)
@@ -51,8 +51,30 @@
             env_w = jnp.where(same, env_ref[w], jnp.zeros_like(env_ref[w]))
             out_ref[w] += jnp.dot(env_w, block, preferred_element_type=jnp.float32)
 
+    @pl.when(step == pl.num_programs(0) - 1)
+    def _():
+        cols = inter_ref.shape[1]
+        phys = out_ref.shape[2] // cols
 
-def masked_apply(env_loc, theta_all, sec_all, my_sec):
+        def one_w(w, acc):
+            for q in range(phys):
+                part = out_ref[w, :, q * cols:(q + 1) * cols]
+                part_hi = part.astype(jnp.bfloat16)
+                part_lo = (part - part_hi.astype(jnp.float32)).astype(jnp.bfloat16)
+                t = to_ref[w, q * cols:(q + 1) * cols, :]
+                t_hi = t.astype(jnp.bfloat16)
+                t_lo = (t - t_hi.astype(jnp.float32)).astype(jnp.bfloat16)
+                acc = acc + jnp.dot(t_hi, part_hi, preferred_element_type=jnp.float32)
+                acc = acc + jnp.dot(t_hi, part_lo, preferred_element_type=jnp.float32)
+                acc = acc + jnp.dot(t_lo, part_hi, preferred_element_type=jnp.float32)
+            return acc
+
+        inter_ref[...] = lax.fori_loop(
+            0, out_ref.shape[0], one_w, jnp.zeros(inter_ref.shape, jnp.float32)
+        )
+
+
+def masked_apply(env_loc, theta_all, sec_all, my_sec, theta_ops, cols):
     chain_w, rows_dev, depth = env_loc.shape
     width = theta_all.shape[1]
     tiles = depth // K_TILE
@@ -71,17 +93,24 @@
             pl.BlockSpec((K_TILE, width), lambda k, s: (tile_of(k, s), 0)),
             pl.BlockSpec((1, K_TILE), lambda k, s: (0, tile_of(k, s))),
             pl.BlockSpec((rows_dev, 1), lambda k, s: (0, 0)),
+            pl.BlockSpec((chain_w, width, rows_dev), lambda k, s: (0, 0, 0)),
         ],
-        out_specs=pl.BlockSpec((chain_w, rows_dev, width), lambda k, s: (0, 0, 0)),
+        out_specs=[
+            pl.BlockSpec((chain_w, rows_dev, width), lambda k, s: (0, 0, 0)),
+            pl.BlockSpec((cols, cols), lambda k, s: (0, 0)),
+        ],
     )
     return pl.pallas_call(
         masked_apply_kernel,
         grid_spec=grid_spec,
-        out_shape=jax.ShapeDtypeStruct((chain_w, rows_dev, width), jnp.float32),
+        out_shape=[
+            jax.ShapeDtypeStruct((chain_w, rows_dev, width), jnp.float32),
+            jax.ShapeDtypeStruct((cols, cols), jnp.float32),
+        ],
         compiler_params=pltpu.CompilerParams(
-            dimension_semantics=("arbitrary",), vmem_limit_bytes=48 * 1024 * 1024
+            dimension_semantics=("arbitrary",), vmem_limit_bytes=56 * 1024 * 1024
         ),
-    )(span, env_loc, theta_all, sec_all.reshape(1, depth), my_sec.reshape(rows_dev, 1))
+    )(span, env_loc, theta_all, sec_all.reshape(1, depth), my_sec.reshape(rows_dev, 1), theta_ops)
 
 
 def per_device(theta, left_env, sector_ids, local_ops, edge_env):
@@ -98,13 +127,15 @@
     row_start = my_block * rows_dev
     my_sec = lax.dynamic_slice_in_dim(sec_all, row_start, rows_dev, 0)
     theta_all = lax.all_gather(theta_loc, "blk", axis=0, tiled=True)
-    applied = masked_apply(env_loc, theta_all, sec_all, my_sec)
+    theta_f = theta_loc.astype(jnp.float32).reshape(rows_dev, phys, cols)
+    theta_ops = jnp.einsum(
+        "wpq,ipc->wqci", ops_loc, theta_f, precision=lax.Precision.HIGHEST
+    ).reshape(chain_w, width, rows_dev)
+    applied, partial_intersection = masked_apply(
+        env_loc, theta_all, sec_all, my_sec, theta_ops, cols
+    )
     applied = applied.reshape(chain_w, rows_dev, phys, cols)
     acted = jnp.einsum("wpq,wiqc->ipc", ops_loc, applied, precision=lax.Precision.HIGH)
-    theta_f = theta_loc.astype(jnp.float32).reshape(rows_dev, phys, cols)
-    partial_intersection = jnp.einsum(
-        "ipc,ipd->cd", theta_f, acted, precision=lax.Precision.HIGH
-    )
     intersection = butterfly_sum(partial_intersection, "blk")
     transfer = (
         intersection

time: 162 us -> 166 us (1.025)
  waiting for transfers between devices: 89.3 us -> 63.6 us
  Pallas kernels: 7.71 us -> 29.1 us
  local copies, waits for them, and re-layouts: 12.1 us -> 24.6 us
  starting transfers between devices: 24.2 us -> 13.3 us
  matrix products: 5.27 us -> 12 us
    pallas_call x1, Pallas kernels: 7.71 us -> 29.1 us  [masked_apply(): pl.pallas_call(masked_apply_kernel, grid_spec=grid_spec, out_shape=[jax.S...]
    all_gather x1, waiting for transfers between devices: 68.5 us -> 52.4 us  [per_device(): theta_all = lax.all_gather(theta_loc, 'blk', axis=0, tiled=True)]
    ppermute x5, starting transfers between devices: 20.9 us -> 8.49 us  [butterfly_sum(): value = value + lax.ppermute(value, axis, pairs)]
    transpose x0 -> x1, local copies, waits for them, and re-layouts: none -> 9.44 us  [per_device(): jnp.einsum('wpq,ipc->wqci', ops_loc, theta_f, precision=lax.Precision.HIG...]
    ppermute x5, waiting for transfers between devices: 16.4 us -> 10.5 us  [butterfly_sum(): value = value + lax.ppermute(value, axis, pairs)]
    dot_general x1, matrix products: 0.72 us -> 5.63 us  [per_device(): jnp.einsum('wpq,ipc->wqci', ops_loc, theta_f, precision=lax.Precision.HIG...]
    ppermute x3, waiting for transfers between devices: 3.78 us -> 0.01 us  [gather_all(): parts.append(lax.ppermute(value, axis, pairs))]
    unnamed x14 -> x12, local copies, waits for them, and re-layouts: 9.11 us -> 11.6 us
  transfers between devices with their start and end apart: 9 -> 9, of which waited for: 8 -> 5; matrix products, arithmetic and copies ran while one was open for 4% -> 21% of each run, Pallas kernels for 0% -> 0%
where the time goes in v6:
time: 166 us; the launch traced here: 165 us
  waiting for transfers between devices  63.6 us (38%)
  Pallas kernels  29.1 us (18%)
  local copies, waits for them, and re-layouts  24.6 us (15%)
  between operations  17.9 us (11%)
  starting transfers between devices  13.3 us (8%)
  matrix products  12 us (7%)
  other arithmetic  4.89 us (3%)
    all_gather x1, waiting for transfers between devices, per_device(): theta_all = lax.all_gather(theta_loc, 'blk', axis=0, tiled=True)  52.4 us
    pallas_call x1, Pallas kernels, masked_apply(): pl.pallas_call(masked_apply_kernel, grid_spec=grid_spec, out_shape=[jax.S...  29.1 us
    unnamed x12, local copies, waits for them, and re-layouts  11.6 us
    ppermute x5, waiting for transfers between devices, butterfly_sum(): value = value + lax.ppermute(value, axis, pairs)  10.5 us
    transpose x1, local copies, waits for them, and re-layouts, per_device(): jnp.einsum('wpq,ipc->wqci', ops_loc, theta_f, precision=lax.Precision.HIG...  9.44 us
    ppermute x5, starting transfers between devices, butterfly_sum(): value = value + lax.ppermute(value, axis, pairs)  8.49 us
    dot_general x1, matrix products, per_device(): jnp.einsum('wpq,ipc->wqci', ops_loc, theta_f, precision=lax.Precision.HIG...  5.63 us
    ppermute x3, starting transfers between devices, gather_all(): parts.append(lax.ppermute(value, axis, pairs))  4.76 us
  transfers between devices with their start and end apart: 9, of which 5 were waited for; matrix products, arithmetic and copies ran while one was open for 21% of the time, Pallas kernels for 0%

profile of v6, /device:TPU:0, one launch (start us, length us, event | category | flops | bytes accessed | tf_op | source)
XLA Modules:
  0.0 165.4 jit_solution(12087561437396661)
XLA Ops:
  7.2 0.7 all-gather.3.cloned.1.call-update
  9.2 2.8 %fusion.13 = (s32[]{:T(128)}, s32[]{:T(128)}) fusion(s32[1,4096]{1,0:T(1,128)} %sec_j_ref.1, s32[]{:T(128)} %bitcast, s32[]{:T(128)} %bitcast.2), kind=kLoop, calls=%fused_computation.30 | loop fusion | flops 24574 | bytes 16400 | tf_op jit(solution)/shard_map/reduce_sum | solution.py:81
  15.6 0.7 copy.9.sec_i_ref
  16.3 1.1 copy.22
  17.5 5.6 %convolution_bitcast_fusion = f32[8,16,128,128]{2,1,0,3:T(8,128)} fusion(bf16[128,16,128,1]{2,1,0,3:T(8,128)(2,1)S(1)} %bitcast.90, f32[1,8,16,16]{3,2,1,0:T(8,128)S(1)} %copy-done), kind=kOutput, calls=%fused_computation.3 | convolution fusion | flops 402653184 | bytes 8921088 | tf_op jit(solution)/shard_map/wpq,ipc->wqci/dot_general | solution.py:131
  23.1 9.4 %copy.8 = f32[8,16,128,128]{3,2,1,0:T(8,128)} copy(f32[8,16,128,128]{2,1,0,3:T(8,128)} %convolution_bitcast_fusion) | data formatting | bytes 16777216 | tf_op jit(solution)/shard_map/wpq,ipc->wqci/transpose | solution.py:131
  33.1 52.4 %all-gather.3.cloned.1.call-done = bf16[1,4096,2048]{2,1,0:T(8,128)(2,1)} async-done(((bf16[1,128,2048]{2,1,0:T(8,128)(2,1)}), bf16[1,4096,2048]{2,1,0:T(8,128)(2,1)}) %all-gather.3.cloned.1.call-update) | async-done | bytes 16777232 | tf_op jit(solution)/shard_map/all_gather | solution.py:129
  85.6 29.1 %shard_map.68 = (f32[8,128,2048]{2,1,0:T(8,128)}, f32[128,128]{1,0:T(8,128)}) custom-call(s32[2]{0:T(128)} %pad_add_fusion.span_ref, bf16[8,128,4096]{2,1,0:T(8,128)(2,1)} %bitcast.89, bf16[4096,2048]{1,0:T(8,128)(2,1)} %bitcast.87, s32[1,4096]{1,0:T(1,128)} %sec_j_ref.1, s32[128,1]{1,0:T(8,128)} %copy.9.sec_i_ref, f32[8,2048,128]{2,1,0:T(8,128)} %bitcast.86), custom_call_target="tpu_custom_call" | custom-call | tf_op jit(solution)/shard_map/pallas_call | solution.py:103
  114.9 1.2 collective-permute-done
  116.1 0.9 add.61
  117.0 1.0 collective-permute-start.1
  118.0 3.3 %collective-permute-done.1 = f32[128,128]{1,0:T(8,128)S(1)} collective-permute-done((f32[128,128]{1,0:T(8,128)S(1)}, f32[128,128]{1,0:T(8,128)S(1)}, u32[]{:S(2)}, u32[]{:S(2)}) %collective-permute-start.1) | collective-permute-done | bytes 65568 | tf_op jit(solution)/shard_map/ppermute | solution.py:22
  121.3 2.6 %collective-permute-start.2 = (f32[128,128]{1,0:T(8,128)S(1)}, f32[128,128]{1,0:T(8,128)S(1)}, u32[]{:S(2)}, u32[]{:S(2)}) collective-permute-start(f32[128,128]{1,0:T(8,128)S(1)} %add.62), channel_id=1, source_target_pairs={{0,4},{1,5},{2,6},{3,7},{4,0},{5,1},{6,2},{7,3},{8,12},{9,13},{10,... | collective-permute-start | bytes 196616 | tf_op jit(solution)/shard_map/ppermute | solution.py:22
  124.1 3.1 %collective-permute-done.2 = f32[128,128]{1,0:T(8,128)S(1)} collective-permute-done((f32[128,128]{1,0:T(8,128)S(1)}, f32[128,128]{1,0:T(8,128)S(1)}, u32[]{:S(2)}, u32[]{:S(2)}) %collective-permute-start.2) | collective-permute-done | bytes 65568 | tf_op jit(solution)/shard_map/ppermute | solution.py:22
  127.2 1.6 collective-permute-start.3
  128.8 2.8 %collective-permute-done.3 = f32[128,128]{1,0:T(8,128)S(1)} collective-permute-done((f32[128,128]{1,0:T(8,128)S(1)}, f32[128,128]{1,0:T(8,128)S(1)}, u32[]{:S(2)}, u32[]{:S(2)}) %collective-permute-start.3) | collective-permute-done | bytes 65568 | tf_op jit(solution)/shard_map/ppermute | solution.py:22
  131.6 3.1 %collective-permute-start.4 = (f32[128,128]{1,0:T(8,128)S(1)}, f32[128,128]{1,0:T(8,128)S(1)}, u32[]{:S(2)}, u32[]{:S(2)}) collective-permute-start(f32[128,128]{1,0:T(8,128)S(1)} %add.64), channel_id=1, source_target_pairs={{0,16},{1,17},{2,18},{3,19},{4,20},{5,21},{6,22},{7,23},{8,24},{9,... | collective-permute-start | bytes 196616 | tf_op jit(solution)/shard_map/ppermute | solution.py:22
  134.6 8.6 %copy.23 = f32[128,8,16,128]{3,2,1,0:T(8,128)} copy(f32[128,8,16,128]{3,1,2,0:T(8,128)} %bitcast.88) | data formatting | bytes 16777216
  144.6 1.6 collective-permute-start.5
  146.1 3.2 %collective-permute-start.6 = (f32[128,128]{1,0:T(8,128)S(1)}, f32[128,128]{1,0:T(8,128)S(1)}, u32[]{:S(2)}, u32[]{:S(2)}) collective-permute-start(f32[128,128]{1,0:T(8,128)S(1)} %multiply_divide_fusion), channel_id=1, source_target_pairs={{0,64},{32,96},{64,0},{96,32},{1,65},{33,97},{65,1},{97,33},{2,66}... | collective-permute-start | bytes 196616 | tf_op jit(solution)/shard_map/ppermute | solution.py:33
  149.3 4.5 %fusion = f32[128,128,16,1]{1,2,0,3:T(8,128)S(1)} fusion(f32[1,8,16,16]{3,2,1,0:T(8,128)S(1)} %copy-done, f32[8,128,16,128]{3,2,1,0:T(8,128)} %bitcast.85), kind=kOutput, calls=%fused_computation.1 | convolution fusion | flops 201326592 | bytes 9445376 | tf_op jit(solution)/shard_map/wpq,wiqc->ipc/dot_general | solution.py:138
  155.9 0.9 convolution_convert_fusion
  156.8 1.0 copy.14
  157.8 0.7 copy.15
  (35 shorter events, 5.5 us)
Async XLA Ops:
  7.2 10.3 %copy-start = (f32[1,8,16,16]{3,2,1,0:T(8,128)S(1)}, f32[1,8,16,16]{3,2,1,0:T(8,128)}, u32[]{:S(2)}) copy-start(f32[1,8,16,16]{3,2,1,0:T(8,128)} %param.8) | copy-start | bytes 24580
  7.2 78.4 %all-gather.3.cloned.1.call-start = ((), (), s32[]{:S(2)}) async-start(), calls=%async_computation | async-start | bytes 17301504 | tf_op jit(solution)/shard_map/all_gather | solution.py:129
  85.6 38.4 %copy-start.1 = (f32[128,128]{1,0:T(8,128)S(1)}, f32[128,128]{1,0:T(8,128)}, u32[]{:S(2)}) copy-start(f32[128,128]{1,0:T(8,128)} %param.9) | copy-start | bytes 196612
  114.7 1.5 collective-permute-start
  117.0 4.3 %collective-permute-start.1 = (f32[128,128]{1,0:T(8,128)S(1)}, f32[128,128]{1,0:T(8,128)S(1)}, u32[]{:S(2)}, u32[]{:S(2)}) collective-permute-start(f32[128,128]{1,0:T(8,128)S(1)} %add.61), channel_id=1, source_target_pairs={{0,2},{1,3},{2,0},{3,1},{4,6},{5,7},{6,4},{7,5},{8,10},{9,11},{10,... | collective-permute-start | bytes 196616 | tf_op jit(solution)/shard_map/ppermute | solution.py:22
  121.3 5.8 %collective-permute-start.2 = (f32[128,128]{1,0:T(8,128)S(1)}, f32[128,128]{1,0:T(8,128)S(1)}, u32[]{:S(2)}, u32[]{:S(2)}) collective-permute-start(f32[128,128]{1,0:T(8,128)S(1)} %add.62), channel_id=1, source_target_pairs={{0,4},{1,5},{2,6},{3,7},{4,0},{5,1},{6,2},{7,3},{8,12},{9,13},{10,... | collective-permute-start | bytes 196616 | tf_op jit(solution)/shard_map/ppermute | solution.py:22
  127.2 4.3 %collective-permute-start.3 = (f32[128,128]{1,0:T(8,128)S(1)}, f32[128,128]{1,0:T(8,128)S(1)}, u32[]{:S(2)}, u32[]{:S(2)}) collective-permute-start(f32[128,128]{1,0:T(8,128)S(1)} %add.63), channel_id=1, source_target_pairs={{0,8},{1,9},{2,10},{3,11},{4,12},{5,13},{6,14},{7,15},{8,0},{9,1},... | collective-permute-start | bytes 196616 | tf_op jit(solution)/shard_map/ppermute | solution.py:22
  131.6 11.7 %collective-permute-start.4 = (f32[128,128]{1,0:T(8,128)S(1)}, f32[128,128]{1,0:T(8,128)S(1)}, u32[]{:S(2)}, u32[]{:S(2)}) collective-permute-start(f32[128,128]{1,0:T(8,128)S(1)} %add.64), channel_id=1, source_target_pairs={{0,16},{1,17},{2,18},{3,19},{4,20},{5,21},{6,22},{7,23},{8,24},{9,... | collective-permute-start | bytes 196616 | tf_op jit(solution)/shard_map/ppermute | solution.py:22
  144.6 9.3 %collective-permute-start.5 = (f32[128,128]{1,0:T(8,128)S(1)}, f32[128,128]{1,0:T(8,128)S(1)}, u32[]{:S(2)}, u32[]{:S(2)}) collective-permute-start(f32[128,128]{1,0:T(8,128)S(1)} %multiply_divide_fusion), channel_id=1, source_target_pairs={{0,32},{32,64},{64,96},{96,0},{1,33},{33,65},{65,97},{97,1},{2,34}... | collective-permute-start | bytes 196616 | tf_op jit(solution)/shard_map/ppermute | solution.py:33
  146.1 7.7 %collective-permute-start.6 = (f32[128,128]{1,0:T(8,128)S(1)}, f32[128,128]{1,0:T(8,128)S(1)}, u32[]{:S(2)}, u32[]{:S(2)}) collective-permute-start(f32[128,128]{1,0:T(8,128)S(1)} %multiply_divide_fusion), channel_id=1, source_target_pairs={{0,64},{32,96},{64,0},{96,32},{1,65},{33,97},{65,1},{97,33},{2,66}... | collective-permute-start | bytes 196616 | tf_op jit(solution)/shard_map/ppermute | solution.py:33
  149.3 4.5 %collective-permute-start.7 = (f32[128,128]{1,0:T(8,128)S(1)}, f32[128,128]{1,0:T(8,128)S(1)}, u32[]{:S(2)}, u32[]{:S(2)}) collective-permute-start(f32[128,128]{1,0:T(8,128)S(1)} %multiply_divide_fusion), channel_id=1, source_target_pairs={{0,96},{32,0},{64,32},{96,64},{1,97},{33,1},{65,33},{97,65},{2,98}... | collective-permute-start | bytes 196616 | tf_op jit(solution)/shard_map/ppermute | solution.py:33
Sparse Core Ops, SparseCore 0:
  10.2 75.2 all-gather.2

commit v7 on v4

--- a/solution.py
+++ b/solution.py
@@ -46,10 +46,10 @@
     @pl.when(span_ref[0] + step <= span_ref[1])
     def _():
         same = sec_i_ref[...] == sec_j_ref[...]
-        block = theta_ref[...]
-        for w in range(out_ref.shape[0]):
-            env_w = jnp.where(same, env_ref[w], jnp.zeros_like(env_ref[w]))
-            out_ref[w] += jnp.dot(env_w, block, preferred_element_type=jnp.float32)
+        env = env_ref[...]
+        masked = jnp.where(same[None], env, jnp.zeros_like(env))
+        masked = masked.reshape(out_ref.shape[0], env.shape[2])
+        out_ref[...] += jnp.dot(masked, theta_ref[...], preferred_element_type=jnp.float32)
 
 
 def masked_apply(env_loc, theta_all, sec_all, my_sec):
@@ -72,12 +72,12 @@
             pl.BlockSpec((1, K_TILE), lambda k, s: (0, tile_of(k, s))),
             pl.BlockSpec((rows_dev, 1), lambda k, s: (0, 0)),
         ],
-        out_specs=pl.BlockSpec((chain_w, rows_dev, width), lambda k, s: (0, 0, 0)),
+        out_specs=pl.BlockSpec((chain_w * rows_dev, width), lambda k, s: (0, 0)),
     )
     return pl.pallas_call(
         masked_apply_kernel,
         grid_spec=grid_spec,
-        out_shape=jax.ShapeDtypeStruct((chain_w, rows_dev, width), jnp.float32),
+        out_shape=jax.ShapeDtypeStruct((chain_w * rows_dev, width), jnp.float32),
         compiler_params=pltpu.CompilerParams(
             dimension_semantics=("arbitrary",), vmem_limit_bytes=48 * 1024 * 1024
         ),

time: 162 us -> 161 us (level)
  waiting for transfers between devices: 89.3 us -> 84.9 us
  starting transfers between devices: 24.2 us -> 27.1 us
    ppermute x5, waiting for transfers between devices: 16.4 us -> 12.9 us  [butterfly_sum(): value = value + lax.ppermute(value, axis, pairs)]
    ppermute x3, starting transfers between devices: 3.3 us -> 5.18 us  [gather_all(): parts.append(lax.ppermute(value, axis, pairs))]
  transfers between devices with their start and end apart: 9 -> 9, of which waited for: 8 -> 9; matrix products, arithmetic and copies ran while one was open for 4% -> 4% of each run, Pallas kernels for 0% -> 0%
where the time goes in v7:
time: 161 us; the launch traced here: 158 us
  waiting for transfers between devices  84.9 us (53%)
  starting transfers between devices  27.1 us (17%)
  between operations  17.9 us (11%)
  local copies, waits for them, and re-layouts  12.1 us (8%)
  Pallas kernels  7.69 us (5%)
  matrix products  5.27 us (3%)
  other arithmetic  3.53 us (2%)
    all_gather x1, waiting for transfers between devices, per_device(): theta_all = lax.all_gather(theta_loc, 'blk', axis=0, tiled=True)  68.5 us
    ppermute x5, starting transfers between devices, butterfly_sum(): value = value + lax.ppermute(value, axis, pairs)  21.9 us
    ppermute x5, waiting for transfers between devices, butterfly_sum(): value = value + lax.ppermute(value, axis, pairs)  12.9 us
    unnamed x14, local copies, waits for them, and re-layouts  9.1 us
    pallas_call x1, Pallas kernels, masked_apply(): pl.pallas_call(masked_apply_kernel, grid_spec=grid_spec, out_shape=jax.Sh...  7.69 us
    ppermute x3, starting transfers between devices, gather_all(): parts.append(lax.ppermute(value, axis, pairs))  5.18 us
  transfers between devices with their start and end apart: 9, of which 9 were waited for; matrix products, arithmetic and copies ran while one was open for 4% of the time, Pallas kernels for 0%

profile of v7, /device:TPU:0, one launch (start us, length us, event | category | flops | bytes accessed | tf_op | source)
XLA Modules:
  0.0 158.5 jit_solution(510764267919481345)
XLA Ops:
  9.2 2.8 %fusion.13 = (s32[]{:T(128)}, s32[]{:T(128)}) fusion(s32[1,4096]{1,0:T(1,128)} %sec_j_ref.1, s32[]{:T(128)} %bitcast, s32[]{:T(128)} %bitcast.2), kind=kLoop, calls=%fused_computation.28 | loop fusion | flops 24574 | bytes 16400 | tf_op jit(solution)/shard_map/reduce_sum | solution.py:59
  15.7 1.1 copy.36
  16.9 68.5 %all-gather.3.cloned.1.call-done = bf16[1,4096,2048]{2,1,0:T(8,128)(2,1)} async-done(((bf16[1,128,2048]{2,1,0:T(8,128)(2,1)}), bf16[1,4096,2048]{2,1,0:T(8,128)(2,1)}) %all-gather.3.cloned.1.call-update) | async-done | bytes 16777232 | tf_op jit(solution)/shard_map/all_gather | solution.py:100
  86.2 7.7 %shard_map.68 = f32[1024,2048]{1,0:T(8,128)} custom-call(s32[2]{0:T(128)S(1)} %pad_add_fusion.span_ref, bf16[8,128,4096]{2,1,0:T(8,128)(2,1)} %bitcast.82, bf16[4096,2048]{1,0:T(8,128)(2,1)} %bitcast.81, s32[1,4096]{1,0:T(1,128)S(1)} %copy-done.1, s32[128,1]{1,0:T(8,128)S(1)} %copy.18.sec_i_ref), custom_call_target="tpu_custom_call" | custom-call | tf_op jit(solution)/shard_map/pallas_call | solution.py:77
  93.9 5.4 %copy.35 = f32[128,8,16,128]{3,2,1,0:T(8,128)S(1)} copy(f32[128,8,16,128]{3,1,2,0:T(8,128)} %bitcast.80) | data formatting | bytes 16777216
  99.3 2.6 %fusion.2 = f32[128,16,128]{2,1,0:T(8,128)S(1)} fusion(f32[1,8,16,16]{3,2,1,0:T(8,128)S(1)} %copy-done, f32[8,128,16,128]{3,2,1,0:T(8,128)S(1)} %bitcast.79), kind=kOutput, calls=%fused_computation.3 | convolution fusion | flops 201326592 | bytes 9445376 | tf_op jit(solution)/shard_map/wpq,wiqc->ipc/dot_general | solution.py:103
  102.6 13.5 %collective-permute-start = (f32[128,128]{0,1:T(8,128)S(1)}, f32[128,128]{0,1:T(8,128)S(1)}, u32[]{:S(2)}, u32[]{:S(2)}) collective-permute-start(f32[128,128]{0,1:T(8,128)S(1)} %convolution_bitcast_fusion), channel_id=1, source_target_pairs={{0,1},{1,0},{2,3},{3,2},{4,5},{5,4},{6,7},{7,6},{8,9},{9,8},{10,11... | collective-permute-start | bytes 196616 | tf_op jit(solution)/shard_map/ppermute | solution.py:22
  116.1 0.9 collective-permute-done
  117.0 1.1 collective-permute-start.1
  118.1 3.3 %collective-permute-done.1 = f32[128,128]{0,1:T(8,128)S(1)} collective-permute-done((f32[128,128]{0,1:T(8,128)S(1)}, f32[128,128]{0,1:T(8,128)S(1)}, u32[]{:S(2)}, u32[]{:S(2)}) %collective-permute-start.1) | collective-permute-done | bytes 65568 | tf_op jit(solution)/shard_map/ppermute | solution.py:22
  121.4 2.6 %collective-permute-start.2 = (f32[128,128]{0,1:T(8,128)S(1)}, f32[128,128]{0,1:T(8,128)S(1)}, u32[]{:S(2)}, u32[]{:S(2)}) collective-permute-start(f32[128,128]{0,1:T(8,128)S(1)} %add.62), channel_id=1, source_target_pairs={{0,4},{1,5},{2,6},{3,7},{4,0},{5,1},{6,2},{7,3},{8,12},{9,13},{10,... | collective-permute-start | bytes 196616 | tf_op jit(solution)/shard_map/ppermute | solution.py:22
  124.1 3.2 %collective-permute-done.2 = f32[128,128]{0,1:T(8,128)S(1)} collective-permute-done((f32[128,128]{0,1:T(8,128)S(1)}, f32[128,128]{0,1:T(8,128)S(1)}, u32[]{:S(2)}, u32[]{:S(2)}) %collective-permute-start.2) | collective-permute-done | bytes 65568 | tf_op jit(solution)/shard_map/ppermute | solution.py:22
  127.3 1.6 collective-permute-start.3
  129.0 2.7 %collective-permute-done.3 = f32[128,128]{0,1:T(8,128)S(1)} collective-permute-done((f32[128,128]{0,1:T(8,128)S(1)}, f32[128,128]{0,1:T(8,128)S(1)}, u32[]{:S(2)}, u32[]{:S(2)}) %collective-permute-start.3) | collective-permute-done | bytes 65568 | tf_op jit(solution)/shard_map/ppermute | solution.py:22
  131.7 3.1 %collective-permute-start.4 = (f32[128,128]{0,1:T(8,128)S(1)}, f32[128,128]{0,1:T(8,128)S(1)}, u32[]{:S(2)}, u32[]{:S(2)}) collective-permute-start(f32[128,128]{0,1:T(8,128)S(1)} %add.64), channel_id=1, source_target_pairs={{0,16},{1,17},{2,18},{3,19},{4,20},{5,21},{6,22},{7,23},{8,24},{9,... | collective-permute-start | bytes 196616 | tf_op jit(solution)/shard_map/ppermute | solution.py:22
  134.7 2.8 %collective-permute-done.4 = f32[128,128]{0,1:T(8,128)S(1)} collective-permute-done((f32[128,128]{0,1:T(8,128)S(1)}, f32[128,128]{0,1:T(8,128)S(1)}, u32[]{:S(2)}, u32[]{:S(2)}) %collective-permute-start.4) | collective-permute-done | bytes 65568 | tf_op jit(solution)/shard_map/ppermute | solution.py:22
  138.8 1.5 collective-permute-start.5
  140.3 2.3 %collective-permute-start.6 = (f32[128,128]{0,1:T(8,128)S(1)}, f32[128,128]{0,1:T(8,128)S(1)}, u32[]{:S(2)}, u32[]{:S(2)}) collective-permute-start(f32[128,128]{0,1:T(8,128)S(1)} %multiply_divide_fusion), channel_id=1, source_target_pairs={{0,64},{32,96},{64,0},{96,32},{1,65},{33,97},{65,1},{97,33},{2,66}... | collective-permute-start | bytes 196616 | tf_op jit(solution)/shard_map/ppermute | solution.py:33
  142.6 1.4 collective-permute-start.7
  144.4 1.7 %collective-permute-done.6 = f32[128,128]{0,1:T(8,128)S(1)} collective-permute-done((f32[128,128]{0,1:T(8,128)S(1)}, f32[128,128]{0,1:T(8,128)S(1)}, u32[]{:S(2)}, u32[]{:S(2)}) %collective-permute-start.6) | collective-permute-done | bytes 65568 | tf_op jit(solution)/shard_map/ppermute | solution.py:33
  146.1 0.8 collective-permute-done.7
  149.0 0.9 convolution_convert_fusion
  149.9 1.0 copy.28
  150.9 0.7 copy.29
  (37 shorter events, 7.5 us)
Async XLA Ops:
  7.2 92.1 %copy-start = (f32[1,8,16,16]{3,2,1,0:T(8,128)S(1)}, f32[1,8,16,16]{3,2,1,0:T(8,128)}, u32[]{:S(2)}) copy-start(f32[1,8,16,16]{3,2,1,0:T(8,128)} %param.8) | copy-start | bytes 24580
  7.2 78.3 %all-gather.3.cloned.1.call-start = ((), (), s32[]{:S(2)}) async-start(), calls=%async_computation | async-start | bytes 17301504 | tf_op jit(solution)/shard_map/all_gather | solution.py:100
  85.4 0.7 copy-start.1
  99.2 29.6 %copy-start.2 = (f32[128,128]{1,0:T(8,128)S(1)}, f32[128,128]{1,0:T(8,128)}, u32[]{:S(2)}) copy-start(f32[128,128]{1,0:T(8,128)} %param.9) | copy-start | bytes 196612
  102.6 14.4 %collective-permute-start = (f32[128,128]{0,1:T(8,128)S(1)}, f32[128,128]{0,1:T(8,128)S(1)}, u32[]{:S(2)}, u32[]{:S(2)}) collective-permute-start(f32[128,128]{0,1:T(8,128)S(1)} %convolution_bitcast_fusion), channel_id=1, source_target_pairs={{0,1},{1,0},{2,3},{3,2},{4,5},{5,4},{6,7},{7,6},{8,9},{9,8},{10,11... | collective-permute-start | bytes 196616 | tf_op jit(solution)/shard_map/ppermute | solution.py:22
  117.0 4.4 %collective-permute-start.1 = (f32[128,128]{0,1:T(8,128)S(1)}, f32[128,128]{0,1:T(8,128)S(1)}, u32[]{:S(2)}, u32[]{:S(2)}) collective-permute-start(f32[128,128]{0,1:T(8,128)S(1)} %add.61), channel_id=1, source_target_pairs={{0,2},{1,3},{2,0},{3,1},{4,6},{5,7},{6,4},{7,5},{8,10},{9,11},{10,... | collective-permute-start | bytes 196616 | tf_op jit(solution)/shard_map/ppermute | solution.py:22
  121.4 5.8 %collective-permute-start.2 = (f32[128,128]{0,1:T(8,128)S(1)}, f32[128,128]{0,1:T(8,128)S(1)}, u32[]{:S(2)}, u32[]{:S(2)}) collective-permute-start(f32[128,128]{0,1:T(8,128)S(1)} %add.62), channel_id=1, source_target_pairs={{0,4},{1,5},{2,6},{3,7},{4,0},{5,1},{6,2},{7,3},{8,12},{9,13},{10,... | collective-permute-start | bytes 196616 | tf_op jit(solution)/shard_map/ppermute | solution.py:22
  127.3 4.3 %collective-permute-start.3 = (f32[128,128]{0,1:T(8,128)S(1)}, f32[128,128]{0,1:T(8,128)S(1)}, u32[]{:S(2)}, u32[]{:S(2)}) collective-permute-start(f32[128,128]{0,1:T(8,128)S(1)} %add.63), channel_id=1, source_target_pairs={{0,8},{1,9},{2,10},{3,11},{4,12},{5,13},{6,14},{7,15},{8,0},{9,1},... | collective-permute-start | bytes 196616 | tf_op jit(solution)/shard_map/ppermute | solution.py:22
  131.7 5.8 %collective-permute-start.4 = (f32[128,128]{0,1:T(8,128)S(1)}, f32[128,128]{0,1:T(8,128)S(1)}, u32[]{:S(2)}, u32[]{:S(2)}) collective-permute-start(f32[128,128]{0,1:T(8,128)S(1)} %add.64), channel_id=1, source_target_pairs={{0,16},{1,17},{2,18},{3,19},{4,20},{5,21},{6,22},{7,23},{8,24},{9,... | collective-permute-start | bytes 196616 | tf_op jit(solution)/shard_map/ppermute | solution.py:22
  138.8 5.5 %collective-permute-start.5 = (f32[128,128]{0,1:T(8,128)S(1)}, f32[128,128]{0,1:T(8,128)S(1)}, u32[]{:S(2)}, u32[]{:S(2)}) collective-permute-start(f32[128,128]{0,1:T(8,128)S(1)} %multiply_divide_fusion), channel_id=1, source_target_pairs={{0,32},{32,64},{64,96},{96,0},{1,33},{33,65},{65,97},{97,1},{2,34}... | collective-permute-start | bytes 196616 | tf_op jit(solution)/shard_map/ppermute | solution.py:33
  140.3 5.8 %collective-permute-start.6 = (f32[128,128]{0,1:T(8,128)S(1)}, f32[128,128]{0,1:T(8,128)S(1)}, u32[]{:S(2)}, u32[]{:S(2)}) collective-permute-start(f32[128,128]{0,1:T(8,128)S(1)} %multiply_divide_fusion), channel_id=1, source_target_pairs={{0,64},{32,96},{64,0},{96,32},{1,65},{33,97},{65,1},{97,33},{2,66}... | collective-permute-start | bytes 196616 | tf_op jit(solution)/shard_map/ppermute | solution.py:33
  142.6 4.3 %collective-permute-start.7 = (f32[128,128]{0,1:T(8,128)S(1)}, f32[128,128]{0,1:T(8,128)S(1)}, u32[]{:S(2)}, u32[]{:S(2)}) collective-permute-start(f32[128,128]{0,1:T(8,128)S(1)} %multiply_divide_fusion), channel_id=1, source_target_pairs={{0,96},{32,0},{64,32},{96,64},{1,97},{33,1},{65,33},{97,65},{2,98}... | collective-permute-start | bytes 196616 | tf_op jit(solution)/shard_map/ppermute | solution.py:33
Sparse Core Ops, SparseCore 0:
  10.2 75.1 all-gather.2

commit v8 on v4

--- a/solution.py
+++ b/solution.py
@@ -36,32 +36,46 @@
     return jnp.zeros_like(stacked).at[order].set(stacked)
 
 
+ROW_PARTS = 4
+
+
 def masked_apply_kernel(span_ref, env_ref, theta_ref, sec_j_ref, sec_i_ref, out_ref):
     step = pl.program_id(0)
+    chain_w, rows_dev, depth = env_ref.shape
+    rows_part = rows_dev // ROW_PARTS
+    tile = span_ref[0] + step
 
     @pl.when(step == 0)
     def _():
         out_ref[...] = jnp.zeros_like(out_ref)
 
-    @pl.when(span_ref[0] + step <= span_ref[1])
-    def _():
-        same = sec_i_ref[...] == sec_j_ref[...]
-        block = theta_ref[...]
-        for w in range(out_ref.shape[0]):
-            env_w = jnp.where(same, env_ref[w], jnp.zeros_like(env_ref[w]))
-            out_ref[w] += jnp.dot(env_w, block, preferred_element_type=jnp.float32)
+    for r in range(ROW_PARTS):
+        rows = slice(r * rows_part, (r + 1) * rows_part)
+
+        @pl.when((span_ref[2 * r] <= tile) & (tile <= span_ref[2 * r + 1]))
+        def _():
+            same = sec_i_ref[rows, :] == sec_j_ref[...]
+            env = env_ref[:, rows, :]
+            masked = jnp.where(same[None], env, jnp.zeros_like(env))
+            masked = masked.reshape(chain_w * rows_part, depth)
+            part = jnp.dot(masked, theta_ref[...], preferred_element_type=jnp.float32)
+            out_ref[:, rows, :] += part.reshape(chain_w, rows_part, part.shape[1])
 
 
 def masked_apply(env_loc, theta_all, sec_all, my_sec):
     chain_w, rows_dev, depth = env_loc.shape
     width = theta_all.shape[1]
     tiles = depth // K_TILE
-    first = jnp.sum((sec_all < my_sec[0]).astype(jnp.int32))
-    last = jnp.sum((sec_all <= my_sec[-1]).astype(jnp.int32)) - 1
-    span = jnp.stack([first // K_TILE, last // K_TILE]).astype(jnp.int32)
+    rows_part = rows_dev // ROW_PARTS
+    bounds = []
+    for r in range(ROW_PARTS):
+        first = jnp.sum((sec_all < my_sec[r * rows_part]).astype(jnp.int32))
+        last = jnp.sum((sec_all <= my_sec[(r + 1) * rows_part - 1]).astype(jnp.int32)) - 1
+        bounds += [first // K_TILE, last // K_TILE]
+    span = jnp.stack(bounds).astype(jnp.int32)
 
     def tile_of(step, span_ref):
-        return jnp.minimum(span_ref[0] + step, span_ref[1])
+        return jnp.minimum(span_ref[0] + step, span_ref[2 * ROW_PARTS - 1])
 
     grid_spec = pltpu.PrefetchScalarGridSpec(
         num_scalar_prefetch=1,

time: 162 us -> 167 us (1.031)
  waiting for transfers between devices: 89.3 us -> 69.6 us
  starting transfers between devices: 24.2 us -> 33.5 us
  between operations: 17.9 us -> 27.2 us
  other arithmetic: 3.53 us -> 7.36 us
  Pallas kernels: 7.71 us -> 10.6 us
    all_gather x1, waiting for transfers between devices: 68.5 us -> 55.3 us  [per_device(): theta_all = lax.all_gather(theta_loc, 'blk', axis=0, tiled=True)]
    ppermute x5, starting transfers between devices: 20.9 us -> 27.8 us  [butterfly_sum(): value = value + lax.ppermute(value, axis, pairs)]
    ppermute x5, waiting for transfers between devices: 16.4 us -> 10.2 us  [butterfly_sum(): value = value + lax.ppermute(value, axis, pairs)]
    reduce_sum x1, other arithmetic: 2.76 us -> 6.67 us  [masked_apply(): jnp.sum((sec_all <= my_sec[(r + 1) * rows_part - 1]).astype(jnp.int32)) - 1]
    pallas_call x1, Pallas kernels: 7.71 us -> 10.6 us  [masked_apply(): pl.pallas_call(masked_apply_kernel, grid_spec=grid_spec, out_shape=jax.Sh...]
    ppermute x3, starting transfers between devices: 3.3 us -> 5.71 us  [gather_all(): parts.append(lax.ppermute(value, axis, pairs))]
  transfers between devices with their start and end apart: 9 -> 9, of which waited for: 8 -> 8; matrix products, arithmetic and copies ran while one was open for 4% -> 6% of each run, Pallas kernels for 0% -> 0%
where the time goes in v8:
time: 167 us; the launch traced here: 166 us
  waiting for transfers between devices  69.6 us (42%)
  starting transfers between devices  33.5 us (20%)
  between operations  27.2 us (16%)
  local copies, waits for them, and re-layouts  12.3 us (7%)
  Pallas kernels  10.6 us (6%)
  other arithmetic  7.36 us (4%)
  matrix products  5.27 us (3%)
    all_gather x1, waiting for transfers between devices, per_device(): theta_all = lax.all_gather(theta_loc, 'blk', axis=0, tiled=True)  55.3 us
    ppermute x5, starting transfers between devices, butterfly_sum(): value = value + lax.ppermute(value, axis, pairs)  27.8 us
    pallas_call x1, Pallas kernels, masked_apply(): pl.pallas_call(masked_apply_kernel, grid_spec=grid_spec, out_shape=jax.Sh...  10.6 us
    ppermute x5, waiting for transfers between devices, butterfly_sum(): value = value + lax.ppermute(value, axis, pairs)  10.2 us
    unnamed x14, local copies, waits for them, and re-layouts  9.12 us
    reduce_sum x1, other arithmetic, masked_apply(): jnp.sum((sec_all <= my_sec[(r + 1) * rows_part - 1]).astype(jnp.int32)) - 1  6.67 us
    ppermute x3, starting transfers between devices, gather_all(): parts.append(lax.ppermute(value, axis, pairs))  5.71 us
  transfers between devices with their start and end apart: 9, of which 8 were waited for; matrix products, arithmetic and copies ran while one was open for 6% of the time, Pallas kernels for 0%

profile of v8, /device:TPU:0, one launch (start us, length us, event | category | flops | bytes accessed | tf_op | source)
XLA Modules:
  0.0 165.8 jit_solution(3442773312593549079)
XLA Ops:
  9.3 6.7 %fusion.20 = (s32[]{:T(128)}, s32[]{:T(128)}, s32[]{:T(128)}, s32[]{:T(128)}, s32[]{:T(128)}, /*index=5*/s32[]{:T(128)}, s32[]{:T(128)}, s32[]{:T(128)}) fusion(s32[1,4096]{1,0:T(1,128)} %sec_j_ref.1, s32[]{:T(128)} %bitcast.14, s32[]{:T(128)} %bitcast.12, s32[]{:T(128)} %bitcast.10, s32[]{:T(128)} %bitcast.8, s32[]{:T(128)} %bitcast.6, s32[]{:T(128)} %bitcast.4, ...), kind=kLoop, calls=%fused_computation.41 | loop fusion | flops 98296 | bytes 16448 | tf_op jit(solution)/shard_map/reduce_sum | solution.py:73
  28.9 1.2 copy.36
  30.2 55.3 %all-gather.3.cloned.1.call-done = bf16[1,4096,2048]{2,1,0:T(8,128)(2,1)} async-done(((bf16[1,128,2048]{2,1,0:T(8,128)(2,1)}), bf16[1,4096,2048]{2,1,0:T(8,128)(2,1)}) %all-gather.3.cloned.1.call-update) | async-done | bytes 16777232 | tf_op jit(solution)/shard_map/all_gather | solution.py:114
  86.2 10.6 %shard_map.68 = f32[8,128,2048]{2,1,0:T(8,128)} custom-call(s32[8]{0:T(128)S(1)} %stack.68.span_ref, bf16[8,128,4096]{2,1,0:T(8,128)(2,1)} %bitcast.95, bf16[4096,2048]{1,0:T(8,128)(2,1)} %bitcast.94, s32[1,4096]{1,0:T(1,128)S(1)} %copy-done.1, s32[128,1]{1,0:T(8,128)S(1)} %copy.18.sec_i_ref), custom_call_target="tpu_custom_call" | custom-call | tf_op jit(solution)/shard_map/pallas_call | solution.py:91
  96.8 5.4 %copy.35 = f32[128,8,16,128]{3,2,1,0:T(8,128)S(1)} copy(f32[128,8,16,128]{3,1,2,0:T(8,128)} %bitcast.93) | data formatting | bytes 16777216
  102.2 2.6 %fusion.2 = f32[128,16,128]{2,1,0:T(8,128)S(1)} fusion(f32[1,8,16,16]{3,2,1,0:T(8,128)S(1)} %copy-done, f32[8,128,16,128]{3,2,1,0:T(8,128)S(1)} %bitcast.92), kind=kOutput, calls=%fused_computation.3 | convolution fusion | flops 201326592 | bytes 9445376 | tf_op jit(solution)/shard_map/wpq,wiqc->ipc/dot_general | solution.py:117
  104.9 0.7 convolution_bitcast_fusion
  105.9 1.0 collective-permute-done
  106.9 9.4 %collective-permute-start.1 = (f32[128,128]{0,1:T(8,128)S(1)}, f32[128,128]{0,1:T(8,128)S(1)}, u32[]{:S(2)}, u32[]{:S(2)}) collective-permute-start(f32[128,128]{0,1:T(8,128)S(1)} %add.70), channel_id=1, source_target_pairs={{0,2},{1,3},{2,0},{3,1},{4,6},{5,7},{6,4},{7,5},{8,10},{9,11},{10,... | collective-permute-start | bytes 196616 | tf_op jit(solution)/shard_map/ppermute | solution.py:22
  116.3 2.6 %collective-permute-done.1 = f32[128,128]{0,1:T(8,128)S(1)} collective-permute-done((f32[128,128]{0,1:T(8,128)S(1)}, f32[128,128]{0,1:T(8,128)S(1)}, u32[]{:S(2)}, u32[]{:S(2)}) %collective-permute-start.1) | collective-permute-done | bytes 65568 | tf_op jit(solution)/shard_map/ppermute | solution.py:22
  118.9 11.9 %collective-permute-start.2 = (f32[128,128]{0,1:T(8,128)S(1)}, f32[128,128]{0,1:T(8,128)S(1)}, u32[]{:S(2)}, u32[]{:S(2)}) collective-permute-start(f32[128,128]{0,1:T(8,128)S(1)} %add.71), channel_id=1, source_target_pairs={{0,4},{1,5},{2,6},{3,7},{4,0},{5,1},{6,2},{7,3},{8,12},{9,13},{10,... | collective-permute-start | bytes 196616 | tf_op jit(solution)/shard_map/ppermute | solution.py:22
  130.8 2.2 %collective-permute-done.2 = f32[128,128]{0,1:T(8,128)S(1)} collective-permute-done((f32[128,128]{0,1:T(8,128)S(1)}, f32[128,128]{0,1:T(8,128)S(1)}, u32[]{:S(2)}, u32[]{:S(2)}) %collective-permute-start.2) | collective-permute-done | bytes 65568 | tf_op jit(solution)/shard_map/ppermute | solution.py:22
  133.1 2.5 %collective-permute-start.3 = (f32[128,128]{0,1:T(8,128)S(1)}, f32[128,128]{0,1:T(8,128)S(1)}, u32[]{:S(2)}, u32[]{:S(2)}) collective-permute-start(f32[128,128]{0,1:T(8,128)S(1)} %add.72), channel_id=1, source_target_pairs={{0,8},{1,9},{2,10},{3,11},{4,12},{5,13},{6,14},{7,15},{8,0},{9,1},... | collective-permute-start | bytes 196616 | tf_op jit(solution)/shard_map/ppermute | solution.py:22
  135.7 2.1 %collective-permute-done.3 = f32[128,128]{0,1:T(8,128)S(1)} collective-permute-done((f32[128,128]{0,1:T(8,128)S(1)}, f32[128,128]{0,1:T(8,128)S(1)}, u32[]{:S(2)}, u32[]{:S(2)}) %collective-permute-start.3) | collective-permute-done | bytes 65568 | tf_op jit(solution)/shard_map/ppermute | solution.py:22
  137.9 3.6 %collective-permute-start.4 = (f32[128,128]{0,1:T(8,128)S(1)}, f32[128,128]{0,1:T(8,128)S(1)}, u32[]{:S(2)}, u32[]{:S(2)}) collective-permute-start(f32[128,128]{0,1:T(8,128)S(1)} %add.73), channel_id=1, source_target_pairs={{0,16},{1,17},{2,18},{3,19},{4,20},{5,21},{6,22},{7,23},{8,24},{9,... | collective-permute-start | bytes 196616 | tf_op jit(solution)/shard_map/ppermute | solution.py:22
  141.5 2.2 %collective-permute-done.4 = f32[128,128]{0,1:T(8,128)S(1)} collective-permute-done((f32[128,128]{0,1:T(8,128)S(1)}, f32[128,128]{0,1:T(8,128)S(1)}, u32[]{:S(2)}, u32[]{:S(2)}) %collective-permute-start.4) | collective-permute-done | bytes 65568 | tf_op jit(solution)/shard_map/ppermute | solution.py:22
  145.1 1.9 %collective-permute-start.5 = (f32[128,128]{0,1:T(8,128)S(1)}, f32[128,128]{0,1:T(8,128)S(1)}, u32[]{:S(2)}, u32[]{:S(2)}) collective-permute-start(f32[128,128]{0,1:T(8,128)S(1)} %multiply_divide_fusion), channel_id=1, source_target_pairs={{0,32},{32,64},{64,96},{96,0},{1,33},{33,65},{65,97},{97,1},{2,34}... | collective-permute-start | bytes 196616 | tf_op jit(solution)/shard_map/ppermute | solution.py:33
  147.0 2.9 %collective-permute-start.6 = (f32[128,128]{0,1:T(8,128)S(1)}, f32[128,128]{0,1:T(8,128)S(1)}, u32[]{:S(2)}, u32[]{:S(2)}) collective-permute-start(f32[128,128]{0,1:T(8,128)S(1)} %multiply_divide_fusion), channel_id=1, source_target_pairs={{0,64},{32,96},{64,0},{96,32},{1,65},{33,97},{65,1},{97,33},{2,66}... | collective-permute-start | bytes 196616 | tf_op jit(solution)/shard_map/ppermute | solution.py:33
  149.9 0.9 collective-permute-start.7
  150.8 2.0 %collective-permute-done.6 = f32[128,128]{0,1:T(8,128)S(1)} collective-permute-done((f32[128,128]{0,1:T(8,128)S(1)}, f32[128,128]{0,1:T(8,128)S(1)}, u32[]{:S(2)}, u32[]{:S(2)}) %collective-permute-start.6) | collective-permute-done | bytes 65568 | tf_op jit(solution)/shard_map/ppermute | solution.py:33
  152.8 1.3 collective-permute-done.7
  156.3 0.9 convolution_convert_fusion
  157.2 1.0 copy.28
  158.2 0.7 copy.29
  (37 shorter events, 6.8 us)
Async XLA Ops:
  7.2 95.0 %copy-start = (f32[1,8,16,16]{3,2,1,0:T(8,128)S(1)}, f32[1,8,16,16]{3,2,1,0:T(8,128)}, u32[]{:S(2)}) copy-start(f32[1,8,16,16]{3,2,1,0:T(8,128)} %param.8) | copy-start | bytes 24580
  7.2 78.3 %all-gather.3.cloned.1.call-start = ((), (), s32[]{:S(2)}) async-start(), calls=%async_computation | async-start | bytes 17301504 | tf_op jit(solution)/shard_map/all_gather | solution.py:114
  85.5 0.7 copy-start.1
  102.2 33.4 %copy-start.2 = (f32[128,128]{1,0:T(8,128)S(1)}, f32[128,128]{1,0:T(8,128)}, u32[]{:S(2)}) copy-start(f32[128,128]{1,0:T(8,128)} %param.9) | copy-start | bytes 196612
  105.6 1.3 collective-permute-start
  106.9 12.0 %collective-permute-start.1 = (f32[128,128]{0,1:T(8,128)S(1)}, f32[128,128]{0,1:T(8,128)S(1)}, u32[]{:S(2)}, u32[]{:S(2)}) collective-permute-start(f32[128,128]{0,1:T(8,128)S(1)} %add.70), channel_id=1, source_target_pairs={{0,2},{1,3},{2,0},{3,1},{4,6},{5,7},{6,4},{7,5},{8,10},{9,11},{10,... | collective-permute-start | bytes 196616 | tf_op jit(solution)/shard_map/ppermute | solution.py:22
  118.9 14.1 %collective-permute-start.2 = (f32[128,128]{0,1:T(8,128)S(1)}, f32[128,128]{0,1:T(8,128)S(1)}, u32[]{:S(2)}, u32[]{:S(2)}) collective-permute-start(f32[128,128]{0,1:T(8,128)S(1)} %add.71), channel_id=1, source_target_pairs={{0,4},{1,5},{2,6},{3,7},{4,0},{5,1},{6,2},{7,3},{8,12},{9,13},{10,... | collective-permute-start | bytes 196616 | tf_op jit(solution)/shard_map/ppermute | solution.py:22
  133.1 4.8 %collective-permute-start.3 = (f32[128,128]{0,1:T(8,128)S(1)}, f32[128,128]{0,1:T(8,128)S(1)}, u32[]{:S(2)}, u32[]{:S(2)}) collective-permute-start(f32[128,128]{0,1:T(8,128)S(1)} %add.72), channel_id=1, source_target_pairs={{0,8},{1,9},{2,10},{3,11},{4,12},{5,13},{6,14},{7,15},{8,0},{9,1},... | collective-permute-start | bytes 196616 | tf_op jit(solution)/shard_map/ppermute | solution.py:22
  137.9 5.9 %collective-permute-start.4 = (f32[128,128]{0,1:T(8,128)S(1)}, f32[128,128]{0,1:T(8,128)S(1)}, u32[]{:S(2)}, u32[]{:S(2)}) collective-permute-start(f32[128,128]{0,1:T(8,128)S(1)} %add.73), channel_id=1, source_target_pairs={{0,16},{1,17},{2,18},{3,19},{4,20},{5,21},{6,22},{7,23},{8,24},{9,... | collective-permute-start | bytes 196616 | tf_op jit(solution)/shard_map/ppermute | solution.py:22
  145.1 5.7 %collective-permute-start.5 = (f32[128,128]{0,1:T(8,128)S(1)}, f32[128,128]{0,1:T(8,128)S(1)}, u32[]{:S(2)}, u32[]{:S(2)}) collective-permute-start(f32[128,128]{0,1:T(8,128)S(1)} %multiply_divide_fusion), channel_id=1, source_target_pairs={{0,32},{32,64},{64,96},{96,0},{1,33},{33,65},{65,97},{97,1},{2,34}... | collective-permute-start | bytes 196616 | tf_op jit(solution)/shard_map/ppermute | solution.py:33
  147.0 5.9 %collective-permute-start.6 = (f32[128,128]{0,1:T(8,128)S(1)}, f32[128,128]{0,1:T(8,128)S(1)}, u32[]{:S(2)}, u32[]{:S(2)}) collective-permute-start(f32[128,128]{0,1:T(8,128)S(1)} %multiply_divide_fusion), channel_id=1, source_target_pairs={{0,64},{32,96},{64,0},{96,32},{1,65},{33,97},{65,1},{97,33},{2,66}... | collective-permute-start | bytes 196616 | tf_op jit(solution)/shard_map/ppermute | solution.py:33
  149.9 4.3 %collective-permute-start.7 = (f32[128,128]{0,1:T(8,128)S(1)}, f32[128,128]{0,1:T(8,128)S(1)}, u32[]{:S(2)}, u32[]{:S(2)}) collective-permute-start(f32[128,128]{0,1:T(8,128)S(1)} %multiply_divide_fusion), channel_id=1, source_target_pairs={{0,96},{32,0},{64,32},{96,64},{1,97},{33,1},{65,33},{97,65},{2,98}... | collective-permute-start | bytes 196616 | tf_op jit(solution)/shard_map/ppermute | solution.py:33
Sparse Core Ops, SparseCore 0:
  10.3 75.2 all-gather.2

commit v9 on v7

--- a/solution.py
+++ b/solution.py
@@ -11,7 +11,7 @@
 
 
 def matprod(first, second):
-    return jnp.dot(first, second, precision=lax.Precision.HIGHEST)
+    return jnp.dot(first, second, precision=lax.Precision.HIGH)
 
 
 def butterfly_sum(value, axis):

time: 161 us -> 160 us (level); the launches traced: 158 us -> 160 us
  no operation moved by 1% of the time
where the time goes in v9:
time: 160 us
  waiting for transfers between devices  84.8 us (53%)
  starting transfers between devices  28.4 us (18%)
  between operations  17.9 us (11%)
  local copies, waits for them, and re-layouts  12.1 us (8%)
  Pallas kernels  7.69 us (5%)
  matrix products  5.13 us (3%)
  other arithmetic  3.53 us (2%)
    all_gather x1, waiting for transfers between devices, per_device(): theta_all = lax.all_gather(theta_loc, 'blk', axis=0, tiled=True)  68.5 us
    ppermute x5, starting transfers between devices, butterfly_sum(): value = value + lax.ppermute(value, axis, pairs)  23 us
    ppermute x5, waiting for transfers between devices, butterfly_sum(): value = value + lax.ppermute(value, axis, pairs)  11.6 us
    unnamed x14, local copies, waits for them, and re-layouts  9.1 us
    pallas_call x1, Pallas kernels, masked_apply(): pl.pallas_call(masked_apply_kernel, grid_spec=grid_spec, out_shape=jax.Sh...  7.69 us
    ppermute x3, starting transfers between devices, gather_all(): parts.append(lax.ppermute(value, axis, pairs))  5.34 us
    ppermute x3, waiting for transfers between devices, gather_all(): parts.append(lax.ppermute(value, axis, pairs))  4.04 us
  transfers between devices with their start and end apart: 9, of which 9 were waited for; matrix products, arithmetic and copies ran while one was open for 4% of the time, Pallas kernels for 0%

profile of v9, /device:TPU:0, one launch (start us, length us, event | category | flops | bytes accessed | tf_op | source)
XLA Modules:
  0.0 159.5 jit_solution(6409035388357712012)
XLA Ops:
  9.2 2.8 %fusion.13 = (s32[]{:T(128)}, s32[]{:T(128)}) fusion(s32[1,4096]{1,0:T(1,128)} %sec_j_ref.1, s32[]{:T(128)} %bitcast, s32[]{:T(128)} %bitcast.2), kind=kLoop, calls=%fused_computation.28 | loop fusion | flops 24574 | bytes 16400 | tf_op jit(solution)/shard_map/reduce_sum | solution.py:59
  15.7 1.1 copy.36
  16.9 68.5 %all-gather.3.cloned.1.call-done = bf16[1,4096,2048]{2,1,0:T(8,128)(2,1)} async-done(((bf16[1,128,2048]{2,1,0:T(8,128)(2,1)}), bf16[1,4096,2048]{2,1,0:T(8,128)(2,1)}) %all-gather.3.cloned.1.call-update) | async-done | bytes 16777232 | tf_op jit(solution)/shard_map/all_gather | solution.py:100
  86.2 7.7 %shard_map.68 = f32[1024,2048]{1,0:T(8,128)} custom-call(s32[2]{0:T(128)S(1)} %pad_add_fusion.span_ref, bf16[8,128,4096]{2,1,0:T(8,128)(2,1)} %bitcast.82, bf16[4096,2048]{1,0:T(8,128)(2,1)} %bitcast.81, s32[1,4096]{1,0:T(1,128)S(1)} %copy-done.1, s32[128,1]{1,0:T(8,128)S(1)} %copy.18.sec_i_ref), custom_call_target="tpu_custom_call" | custom-call | tf_op jit(solution)/shard_map/pallas_call | solution.py:77
  93.9 5.4 %copy.35 = f32[128,8,16,128]{3,2,1,0:T(8,128)S(1)} copy(f32[128,8,16,128]{3,1,2,0:T(8,128)} %bitcast.80) | data formatting | bytes 16777216
  99.3 2.6 %fusion.2 = f32[128,16,128]{2,1,0:T(8,128)S(1)} fusion(f32[1,8,16,16]{3,2,1,0:T(8,128)S(1)} %copy-done, f32[8,128,16,128]{3,2,1,0:T(8,128)S(1)} %bitcast.79), kind=kOutput, calls=%fused_computation.3 | convolution fusion | flops 201326592 | bytes 9445376 | tf_op jit(solution)/shard_map/wpq,wiqc->ipc/dot_general | solution.py:103
  101.9 0.7 convolution_bitcast_fusion
  102.6 1.6 %collective-permute-start = (f32[128,128]{0,1:T(8,128)S(1)}, f32[128,128]{0,1:T(8,128)S(1)}, u32[]{:S(2)}, u32[]{:S(2)}) collective-permute-start(f32[128,128]{0,1:T(8,128)S(1)} %convolution_bitcast_fusion), channel_id=1, source_target_pairs={{0,1},{1,0},{2,3},{3,2},{4,5},{5,4},{6,7},{7,6},{8,9},{9,8},{10,11... | collective-permute-start | bytes 196616 | tf_op jit(solution)/shard_map/ppermute | solution.py:22
  104.3 0.9 collective-permute-done
  105.2 1.1 collective-permute-start.1
  106.3 3.3 %collective-permute-done.1 = f32[128,128]{0,1:T(8,128)S(1)} collective-permute-done((f32[128,128]{0,1:T(8,128)S(1)}, f32[128,128]{0,1:T(8,128)S(1)}, u32[]{:S(2)}, u32[]{:S(2)}) %collective-permute-start.1) | collective-permute-done | bytes 65568 | tf_op jit(solution)/shard_map/ppermute | solution.py:22
  109.6 15.3 %collective-permute-start.2 = (f32[128,128]{0,1:T(8,128)S(1)}, f32[128,128]{0,1:T(8,128)S(1)}, u32[]{:S(2)}, u32[]{:S(2)}) collective-permute-start(f32[128,128]{0,1:T(8,128)S(1)} %add.62), channel_id=1, source_target_pairs={{0,4},{1,5},{2,6},{3,7},{4,0},{5,1},{6,2},{7,3},{8,12},{9,13},{10,... | collective-permute-start | bytes 196616 | tf_op jit(solution)/shard_map/ppermute | solution.py:22
  124.9 2.2 %collective-permute-done.2 = f32[128,128]{0,1:T(8,128)S(1)} collective-permute-done((f32[128,128]{0,1:T(8,128)S(1)}, f32[128,128]{0,1:T(8,128)S(1)}, u32[]{:S(2)}, u32[]{:S(2)}) %collective-permute-start.2) | collective-permute-done | bytes 65568 | tf_op jit(solution)/shard_map/ppermute | solution.py:22
  127.1 1.7 %collective-permute-start.3 = (f32[128,128]{0,1:T(8,128)S(1)}, f32[128,128]{0,1:T(8,128)S(1)}, u32[]{:S(2)}, u32[]{:S(2)}) collective-permute-start(f32[128,128]{0,1:T(8,128)S(1)} %add.63), channel_id=1, source_target_pairs={{0,8},{1,9},{2,10},{3,11},{4,12},{5,13},{6,14},{7,15},{8,0},{9,1},... | collective-permute-start | bytes 196616 | tf_op jit(solution)/shard_map/ppermute | solution.py:22
  129.0 2.5 %collective-permute-done.3 = f32[128,128]{0,1:T(8,128)S(1)} collective-permute-done((f32[128,128]{0,1:T(8,128)S(1)}, f32[128,128]{0,1:T(8,128)S(1)}, u32[]{:S(2)}, u32[]{:S(2)}) %collective-permute-start.3) | collective-permute-done | bytes 65568 | tf_op jit(solution)/shard_map/ppermute | solution.py:22
  131.5 3.2 %collective-permute-start.4 = (f32[128,128]{0,1:T(8,128)S(1)}, f32[128,128]{0,1:T(8,128)S(1)}, u32[]{:S(2)}, u32[]{:S(2)}) collective-permute-start(f32[128,128]{0,1:T(8,128)S(1)} %add.64), channel_id=1, source_target_pairs={{0,16},{1,17},{2,18},{3,19},{4,20},{5,21},{6,22},{7,23},{8,24},{9,... | collective-permute-start | bytes 196616 | tf_op jit(solution)/shard_map/ppermute | solution.py:22
  134.7 2.6 %collective-permute-done.4 = f32[128,128]{0,1:T(8,128)S(1)} collective-permute-done((f32[128,128]{0,1:T(8,128)S(1)}, f32[128,128]{0,1:T(8,128)S(1)}, u32[]{:S(2)}, u32[]{:S(2)}) %collective-permute-start.4) | collective-permute-done | bytes 65568 | tf_op jit(solution)/shard_map/ppermute | solution.py:22
  138.7 1.2 collective-permute-start.5
  139.9 3.9 %collective-permute-start.6 = (f32[128,128]{0,1:T(8,128)S(1)}, f32[128,128]{0,1:T(8,128)S(1)}, u32[]{:S(2)}, u32[]{:S(2)}) collective-permute-start(f32[128,128]{0,1:T(8,128)S(1)} %multiply_divide_fusion), channel_id=1, source_target_pairs={{0,64},{32,96},{64,0},{96,32},{1,65},{33,97},{65,1},{97,33},{2,66}... | collective-permute-start | bytes 196616 | tf_op jit(solution)/shard_map/ppermute | solution.py:33
  144.6 2.2 %collective-permute-done.6 = f32[128,128]{0,1:T(8,128)S(1)} collective-permute-done((f32[128,128]{0,1:T(8,128)S(1)}, f32[128,128]{0,1:T(8,128)S(1)}, u32[]{:S(2)}, u32[]{:S(2)}) %collective-permute-start.6) | collective-permute-done | bytes 65568 | tf_op jit(solution)/shard_map/ppermute | solution.py:33
  146.8 1.3 collective-permute-done.7
  150.1 0.9 convolution_convert_fusion
  151.0 1.0 copy.28
  152.0 0.7 copy.29
  (37 shorter events, 7.0 us)
Async XLA Ops:
  7.2 92.1 %copy-start = (f32[1,8,16,16]{3,2,1,0:T(8,128)S(1)}, f32[1,8,16,16]{3,2,1,0:T(8,128)}, u32[]{:S(2)}) copy-start(f32[1,8,16,16]{3,2,1,0:T(8,128)} %param.8) | copy-start | bytes 24580
  7.2 78.3 %all-gather.3.cloned.1.call-start = ((), (), s32[]{:S(2)}) async-start(), calls=%async_computation | async-start | bytes 17301504 | tf_op jit(solution)/shard_map/all_gather | solution.py:100
  85.4 0.7 copy-start.1
  99.2 29.6 %copy-start.2 = (f32[128,128]{1,0:T(8,128)S(1)}, f32[128,128]{1,0:T(8,128)}, u32[]{:S(2)}) copy-start(f32[128,128]{1,0:T(8,128)} %param.9) | copy-start | bytes 196612
  102.6 2.5 %collective-permute-start = (f32[128,128]{0,1:T(8,128)S(1)}, f32[128,128]{0,1:T(8,128)S(1)}, u32[]{:S(2)}, u32[]{:S(2)}) collective-permute-start(f32[128,128]{0,1:T(8,128)S(1)} %convolution_bitcast_fusion), channel_id=1, source_target_pairs={{0,1},{1,0},{2,3},{3,2},{4,5},{5,4},{6,7},{7,6},{8,9},{9,8},{10,11... | collective-permute-start | bytes 196616 | tf_op jit(solution)/shard_map/ppermute | solution.py:22
  105.2 4.4 %collective-permute-start.1 = (f32[128,128]{0,1:T(8,128)S(1)}, f32[128,128]{0,1:T(8,128)S(1)}, u32[]{:S(2)}, u32[]{:S(2)}) collective-permute-start(f32[128,128]{0,1:T(8,128)S(1)} %add.61), channel_id=1, source_target_pairs={{0,2},{1,3},{2,0},{3,1},{4,6},{5,7},{6,4},{7,5},{8,10},{9,11},{10,... | collective-permute-start | bytes 196616 | tf_op jit(solution)/shard_map/ppermute | solution.py:22
  109.6 17.5 %collective-permute-start.2 = (f32[128,128]{0,1:T(8,128)S(1)}, f32[128,128]{0,1:T(8,128)S(1)}, u32[]{:S(2)}, u32[]{:S(2)}) collective-permute-start(f32[128,128]{0,1:T(8,128)S(1)} %add.62), channel_id=1, source_target_pairs={{0,4},{1,5},{2,6},{3,7},{4,0},{5,1},{6,2},{7,3},{8,12},{9,13},{10,... | collective-permute-start | bytes 196616 | tf_op jit(solution)/shard_map/ppermute | solution.py:22
  127.1 4.3 %collective-permute-start.3 = (f32[128,128]{0,1:T(8,128)S(1)}, f32[128,128]{0,1:T(8,128)S(1)}, u32[]{:S(2)}, u32[]{:S(2)}) collective-permute-start(f32[128,128]{0,1:T(8,128)S(1)} %add.63), channel_id=1, source_target_pairs={{0,8},{1,9},{2,10},{3,11},{4,12},{5,13},{6,14},{7,15},{8,0},{9,1},... | collective-permute-start | bytes 196616 | tf_op jit(solution)/shard_map/ppermute | solution.py:22
  131.5 5.8 %collective-permute-start.4 = (f32[128,128]{0,1:T(8,128)S(1)}, f32[128,128]{0,1:T(8,128)S(1)}, u32[]{:S(2)}, u32[]{:S(2)}) collective-permute-start(f32[128,128]{0,1:T(8,128)S(1)} %add.64), channel_id=1, source_target_pairs={{0,16},{1,17},{2,18},{3,19},{4,20},{5,21},{6,22},{7,23},{8,24},{9,... | collective-permute-start | bytes 196616 | tf_op jit(solution)/shard_map/ppermute | solution.py:22
  138.7 5.9 %collective-permute-start.5 = (f32[128,128]{0,1:T(8,128)S(1)}, f32[128,128]{0,1:T(8,128)S(1)}, u32[]{:S(2)}, u32[]{:S(2)}) collective-permute-start(f32[128,128]{0,1:T(8,128)S(1)} %multiply_divide_fusion), channel_id=1, source_target_pairs={{0,32},{32,64},{64,96},{96,0},{1,33},{33,65},{65,97},{97,1},{2,34}... | collective-permute-start | bytes 196616 | tf_op jit(solution)/shard_map/ppermute | solution.py:33
  139.9 6.9 %collective-permute-start.6 = (f32[128,128]{0,1:T(8,128)S(1)}, f32[128,128]{0,1:T(8,128)S(1)}, u32[]{:S(2)}, u32[]{:S(2)}) collective-permute-start(f32[128,128]{0,1:T(8,128)S(1)} %multiply_divide_fusion), channel_id=1, source_target_pairs={{0,64},{32,96},{64,0},{96,32},{1,65},{33,97},{65,1},{97,33},{2,66}... | collective-permute-start | bytes 196616 | tf_op jit(solution)/shard_map/ppermute | solution.py:33
  143.8 4.3 %collective-permute-start.7 = (f32[128,128]{0,1:T(8,128)S(1)}, f32[128,128]{0,1:T(8,128)S(1)}, u32[]{:S(2)}, u32[]{:S(2)}) collective-permute-start(f32[128,128]{0,1:T(8,128)S(1)} %multiply_divide_fusion), channel_id=1, source_target_pairs={{0,96},{32,0},{64,32},{96,64},{1,97},{33,1},{65,33},{97,65},{2,98}... | collective-permute-start | bytes 196616 | tf_op jit(solution)/shard_map/ppermute | solution.py:33
Sparse Core Ops, SparseCore 0:
  10.2 75.1 all-gather.2

commit v10 on v9

--- a/solution.py
+++ b/solution.py
@@ -99,11 +99,23 @@
     my_sec = lax.dynamic_slice_in_dim(sec_all, row_start, rows_dev, 0)
     theta_all = lax.all_gather(theta_loc, "blk", axis=0, tiled=True)
     applied = masked_apply(env_loc, theta_all, sec_all, my_sec)
-    applied = applied.reshape(chain_w, rows_dev, phys, cols)
-    acted = jnp.einsum("wpq,wiqc->ipc", ops_loc, applied, precision=lax.Precision.HIGH)
+    applied = applied.reshape(chain_w, rows_dev, width)
     theta_f = theta_loc.astype(jnp.float32).reshape(rows_dev, phys, cols)
-    partial_intersection = jnp.einsum(
-        "ipc,ipd->cd", theta_f, acted, precision=lax.Precision.HIGH
+    theta_ops = jnp.einsum("wpq,ipc->qwic", ops_loc, theta_f, precision=lax.Precision.HIGHEST)
+    partial_intersection = sum(
+        jnp.einsum(
+            "wic,wid->cd",
+            theta_ops[q],
+            applied[:, :, q * cols:(q + 1) * cols],
+            precision=lax.Precision.HIGH,
+        )
+        for q in range(phys)
+    )
+    acted = jnp.einsum(
+        "wpq,wiqc->ipc",
+        ops_loc,
+        applied.reshape(chain_w, rows_dev, phys, cols),
+        precision=lax.Precision.HIGH,
     )
     intersection = butterfly_sum(partial_intersection, "blk")
     transfer = (

time: 160 us -> 174 us (1.087)
  waiting for transfers between devices: 84.8 us -> 46.4 us
  local copies, waits for them, and re-layouts: 12.1 us -> 46.8 us
  matrix products: 5.13 us -> 24.7 us
  starting transfers between devices: 28.4 us -> 26.4 us
    all_gather x1, waiting for transfers between devices: 68.5 us -> 35.1 us  [per_device(): theta_all = lax.all_gather(theta_loc, 'blk', axis=0, tiled=True)]
    slice x0 -> x2, local copies, waits for them, and re-layouts: none -> 32.2 us  [the longest x1 28 us: per_device(): theta_ops[q]]
    dot_general x2 -> x18, matrix products: 3.36 us -> 22.9 us  [the longest x16 12.7 us: per_device(): jnp.einsum('wic,wid->cd', theta_ops[q], applied[:, :, q * cols:(q + 1) *...]
    ppermute x3, waiting for transfers between devices: 4.04 us -> 0.94 us  [gather_all(): parts.append(lax.ppermute(value, axis, pairs))]
    unnamed x14 -> x34, local copies, waits for them, and re-layouts: 9.1 us -> 11.7 us
    ppermute x5, starting transfers between devices: 23 us -> 21 us  [butterfly_sum(): value = value + lax.ppermute(value, axis, pairs)]
    ppermute x5, waiting for transfers between devices: 11.6 us -> 9.7 us  [butterfly_sum(): value = value + lax.ppermute(value, axis, pairs)]
  transfers between devices with their start and end apart: 9 -> 9, of which waited for: 9 -> 6; matrix products, arithmetic and copies ran while one was open for 4% -> 30% of each run, Pallas kernels for 0% -> 0%
where the time goes in v10:
time: 174 us; the launch traced here: 175 us
  local copies, waits for them, and re-layouts  46.8 us (27%)
  waiting for transfers between devices  46.4 us (27%)
  starting transfers between devices  26.4 us (15%)
  matrix products  24.7 us (14%)
  between operations  17.9 us (10%)
  Pallas kernels  9 us (5%)
  other arithmetic  3.46 us (2%)
    all_gather x1, waiting for transfers between devices, per_device(): theta_all = lax.all_gather(theta_loc, 'blk', axis=0, tiled=True)  35.1 us
    slice x1, local copies, waits for them, and re-layouts, per_device(): theta_ops[q]  28 us
    ppermute x5, starting transfers between devices, butterfly_sum(): value = value + lax.ppermute(value, axis, pairs)  21 us
    dot_general x16, matrix products, per_device(): jnp.einsum('wic,wid->cd', theta_ops[q], applied[:, :, q * cols:(q + 1) *...  12.7 us
    unnamed x34, local copies, waits for them, and re-layouts  11.7 us
    ppermute x5, waiting for transfers between devices, butterfly_sum(): value = value + lax.ppermute(value, axis, pairs)  9.7 us
    pallas_call x1, Pallas kernels, masked_apply(): pl.pallas_call(masked_apply_kernel, grid_spec=grid_spec, out_shape=jax.Sh...  9 us
    dot_general x1, matrix products, per_device(): jnp.einsum('wpq,ipc->qwic', ops_loc, theta_f, precision=lax.Precision.HIG...  5.67 us
  transfers between devices with their start and end apart: 9, of which 6 were waited for; matrix products, arithmetic and copies ran while one was open for 30% of the time, Pallas kernels for 0%

profile of v10, /device:TPU:0, one launch (start us, length us, event | category | flops | bytes accessed | tf_op | source)
XLA Modules:
  0.0 174.6 jit_solution(8179769625423020040)
XLA Ops:
  9.2 2.7 %fusion.44 = (s32[]{:T(128)}, s32[]{:T(128)}) fusion(s32[1,4096]{1,0:T(1,128)} %sec_j_ref.1, s32[]{:T(128)} %bitcast, s32[]{:T(128)} %bitcast.2), kind=kLoop, calls=%fused_computation.77 | loop fusion | flops 24574 | bytes 16400 | tf_op jit(solution)/shard_map/reduce_sum | solution.py:59
  15.4 1.1 copy.70
  16.7 5.7 %convolution_bitcast_fusion = f32[16,8,128,128]{3,0,1,2:T(8,128)} fusion(bf16[128,16,128,1]{2,1,0,3:T(8,128)(2,1)S(1)} %bitcast.183, f32[1,8,16,16]{3,2,1,0:T(8,128)S(1)} %copy-done), kind=kOutput, calls=%fused_computation.3 | convolution fusion | flops 402653184 | bytes 8921088 | tf_op jit(solution)/shard_map/wpq,ipc->qwic/dot_general | solution.py:104
  22.3 28.0 %fusion.50 = (f32[1,8,128,128]{3,0,1,2:T(1,128)S(1)}, f32[1,8,128,128]{3,0,1,2:T(1,128)}, f32[1,8,128,128]{3,0,1,2:T(1,128)}, f32[1,8,128,128]{3,0,1,2:T(1,128)}...) fusion(f32[16,8,128,128]{3,0,1,2:T(8,128)} %convolution_bitcast, ...), kind=kLoop, calls=%fused_computation.90 | loop fusion | bytes 16777216 | tf_op jit(solution)/shard_map/slice | solution.py:108
  50.3 35.1 %all-gather.3.cloned.1.call-done = bf16[1,4096,2048]{2,1,0:T(8,128)(2,1)} async-done(((bf16[1,128,2048]{2,1,0:T(8,128)(2,1)}), bf16[1,4096,2048]{2,1,0:T(8,128)(2,1)}) %all-gather.3.cloned.1.call-update) | async-done | bytes 16777232 | tf_op jit(solution)/shard_map/all_gather | solution.py:100
  85.4 9.0 %shard_map.68 = f32[1024,2048]{1,0:T(8,128)} custom-call(s32[2]{0:T(128)S(1)} %pad_add_fusion.span_ref, bf16[8,128,4096]{2,1,0:T(8,128)(2,1)} %bitcast.182, bf16[4096,2048]{1,0:T(8,128)(2,1)} %bitcast.181, s32[1,4096]{1,0:T(1,128)S(1)} %copy-done.1, s32[128,1]{1,0:T(8,128)S(1)} %copy.7.sec_i_ref), custom_call_target="tpu_custom_call" | custom-call | tf_op jit(solution)/shard_map/pallas_call | solution.py:77
  94.5 4.2 %fusion.49 = (f32[8,128,128]{2,1,0:T(8,128)S(1)}, f32[8,128,128]{2,1,0:T(8,128)S(1)}, f32[8,128,128]{2,1,0:T(8,128)S(1)}, f32[8,128,128]{2,1,0:T(8,128)S(1)}, f3...) fusion(f32[8,128,2048]{2,1,0:T(8,128)} %bitcast.178), kind=kLoop, calls=%fused_computation.89 | loop fusion | bytes 16777216 | tf_op jit(solution)/shard_map/slice | solution.py:109
  104.2 0.8 convolution_bitcast_fusion.9
  110.6 1.0 fusion.17
  112.0 1.0 collective-permute-done
  113.0 1.0 collective-permute-start.1
  114.0 3.3 %collective-permute-done.1 = f32[128,128]{1,0:T(8,128)S(1)} collective-permute-done((f32[128,128]{1,0:T(8,128)S(1)}, f32[128,128]{1,0:T(8,128)S(1)}, u32[]{:S(2)}, u32[]{:S(2)}) %collective-permute-start.1) | collective-permute-done | bytes 65568 | tf_op jit(solution)/shard_map/ppermute | solution.py:22
  117.4 2.6 %collective-permute-start.2 = (f32[128,128]{1,0:T(8,128)S(1)}, f32[128,128]{1,0:T(8,128)S(1)}, u32[]{:S(2)}, u32[]{:S(2)}) collective-permute-start(f32[128,128]{1,0:T(8,128)S(1)} %add.122), channel_id=1, source_target_pairs={{0,4},{1,5},{2,6},{3,7},{4,0},{5,1},{6,2},{7,3},{8,12},{9,13},{10,... | collective-permute-start | bytes 196616 | tf_op jit(solution)/shard_map/ppermute | solution.py:22
  120.1 3.1 %collective-permute-done.2 = f32[128,128]{1,0:T(8,128)S(1)} collective-permute-done((f32[128,128]{1,0:T(8,128)S(1)}, f32[128,128]{1,0:T(8,128)S(1)}, u32[]{:S(2)}, u32[]{:S(2)}) %collective-permute-start.2) | collective-permute-done | bytes 65568 | tf_op jit(solution)/shard_map/ppermute | solution.py:22
  123.2 14.7 %collective-permute-start.3 = (f32[128,128]{1,0:T(8,128)S(1)}, f32[128,128]{1,0:T(8,128)S(1)}, u32[]{:S(2)}, u32[]{:S(2)}) collective-permute-start(f32[128,128]{1,0:T(8,128)S(1)} %add.123), channel_id=1, source_target_pairs={{0,8},{1,9},{2,10},{3,11},{4,12},{5,13},{6,14},{7,15},{8,0},{9,1},... | collective-permute-start | bytes 196616 | tf_op jit(solution)/shard_map/ppermute | solution.py:22
  137.9 2.2 %collective-permute-done.3 = f32[128,128]{1,0:T(8,128)S(1)} collective-permute-done((f32[128,128]{1,0:T(8,128)S(1)}, f32[128,128]{1,0:T(8,128)S(1)}, u32[]{:S(2)}, u32[]{:S(2)}) %collective-permute-start.3) | collective-permute-done | bytes 65568 | tf_op jit(solution)/shard_map/ppermute | solution.py:22
  140.2 2.3 %collective-permute-start.4 = (f32[128,128]{1,0:T(8,128)S(1)}, f32[128,128]{1,0:T(8,128)S(1)}, u32[]{:S(2)}, u32[]{:S(2)}) collective-permute-start(f32[128,128]{1,0:T(8,128)S(1)} %add.124), channel_id=1, source_target_pairs={{0,16},{1,17},{2,18},{3,19},{4,20},{5,21},{6,22},{7,23},{8,24},{9,... | collective-permute-start | bytes 196616 | tf_op jit(solution)/shard_map/ppermute | solution.py:22
  142.5 8.6 %copy.69 = f32[128,8,16,128]{3,2,1,0:T(8,128)} copy(f32[128,8,16,128]{3,1,2,0:T(8,128)} %bitcast.179) | data formatting | bytes 16777216
  152.4 2.8 %collective-permute-start.7 = (f32[128,128]{1,0:T(8,128)S(1)}, f32[128,128]{1,0:T(8,128)S(1)}, u32[]{:S(2)}, u32[]{:S(2)}) collective-permute-start(f32[128,128]{1,0:T(8,128)S(1)} %multiply_divide_fusion), channel_id=1, source_target_pairs={{0,96},{32,0},{64,32},{96,64},{1,97},{33,1},{65,33},{97,65},{2,98}... | collective-permute-start | bytes 196616 | tf_op jit(solution)/shard_map/ppermute | solution.py:33
  155.2 2.6 %collective-permute-start.6 = (f32[128,128]{1,0:T(8,128)S(1)}, f32[128,128]{1,0:T(8,128)S(1)}, u32[]{:S(2)}, u32[]{:S(2)}) collective-permute-start(f32[128,128]{1,0:T(8,128)S(1)} %multiply_divide_fusion), channel_id=1, source_target_pairs={{0,64},{32,96},{64,0},{96,32},{1,65},{33,97},{65,1},{97,33},{2,66}... | collective-permute-start | bytes 196616 | tf_op jit(solution)/shard_map/ppermute | solution.py:33
  157.8 4.5 %fusion = f32[128,128,16,1]{1,2,0,3:T(8,128)S(1)} fusion(f32[1,8,16,16]{3,2,1,0:T(8,128)S(1)} %copy-done, f32[8,128,16,128]{3,2,1,0:T(8,128)} %bitcast.180), kind=kOutput, calls=%fused_computation.1 | convolution fusion | flops 201326592 | bytes 9445376 | tf_op jit(solution)/shard_map/wpq,wiqc->ipc/dot_general | solution.py:114
  162.4 0.9 collective-permute-done.5
  165.2 0.9 convolution_convert_fusion
  166.0 1.0 copy.29
  (74 shorter events, 17.5 us)
Async XLA Ops:
  7.2 9.5 %copy-start = (f32[1,8,16,16]{3,2,1,0:T(8,128)S(1)}, f32[1,8,16,16]{3,2,1,0:T(8,128)}, u32[]{:S(2)}) copy-start(f32[1,8,16,16]{3,2,1,0:T(8,128)} %param.8) | copy-start | bytes 24580
  7.2 78.3 %all-gather.3.cloned.1.call-start = ((), (), s32[]{:S(2)}) async-start(), calls=%async_computation | async-start | bytes 17301504 | tf_op jit(solution)/shard_map/all_gather | solution.py:100
  22.3 63.1 %copy-start.1 = (s32[1,4096]{1,0:T(1,128)S(1)}, s32[1,4096]{1,0:T(1,128)}, u32[]{:S(2)}) copy-start(s32[1,4096]{1,0:T(1,128)} %sec_j_ref.1) | copy-start | bytes 49156
  94.5 4.2 %copy-start.11 = (f32[1,8,128,128]{3,0,1,2:T(1,128)S(1)}, f32[1,8,128,128]{3,0,1,2:T(1,128)}, u32[]{:S(2)}) copy-start(f32[1,8,128,128]{3,0,1,2:T(1,128)} %get-tuple-element.23) | copy-start | bytes 1572868
  94.5 5.0 %copy-start.10 = (f32[1,8,128,128]{3,0,1,2:T(1,128)S(1)}, f32[1,8,128,128]{3,0,1,2:T(1,128)}, u32[]{:S(2)}) copy-start(f32[1,8,128,128]{3,0,1,2:T(1,128)} %get-tuple-element.24) | copy-start | bytes 1572868
  94.5 5.8 %copy-start.9 = (f32[1,8,128,128]{3,0,1,2:T(1,128)S(1)}, f32[1,8,128,128]{3,0,1,2:T(1,128)}, u32[]{:S(2)}) copy-start(f32[1,8,128,128]{3,0,1,2:T(1,128)} %get-tuple-element.25) | copy-start | bytes 1572868
  98.7 2.3 %copy-start.8 = (f32[1,8,128,128]{3,0,1,2:T(1,128)S(1)}, f32[1,8,128,128]{3,0,1,2:T(1,128)}, u32[]{:S(2)}) copy-start(f32[1,8,128,128]{3,0,1,2:T(1,128)} %get-tuple-element.26) | copy-start | bytes 1572868
  98.7 3.1 %copy-start.7 = (f32[1,8,128,128]{3,0,1,2:T(1,128)S(1)}, f32[1,8,128,128]{3,0,1,2:T(1,128)}, u32[]{:S(2)}) copy-start(f32[1,8,128,128]{3,0,1,2:T(1,128)} %get-tuple-element.27) | copy-start | bytes 1572868
  99.4 3.2 %copy-start.6 = (f32[1,8,128,128]{3,0,1,2:T(1,128)S(1)}, f32[1,8,128,128]{3,0,1,2:T(1,128)}, u32[]{:S(2)}) copy-start(f32[1,8,128,128]{3,0,1,2:T(1,128)} %get-tuple-element.28) | copy-start | bytes 1572868
  100.2 3.2 %copy-start.5 = (f32[1,8,128,128]{3,0,1,2:T(1,128)S(1)}, f32[1,8,128,128]{3,0,1,2:T(1,128)}, u32[]{:S(2)}) copy-start(f32[1,8,128,128]{3,0,1,2:T(1,128)} %get-tuple-element.29) | copy-start | bytes 1572868
  101.0 3.2 %copy-start.4 = (f32[1,8,128,128]{3,0,1,2:T(1,128)S(1)}, f32[1,8,128,128]{3,0,1,2:T(1,128)}, u32[]{:S(2)}) copy-start(f32[1,8,128,128]{3,0,1,2:T(1,128)} %get-tuple-element.30) | copy-start | bytes 1572868
  101.8 3.2 %copy-start.3 = (f32[1,8,128,128]{3,0,1,2:T(1,128)S(1)}, f32[1,8,128,128]{3,0,1,2:T(1,128)}, u32[]{:S(2)}) copy-start(f32[1,8,128,128]{3,0,1,2:T(1,128)} %get-tuple-element.31) | copy-start | bytes 1572868
  102.6 3.2 %copy-start.2 = (f32[1,8,128,128]{3,0,1,2:T(1,128)S(1)}, f32[1,8,128,128]{3,0,1,2:T(1,128)}, u32[]{:S(2)}) copy-start(f32[1,8,128,128]{3,0,1,2:T(1,128)} %get-tuple-element.32) | copy-start | bytes 1572868
  108.2 11.8 %copy-start.12 = (f32[128,128]{1,0:T(8,128)S(1)}, f32[128,128]{1,0:T(8,128)}, u32[]{:S(2)}) copy-start(f32[128,128]{1,0:T(8,128)} %param.9) | copy-start | bytes 196612
  111.7 1.3 collective-permute-start
  113.0 4.3 %collective-permute-start.1 = (f32[128,128]{1,0:T(8,128)S(1)}, f32[128,128]{1,0:T(8,128)S(1)}, u32[]{:S(2)}, u32[]{:S(2)}) collective-permute-start(f32[128,128]{1,0:T(8,128)S(1)} %add.121), channel_id=1, source_target_pairs={{0,2},{1,3},{2,0},{3,1},{4,6},{5,7},{6,4},{7,5},{8,10},{9,11},{10,... | collective-permute-start | bytes 196616 | tf_op jit(solution)/shard_map/ppermute | solution.py:22
  117.4 5.8 %collective-permute-start.2 = (f32[128,128]{1,0:T(8,128)S(1)}, f32[128,128]{1,0:T(8,128)S(1)}, u32[]{:S(2)}, u32[]{:S(2)}) collective-permute-start(f32[128,128]{1,0:T(8,128)S(1)} %add.122), channel_id=1, source_target_pairs={{0,4},{1,5},{2,6},{3,7},{4,0},{5,1},{6,2},{7,3},{8,12},{9,13},{10,... | collective-permute-start | bytes 196616 | tf_op jit(solution)/shard_map/ppermute | solution.py:22
  123.2 16.9 %collective-permute-start.3 = (f32[128,128]{1,0:T(8,128)S(1)}, f32[128,128]{1,0:T(8,128)S(1)}, u32[]{:S(2)}, u32[]{:S(2)}) collective-permute-start(f32[128,128]{1,0:T(8,128)S(1)} %add.123), channel_id=1, source_target_pairs={{0,8},{1,9},{2,10},{3,11},{4,12},{5,13},{6,14},{7,15},{8,0},{9,1},... | collective-permute-start | bytes 196616 | tf_op jit(solution)/shard_map/ppermute | solution.py:22
  140.2 10.9 %collective-permute-start.4 = (f32[128,128]{1,0:T(8,128)S(1)}, f32[128,128]{1,0:T(8,128)S(1)}, u32[]{:S(2)}, u32[]{:S(2)}) collective-permute-start(f32[128,128]{1,0:T(8,128)S(1)} %add.124), channel_id=1, source_target_pairs={{0,16},{1,17},{2,18},{3,19},{4,20},{5,21},{6,22},{7,23},{8,24},{9,... | collective-permute-start | bytes 196616 | tf_op jit(solution)/shard_map/ppermute | solution.py:22
  152.4 9.9 %collective-permute-start.7 = (f32[128,128]{1,0:T(8,128)S(1)}, f32[128,128]{1,0:T(8,128)S(1)}, u32[]{:S(2)}, u32[]{:S(2)}) collective-permute-start(f32[128,128]{1,0:T(8,128)S(1)} %multiply_divide_fusion), channel_id=1, source_target_pairs={{0,96},{32,0},{64,32},{96,64},{1,97},{33,1},{65,33},{97,65},{2,98}... | collective-permute-start | bytes 196616 | tf_op jit(solution)/shard_map/ppermute | solution.py:33
  155.2 7.1 %collective-permute-start.6 = (f32[128,128]{1,0:T(8,128)S(1)}, f32[128,128]{1,0:T(8,128)S(1)}, u32[]{:S(2)}, u32[]{:S(2)}) collective-permute-start(f32[128,128]{1,0:T(8,128)S(1)} %multiply_divide_fusion), channel_id=1, source_target_pairs={{0,64},{32,96},{64,0},{96,32},{1,65},{33,97},{65,1},{97,33},{2,66}... | collective-permute-start | bytes 196616 | tf_op jit(solution)/shard_map/ppermute | solution.py:33
  157.8 5.5 %collective-permute-start.5 = (f32[128,128]{1,0:T(8,128)S(1)}, f32[128,128]{1,0:T(8,128)S(1)}, u32[]{:S(2)}, u32[]{:S(2)}) collective-permute-start(f32[128,128]{1,0:T(8,128)S(1)} %multiply_divide_fusion), channel_id=1, source_target_pairs={{0,32},{32,64},{64,96},{96,0},{1,33},{33,65},{65,97},{97,1},{2,34}... | collective-permute-start | bytes 196616 | tf_op jit(solution)/shard_map/ppermute | solution.py:33
Sparse Core Ops, SparseCore 0:
  10.2 75.1 all-gather.2

commit v11 on v9

--- a/solution.py
+++ b/solution.py
@@ -45,10 +45,10 @@
 
     @pl.when(span_ref[0] + step <= span_ref[1])
     def _():
+        env = env_ref[...]
+        env = env.reshape(env.shape[0] * env.shape[1], env.shape[2])
         same = sec_i_ref[...] == sec_j_ref[...]
-        env = env_ref[...]
-        masked = jnp.where(same[None], env, jnp.zeros_like(env))
-        masked = masked.reshape(out_ref.shape[0], env.shape[2])
+        masked = jnp.where(same, env, jnp.zeros_like(env))
         out_ref[...] += jnp.dot(masked, theta_ref[...], preferred_element_type=jnp.float32)
 
 
@@ -59,6 +59,9 @@
     first = jnp.sum((sec_all < my_sec[0]).astype(jnp.int32))
     last = jnp.sum((sec_all <= my_sec[-1]).astype(jnp.int32)) - 1
     span = jnp.stack([first // K_TILE, last // K_TILE]).astype(jnp.int32)
+    group = 16
+    env_rows = jnp.transpose(env_loc, (1, 0, 2)).reshape(chain_w * rows_dev // group, group, depth)
+    sec_rows = jnp.repeat(my_sec, chain_w).reshape(chain_w * rows_dev, 1)
 
     def tile_of(step, span_ref):
         return jnp.minimum(span_ref[0] + step, span_ref[1])
@@ -67,10 +70,10 @@
         num_scalar_prefetch=1,
         grid=(tiles,),
         in_specs=[
-            pl.BlockSpec((chain_w, rows_dev, K_TILE), lambda k, s: (0, 0, tile_of(k, s))),
+            pl.BlockSpec((chain_w * rows_dev // group, group, K_TILE), lambda k, s: (0, 0, tile_of(k, s))),
             pl.BlockSpec((K_TILE, width), lambda k, s: (tile_of(k, s), 0)),
             pl.BlockSpec((1, K_TILE), lambda k, s: (0, tile_of(k, s))),
-            pl.BlockSpec((rows_dev, 1), lambda k, s: (0, 0)),
+            pl.BlockSpec((chain_w * rows_dev, 1), lambda k, s: (0, 0)),
         ],
         out_specs=pl.BlockSpec((chain_w * rows_dev, width), lambda k, s: (0, 0)),
     )
@@ -81,7 +84,7 @@
         compiler_params=pltpu.CompilerParams(
             dimension_semantics=("arbitrary",), vmem_limit_bytes=48 * 1024 * 1024
         ),
-    )(span, env_loc, theta_all, sec_all.reshape(1, depth), my_sec.reshape(rows_dev, 1))
+    )(span, env_rows, theta_all, sec_all.reshape(1, depth), sec_rows)
 
 
 def per_device(theta, left_env, sector_ids, local_ops, edge_env):
@@ -99,8 +102,8 @@
     my_sec = lax.dynamic_slice_in_dim(sec_all, row_start, rows_dev, 0)
     theta_all = lax.all_gather(theta_loc, "blk", axis=0, tiled=True)
     applied = masked_apply(env_loc, theta_all, sec_all, my_sec)
-    applied = applied.reshape(chain_w, rows_dev, phys, cols)
-    acted = jnp.einsum("wpq,wiqc->ipc", ops_loc, applied, precision=lax.Precision.HIGH)
+    applied = applied.reshape(rows_dev, chain_w, phys, cols)
+    acted = jnp.einsum("wpq,iwqc->ipc", ops_loc, applied, precision=lax.Precision.HIGH)
     theta_f = theta_loc.astype(jnp.float32).reshape(rows_dev, phys, cols)
     partial_intersection = jnp.einsum(
         "ipc,ipd->cd", theta_f, acted, precision=lax.Precision.HIGH

time: 160 us -> 156 us (0.975)
  waiting for transfers between devices: 84.8 us -> 72.3 us
  local copies, waits for them, and re-layouts: 12.1 us -> 16.5 us
  matrix products: 5.13 us -> 7.12 us
    transpose x0 -> x1, local copies, waits for them, and re-layouts: none -> 11.3 us  [masked_apply(): jnp.transpose(env_loc, (1, 0, 2))]
    all_gather x1, waiting for transfers between devices: 68.5 us -> 57.6 us  [per_device(): theta_all = lax.all_gather(theta_loc, 'blk', axis=0, tiled=True)]
    unnamed x14 -> x15, local copies, waits for them, and re-layouts: 9.1 us -> 1.98 us
    dot_general x1, matrix products: 2.63 us -> 4.59 us  [per_device(): jnp.einsum('wpq,iwqc->ipc', ops_loc, applied, precision=lax.Precision.HIGH)]
    ppermute x3, waiting for transfers between devices: 4.04 us -> 2.37 us  [gather_all(): parts.append(lax.ppermute(value, axis, pairs))]
  transfers between devices with their start and end apart: 9 -> 9, of which waited for: 9 -> 8; matrix products, arithmetic and copies ran while one was open for 4% -> 11% of each run, Pallas kernels for 0% -> 0%
where the time goes in v11:
time: 156 us; the launch traced here: 154 us
  waiting for transfers between devices  72.3 us (46%)
  starting transfers between devices  28.8 us (18%)
  between operations  18.3 us (12%)
  local copies, waits for them, and re-layouts  16.5 us (11%)
  Pallas kernels  7.7 us (5%)
  matrix products  7.12 us (5%)
  other arithmetic  3.53 us (2%)
    all_gather x1, waiting for transfers between devices, per_device(): theta_all = lax.all_gather(theta_loc, 'blk', axis=0, tiled=True)  57.6 us
    ppermute x5, starting transfers between devices, butterfly_sum(): value = value + lax.ppermute(value, axis, pairs)  23.9 us
    ppermute x5, waiting for transfers between devices, butterfly_sum(): value = value + lax.ppermute(value, axis, pairs)  11.6 us
    transpose x1, local copies, waits for them, and re-layouts, masked_apply(): jnp.transpose(env_loc, (1, 0, 2))  11.3 us
    pallas_call x1, Pallas kernels, masked_apply(): pl.pallas_call(masked_apply_kernel, grid_spec=grid_spec, out_shape=jax.Sh...  7.7 us
    ppermute x3, starting transfers between devices, gather_all(): parts.append(lax.ppermute(value, axis, pairs))  4.87 us
    dot_general x1, matrix products, per_device(): jnp.einsum('wpq,iwqc->ipc', ops_loc, applied, precision=lax.Precision.HIGH)  4.59 us
  transfers between devices with their start and end apart: 9, of which 8 were waited for; matrix products, arithmetic and copies ran while one was open for 11% of the time, Pallas kernels for 0%

profile of v11, /device:TPU:0, one launch (start us, length us, event | category | flops | bytes accessed | tf_op | source)
XLA Modules:
  0.0 154.2 jit_solution(4196247188053901356)
XLA Ops:
  7.2 0.7 all-gather.3.cloned.1.call-update
  9.1 2.8 %fusion.12 = (s32[]{:T(128)}, s32[]{:T(128)}) fusion(s32[1,4096]{1,0:T(1,128)} %sec_j_ref.1, s32[]{:T(128)} %bitcast, s32[]{:T(128)} %bitcast.2), kind=kLoop, calls=%fused_computation.27 | loop fusion | flops 24574 | bytes 16400 | tf_op jit(solution)/shard_map/reduce_sum | solution.py:59
  16.2 11.3 %copy.18 = bf16[128,8,4096]{2,1,0:T(8,128)(2,1)} copy(bf16[128,8,4096]{2,0,1:T(8,128)(2,1)} %bitcast.78) | data formatting | bytes 16777216 | tf_op jit(solution)/shard_map/transpose | solution.py:63
  27.8 57.6 %all-gather.3.cloned.1.call-done = bf16[1,4096,2048]{2,1,0:T(8,128)(2,1)} async-done(((bf16[1,128,2048]{2,1,0:T(8,128)(2,1)}), bf16[1,4096,2048]{2,1,0:T(8,128)(2,1)}) %all-gather.3.cloned.1.call-update) | async-done | bytes 16777232 | tf_op jit(solution)/shard_map/all_gather | solution.py:103
  85.4 7.7 %shard_map.68 = f32[1024,2048]{1,0:T(8,128)} custom-call(s32[2]{0:T(128)S(1)} %pad_add_fusion.span_ref, bf16[64,16,4096]{2,1,0:T(8,128)(2,1)} %bitcast.76, bf16[4096,2048]{1,0:T(8,128)(2,1)} %bitcast.77, s32[1,4096]{1,0:T(1,128)S(1)} %copy-done, s32[1024,1]{1,0:T(8,128)S(1)} %reshape_reshape.4.sec_i_ref), custom_call_target="tpu_custom_call" | custom-call | tf_op jit(solution)/shard_map/pallas_call | solution.py:80
  93.1 4.6 %fusion.2 = f32[128,16,128]{2,1,0:T(8,128)S(1)} fusion(f32[8,16,16,1]{1,0,2,3:T(8,128)S(1)} %copy.32, f32[1024,2048]{1,0:T(8,128)} %shard_map.68), kind=kOutput, calls=%fused_computation.3 | convolution fusion | flops 201326592 | bytes 9445376 | tf_op jit(solution)/shard_map/wpq,iwqc->ipc/dot_general | solution.py:106
  97.7 0.7 convolution_bitcast_fusion
  98.5 1.6 %collective-permute-start = (f32[128,128]{0,1:T(8,128)S(1)}, f32[128,128]{0,1:T(8,128)S(1)}, u32[]{:S(2)}, u32[]{:S(2)}) collective-permute-start(f32[128,128]{0,1:T(8,128)S(1)} %convolution_bitcast_fusion), channel_id=1, source_target_pairs={{0,1},{1,0},{2,3},{3,2},{4,5},{5,4},{6,7},{7,6},{8,9},{9,8},{10,11... | collective-permute-start | bytes 196616 | tf_op jit(solution)/shard_map/ppermute | solution.py:22
  100.1 0.9 collective-permute-done
  101.0 2.4 %collective-permute-start.1 = (f32[128,128]{0,1:T(8,128)S(1)}, f32[128,128]{0,1:T(8,128)S(1)}, u32[]{:S(2)}, u32[]{:S(2)}) collective-permute-start(f32[128,128]{0,1:T(8,128)S(1)} %add.61), channel_id=1, source_target_pairs={{0,2},{1,3},{2,0},{3,1},{4,6},{5,7},{6,4},{7,5},{8,10},{9,11},{10,... | collective-permute-start | bytes 196616 | tf_op jit(solution)/shard_map/ppermute | solution.py:22
  103.4 2.6 %collective-permute-done.1 = f32[128,128]{0,1:T(8,128)S(1)} collective-permute-done((f32[128,128]{0,1:T(8,128)S(1)}, f32[128,128]{0,1:T(8,128)S(1)}, u32[]{:S(2)}, u32[]{:S(2)}) %collective-permute-start.1) | collective-permute-done | bytes 65568 | tf_op jit(solution)/shard_map/ppermute | solution.py:22
  106.0 3.4 %collective-permute-start.2 = (f32[128,128]{0,1:T(8,128)S(1)}, f32[128,128]{0,1:T(8,128)S(1)}, u32[]{:S(2)}, u32[]{:S(2)}) collective-permute-start(f32[128,128]{0,1:T(8,128)S(1)} %add.62), channel_id=1, source_target_pairs={{0,4},{1,5},{2,6},{3,7},{4,0},{5,1},{6,2},{7,3},{8,12},{9,13},{10,... | collective-permute-start | bytes 196616 | tf_op jit(solution)/shard_map/ppermute | solution.py:22
  109.4 2.4 %collective-permute-done.2 = f32[128,128]{0,1:T(8,128)S(1)} collective-permute-done((f32[128,128]{0,1:T(8,128)S(1)}, f32[128,128]{0,1:T(8,128)S(1)}, u32[]{:S(2)}, u32[]{:S(2)}) %collective-permute-start.2) | collective-permute-done | bytes 65568 | tf_op jit(solution)/shard_map/ppermute | solution.py:22
  111.9 14.2 %collective-permute-start.3 = (f32[128,128]{0,1:T(8,128)S(1)}, f32[128,128]{0,1:T(8,128)S(1)}, u32[]{:S(2)}, u32[]{:S(2)}) collective-permute-start(f32[128,128]{0,1:T(8,128)S(1)} %add.63), channel_id=1, source_target_pairs={{0,8},{1,9},{2,10},{3,11},{4,12},{5,13},{6,14},{7,15},{8,0},{9,1},... | collective-permute-start | bytes 196616 | tf_op jit(solution)/shard_map/ppermute | solution.py:22
  126.1 2.1 %collective-permute-done.3 = f32[128,128]{0,1:T(8,128)S(1)} collective-permute-done((f32[128,128]{0,1:T(8,128)S(1)}, f32[128,128]{0,1:T(8,128)S(1)}, u32[]{:S(2)}, u32[]{:S(2)}) %collective-permute-start.3) | collective-permute-done | bytes 65568 | tf_op jit(solution)/shard_map/ppermute | solution.py:22
  128.3 2.3 %collective-permute-start.4 = (f32[128,128]{0,1:T(8,128)S(1)}, f32[128,128]{0,1:T(8,128)S(1)}, u32[]{:S(2)}, u32[]{:S(2)}) collective-permute-start(f32[128,128]{0,1:T(8,128)S(1)} %add.64), channel_id=1, source_target_pairs={{0,16},{1,17},{2,18},{3,19},{4,20},{5,21},{6,22},{7,23},{8,24},{9,... | collective-permute-start | bytes 196616 | tf_op jit(solution)/shard_map/ppermute | solution.py:22
  130.6 3.5 %collective-permute-done.4 = f32[128,128]{0,1:T(8,128)S(1)} collective-permute-done((f32[128,128]{0,1:T(8,128)S(1)}, f32[128,128]{0,1:T(8,128)S(1)}, u32[]{:S(2)}, u32[]{:S(2)}) %collective-permute-start.4) | collective-permute-done | bytes 65568 | tf_op jit(solution)/shard_map/ppermute | solution.py:22
  135.7 2.7 %collective-permute-start.6 = (f32[128,128]{0,1:T(8,128)S(1)}, f32[128,128]{0,1:T(8,128)S(1)}, u32[]{:S(2)}, u32[]{:S(2)}) collective-permute-start(f32[128,128]{0,1:T(8,128)S(1)} %multiply_divide_fusion), channel_id=1, source_target_pairs={{0,64},{32,96},{64,0},{96,32},{1,65},{33,97},{65,1},{97,33},{2,66}... | collective-permute-start | bytes 196616 | tf_op jit(solution)/shard_map/ppermute | solution.py:33
  138.5 1.9 %collective-permute-start.7 = (f32[128,128]{0,1:T(8,128)S(1)}, f32[128,128]{0,1:T(8,128)S(1)}, u32[]{:S(2)}, u32[]{:S(2)}) collective-permute-start(f32[128,128]{0,1:T(8,128)S(1)} %multiply_divide_fusion), channel_id=1, source_target_pairs={{0,96},{32,0},{64,32},{96,64},{1,97},{33,1},{65,33},{97,65},{2,98}... | collective-permute-start | bytes 196616 | tf_op jit(solution)/shard_map/ppermute | solution.py:33
  140.4 1.4 collective-permute-done.5
  141.7 1.0 collective-permute-done.7
  144.7 0.9 convolution_convert_fusion
  145.6 1.0 copy.29
  146.6 0.7 copy.30
  (41 shorter events, 5.5 us)
Async XLA Ops:
  7.2 78.3 %all-gather.3.cloned.1.call-start = ((), (), s32[]{:S(2)}) async-start(), calls=%async_computation | async-start | bytes 17301504 | tf_op jit(solution)/shard_map/all_gather | solution.py:103
  16.2 11.3 %copy-start.3 = (f32[1,8,16,16]{3,2,1,0:T(8,128)S(1)}, f32[1,8,16,16]{3,2,1,0:T(8,128)}, u32[]{:S(2)}) copy-start(f32[1,8,16,16]{3,2,1,0:T(8,128)} %param.8) | copy-start | bytes 24580
  16.2 11.4 %copy-start.1 = (bf16[1,128,2048]{2,1,0:T(8,128)(2,1)S(1)}, bf16[1,128,2048]{2,1,0:T(8,128)(2,1)}, u32[]{:S(2)}) copy-start(bf16[1,128,2048]{2,1,0:T(8,128)(2,1)} %param.5) | copy-start | bytes 1572868
  16.2 69.2 %copy-start = (s32[1,4096]{1,0:T(1,128)S(1)}, s32[1,4096]{1,0:T(1,128)}, u32[]{:S(2)}) copy-start(s32[1,4096]{1,0:T(1,128)} %sec_j_ref.1) | copy-start | bytes 49156
  93.1 32.9 %copy-start.2 = (f32[128,128]{1,0:T(8,128)S(1)}, f32[128,128]{1,0:T(8,128)}, u32[]{:S(2)}) copy-start(f32[128,128]{1,0:T(8,128)} %param.9) | copy-start | bytes 196612
  98.5 2.5 %collective-permute-start = (f32[128,128]{0,1:T(8,128)S(1)}, f32[128,128]{0,1:T(8,128)S(1)}, u32[]{:S(2)}, u32[]{:S(2)}) collective-permute-start(f32[128,128]{0,1:T(8,128)S(1)} %convolution_bitcast_fusion), channel_id=1, source_target_pairs={{0,1},{1,0},{2,3},{3,2},{4,5},{5,4},{6,7},{7,6},{8,9},{9,8},{10,11... | collective-permute-start | bytes 196616 | tf_op jit(solution)/shard_map/ppermute | solution.py:22
  101.0 5.0 %collective-permute-start.1 = (f32[128,128]{0,1:T(8,128)S(1)}, f32[128,128]{0,1:T(8,128)S(1)}, u32[]{:S(2)}, u32[]{:S(2)}) collective-permute-start(f32[128,128]{0,1:T(8,128)S(1)} %add.61), channel_id=1, source_target_pairs={{0,2},{1,3},{2,0},{3,1},{4,6},{5,7},{6,4},{7,5},{8,10},{9,11},{10,... | collective-permute-start | bytes 196616 | tf_op jit(solution)/shard_map/ppermute | solution.py:22
  106.0 5.8 %collective-permute-start.2 = (f32[128,128]{0,1:T(8,128)S(1)}, f32[128,128]{0,1:T(8,128)S(1)}, u32[]{:S(2)}, u32[]{:S(2)}) collective-permute-start(f32[128,128]{0,1:T(8,128)S(1)} %add.62), channel_id=1, source_target_pairs={{0,4},{1,5},{2,6},{3,7},{4,0},{5,1},{6,2},{7,3},{8,12},{9,13},{10,... | collective-permute-start | bytes 196616 | tf_op jit(solution)/shard_map/ppermute | solution.py:22
  111.9 16.4 %collective-permute-start.3 = (f32[128,128]{0,1:T(8,128)S(1)}, f32[128,128]{0,1:T(8,128)S(1)}, u32[]{:S(2)}, u32[]{:S(2)}) collective-permute-start(f32[128,128]{0,1:T(8,128)S(1)} %add.63), channel_id=1, source_target_pairs={{0,8},{1,9},{2,10},{3,11},{4,12},{5,13},{6,14},{7,15},{8,0},{9,1},... | collective-permute-start | bytes 196616 | tf_op jit(solution)/shard_map/ppermute | solution.py:22
  128.3 5.8 %collective-permute-start.4 = (f32[128,128]{0,1:T(8,128)S(1)}, f32[128,128]{0,1:T(8,128)S(1)}, u32[]{:S(2)}, u32[]{:S(2)}) collective-permute-start(f32[128,128]{0,1:T(8,128)S(1)} %add.64), channel_id=1, source_target_pairs={{0,16},{1,17},{2,18},{3,19},{4,20},{5,21},{6,22},{7,23},{8,24},{9,... | collective-permute-start | bytes 196616 | tf_op jit(solution)/shard_map/ppermute | solution.py:22
  135.5 6.2 %collective-permute-start.5 = (f32[128,128]{0,1:T(8,128)S(1)}, f32[128,128]{0,1:T(8,128)S(1)}, u32[]{:S(2)}, u32[]{:S(2)}) collective-permute-start(f32[128,128]{0,1:T(8,128)S(1)} %multiply_divide_fusion), channel_id=1, source_target_pairs={{0,32},{32,64},{64,96},{96,0},{1,33},{33,65},{65,97},{97,1},{2,34}... | collective-permute-start | bytes 196616 | tf_op jit(solution)/shard_map/ppermute | solution.py:33
  135.7 6.0 %collective-permute-start.6 = (f32[128,128]{0,1:T(8,128)S(1)}, f32[128,128]{0,1:T(8,128)S(1)}, u32[]{:S(2)}, u32[]{:S(2)}) collective-permute-start(f32[128,128]{0,1:T(8,128)S(1)} %multiply_divide_fusion), channel_id=1, source_target_pairs={{0,64},{32,96},{64,0},{96,32},{1,65},{33,97},{65,1},{97,33},{2,66}... | collective-permute-start | bytes 196616 | tf_op jit(solution)/shard_map/ppermute | solution.py:33
  138.5 4.3 %collective-permute-start.7 = (f32[128,128]{0,1:T(8,128)S(1)}, f32[128,128]{0,1:T(8,128)S(1)}, u32[]{:S(2)}, u32[]{:S(2)}) collective-permute-start(f32[128,128]{0,1:T(8,128)S(1)} %multiply_divide_fusion), channel_id=1, source_target_pairs={{0,96},{32,0},{64,32},{96,64},{1,97},{33,1},{65,33},{97,65},{2,98}... | collective-permute-start | bytes 196616 | tf_op jit(solution)/shard_map/ppermute | solution.py:33
Sparse Core Ops, SparseCore 0:
  10.2 75.1 all-gather.2

commit v12 on v11

--- a/solution.py
+++ b/solution.py
@@ -39,17 +39,20 @@
 def masked_apply_kernel(span_ref, env_ref, theta_ref, sec_j_ref, sec_i_ref, out_ref):
     step = pl.program_id(0)
 
-    @pl.when(step == 0)
-    def _():
-        out_ref[...] = jnp.zeros_like(out_ref)
-
-    @pl.when(span_ref[0] + step <= span_ref[1])
-    def _():
+    def product():
         env = env_ref[...]
         env = env.reshape(env.shape[0] * env.shape[1], env.shape[2])
         same = sec_i_ref[...] == sec_j_ref[...]
         masked = jnp.where(same, env, jnp.zeros_like(env))
-        out_ref[...] += jnp.dot(masked, theta_ref[...], preferred_element_type=jnp.float32)
+        return jnp.dot(masked, theta_ref[...], preferred_element_type=jnp.float32)
+
+    @pl.when(step == 0)
+    def _():
+        out_ref[...] = product()
+
+    @pl.when((step > 0) & (span_ref[0] + step <= span_ref[1]))
+    def _():
+        out_ref[...] += product()
 
 
 def masked_apply(env_loc, theta_all, sec_all, my_sec):

time: 156 us -> 155 us (level)
  starting transfers between devices: 28.8 us -> 26 us
  waiting for transfers between devices: 72.3 us -> 74.3 us
    ppermute x5, starting transfers between devices: 23.9 us -> 21.2 us  [butterfly_sum(): value = value + lax.ppermute(value, axis, pairs)]
  transfers between devices with their start and end apart: 9 -> 9, of which waited for: 8 -> 9; matrix products, arithmetic and copies ran while one was open for 11% -> 11% of each run, Pallas kernels for 0% -> 0%
where the time goes in v12:
time: 155 us; the launch traced here: 154 us
  waiting for transfers between devices  74.3 us (48%)
  starting transfers between devices  26 us (17%)
  between operations  18.3 us (12%)
  local copies, waits for them, and re-layouts  16.5 us (11%)
  Pallas kernels  8.46 us (5%)
  matrix products  7.12 us (5%)
  other arithmetic  3.53 us (2%)
    all_gather x1, waiting for transfers between devices, per_device(): theta_all = lax.all_gather(theta_loc, 'blk', axis=0, tiled=True)  57.6 us
    ppermute x5, starting transfers between devices, butterfly_sum(): value = value + lax.ppermute(value, axis, pairs)  21.2 us
    ppermute x5, waiting for transfers between devices, butterfly_sum(): value = value + lax.ppermute(value, axis, pairs)  13 us
    transpose x1, local copies, waits for them, and re-layouts, masked_apply(): jnp.transpose(env_loc, (1, 0, 2))  11.3 us
    pallas_call x1, Pallas kernels, masked_apply(): pl.pallas_call(masked_apply_kernel, grid_spec=grid_spec, out_shape=jax.Sh...  8.46 us
    ppermute x3, starting transfers between devices, gather_all(): parts.append(lax.ppermute(value, axis, pairs))  4.8 us
    dot_general x1, matrix products, per_device(): jnp.einsum('wpq,iwqc->ipc', ops_loc, applied, precision=lax.Precision.HIGH)  4.59 us
  transfers between devices with their start and end apart: 9, of which 9 were waited for; matrix products, arithmetic and copies ran while one was open for 11% of the time, Pallas kernels for 0%

profile of v12, /device:TPU:0, one launch (start us, length us, event | category | flops | bytes accessed | tf_op | source)
XLA Modules:
  0.0 154.2 jit_solution(16178123945327024872)
XLA Ops:
  7.2 0.7 all-gather.3.cloned.1.call-update
  9.1 2.8 %fusion.12 = (s32[]{:T(128)}, s32[]{:T(128)}) fusion(s32[1,4096]{1,0:T(1,128)} %sec_j_ref.1, s32[]{:T(128)} %bitcast, s32[]{:T(128)} %bitcast.2), kind=kLoop, calls=%fused_computation.27 | loop fusion | flops 24574 | bytes 16400 | tf_op jit(solution)/shard_map/reduce_sum | solution.py:62
  16.2 11.3 %copy.18 = bf16[128,8,4096]{2,1,0:T(8,128)(2,1)} copy(bf16[128,8,4096]{2,0,1:T(8,128)(2,1)} %bitcast.78) | data formatting | bytes 16777216 | tf_op jit(solution)/shard_map/transpose | solution.py:66
  27.8 57.6 %all-gather.3.cloned.1.call-done = bf16[1,4096,2048]{2,1,0:T(8,128)(2,1)} async-done(((bf16[1,128,2048]{2,1,0:T(8,128)(2,1)}), bf16[1,4096,2048]{2,1,0:T(8,128)(2,1)}) %all-gather.3.cloned.1.call-update) | async-done | bytes 16777232 | tf_op jit(solution)/shard_map/all_gather | solution.py:106
  85.4 8.5 %shard_map.68 = f32[1024,2048]{1,0:T(8,128)} custom-call(s32[2]{0:T(128)S(1)} %pad_add_fusion.span_ref, bf16[64,16,4096]{2,1,0:T(8,128)(2,1)} %bitcast.76, bf16[4096,2048]{1,0:T(8,128)(2,1)} %bitcast.77, s32[1,4096]{1,0:T(1,128)S(1)} %copy-done, s32[1024,1]{1,0:T(8,128)S(1)} %reshape_reshape.4.sec_i_ref), custom_call_target="tpu_custom_call" | custom-call | tf_op jit(solution)/shard_map/pallas_call | solution.py:83
  93.9 4.6 %fusion.2 = f32[128,16,128]{2,1,0:T(8,128)S(1)} fusion(f32[8,16,16,1]{1,0,2,3:T(8,128)S(1)} %copy.32, f32[1024,2048]{1,0:T(8,128)} %shard_map.68), kind=kOutput, calls=%fused_computation.3 | convolution fusion | flops 201326592 | bytes 9445376 | tf_op jit(solution)/shard_map/wpq,iwqc->ipc/dot_general | solution.py:109
  98.5 0.7 convolution_bitcast_fusion
  99.6 1.0 collective-permute-done
  100.6 2.2 %collective-permute-start.1 = (f32[128,128]{0,1:T(8,128)S(1)}, f32[128,128]{0,1:T(8,128)S(1)}, u32[]{:S(2)}, u32[]{:S(2)}) collective-permute-start(f32[128,128]{0,1:T(8,128)S(1)} %add.61), channel_id=1, source_target_pairs={{0,2},{1,3},{2,0},{3,1},{4,6},{5,7},{6,4},{7,5},{8,10},{9,11},{10,... | collective-permute-start | bytes 196616 | tf_op jit(solution)/shard_map/ppermute | solution.py:22
  102.8 2.6 %collective-permute-done.1 = f32[128,128]{0,1:T(8,128)S(1)} collective-permute-done((f32[128,128]{0,1:T(8,128)S(1)}, f32[128,128]{0,1:T(8,128)S(1)}, u32[]{:S(2)}, u32[]{:S(2)}) %collective-permute-start.1) | collective-permute-done | bytes 65568 | tf_op jit(solution)/shard_map/ppermute | solution.py:22
  105.5 2.1 %collective-permute-start.2 = (f32[128,128]{0,1:T(8,128)S(1)}, f32[128,128]{0,1:T(8,128)S(1)}, u32[]{:S(2)}, u32[]{:S(2)}) collective-permute-start(f32[128,128]{0,1:T(8,128)S(1)} %add.62), channel_id=1, source_target_pairs={{0,4},{1,5},{2,6},{3,7},{4,0},{5,1},{6,2},{7,3},{8,12},{9,13},{10,... | collective-permute-start | bytes 196616 | tf_op jit(solution)/shard_map/ppermute | solution.py:22
  107.6 3.7 %collective-permute-done.2 = f32[128,128]{0,1:T(8,128)S(1)} collective-permute-done((f32[128,128]{0,1:T(8,128)S(1)}, f32[128,128]{0,1:T(8,128)S(1)}, u32[]{:S(2)}, u32[]{:S(2)}) %collective-permute-start.2) | collective-permute-done | bytes 65568 | tf_op jit(solution)/shard_map/ppermute | solution.py:22
  111.3 14.2 %collective-permute-start.3 = (f32[128,128]{0,1:T(8,128)S(1)}, f32[128,128]{0,1:T(8,128)S(1)}, u32[]{:S(2)}, u32[]{:S(2)}) collective-permute-start(f32[128,128]{0,1:T(8,128)S(1)} %add.63), channel_id=1, source_target_pairs={{0,8},{1,9},{2,10},{3,11},{4,12},{5,13},{6,14},{7,15},{8,0},{9,1},... | collective-permute-start | bytes 196616 | tf_op jit(solution)/shard_map/ppermute | solution.py:22
  125.6 2.1 %collective-permute-done.3 = f32[128,128]{0,1:T(8,128)S(1)} collective-permute-done((f32[128,128]{0,1:T(8,128)S(1)}, f32[128,128]{0,1:T(8,128)S(1)}, u32[]{:S(2)}, u32[]{:S(2)}) %collective-permute-start.3) | collective-permute-done | bytes 65568 | tf_op jit(solution)/shard_map/ppermute | solution.py:22
  127.8 2.3 %collective-permute-start.4 = (f32[128,128]{0,1:T(8,128)S(1)}, f32[128,128]{0,1:T(8,128)S(1)}, u32[]{:S(2)}, u32[]{:S(2)}) collective-permute-start(f32[128,128]{0,1:T(8,128)S(1)} %add.64), channel_id=1, source_target_pairs={{0,16},{1,17},{2,18},{3,19},{4,20},{5,21},{6,22},{7,23},{8,24},{9,... | collective-permute-start | bytes 196616 | tf_op jit(solution)/shard_map/ppermute | solution.py:22
  130.1 3.5 %collective-permute-done.4 = f32[128,128]{0,1:T(8,128)S(1)} collective-permute-done((f32[128,128]{0,1:T(8,128)S(1)}, f32[128,128]{0,1:T(8,128)S(1)}, u32[]{:S(2)}, u32[]{:S(2)}) %collective-permute-start.4) | collective-permute-done | bytes 65568 | tf_op jit(solution)/shard_map/ppermute | solution.py:22
  135.0 3.4 %collective-permute-start.6 = (f32[128,128]{0,1:T(8,128)S(1)}, f32[128,128]{0,1:T(8,128)S(1)}, u32[]{:S(2)}, u32[]{:S(2)}) collective-permute-start(f32[128,128]{0,1:T(8,128)S(1)} %multiply_divide_fusion), channel_id=1, source_target_pairs={{0,64},{32,96},{64,0},{96,32},{1,65},{33,97},{65,1},{97,33},{2,66}... | collective-permute-start | bytes 196616 | tf_op jit(solution)/shard_map/ppermute | solution.py:33
  138.5 1.3 collective-permute-start.7
  139.8 0.7 collective-permute-done.5
  140.5 0.9 collective-permute-done.6
  141.4 1.3 collective-permute-done.7
  144.7 0.9 convolution_convert_fusion
  145.6 1.0 copy.29
  146.6 0.7 copy.30
  (41 shorter events, 5.6 us)
Async XLA Ops:
  7.2 78.3 %all-gather.3.cloned.1.call-start = ((), (), s32[]{:S(2)}) async-start(), calls=%async_computation | async-start | bytes 17301504 | tf_op jit(solution)/shard_map/all_gather | solution.py:106
  16.2 11.3 %copy-start.3 = (f32[1,8,16,16]{3,2,1,0:T(8,128)S(1)}, f32[1,8,16,16]{3,2,1,0:T(8,128)}, u32[]{:S(2)}) copy-start(f32[1,8,16,16]{3,2,1,0:T(8,128)} %param.8) | copy-start | bytes 24580
  16.2 11.4 %copy-start.1 = (bf16[1,128,2048]{2,1,0:T(8,128)(2,1)S(1)}, bf16[1,128,2048]{2,1,0:T(8,128)(2,1)}, u32[]{:S(2)}) copy-start(bf16[1,128,2048]{2,1,0:T(8,128)(2,1)} %param.5) | copy-start | bytes 1572868
  16.2 69.2 %copy-start = (s32[1,4096]{1,0:T(1,128)S(1)}, s32[1,4096]{1,0:T(1,128)}, u32[]{:S(2)}) copy-start(s32[1,4096]{1,0:T(1,128)} %sec_j_ref.1) | copy-start | bytes 49156
  93.9 31.6 %copy-start.2 = (f32[128,128]{1,0:T(8,128)S(1)}, f32[128,128]{1,0:T(8,128)}, u32[]{:S(2)}) copy-start(f32[128,128]{1,0:T(8,128)} %param.9) | copy-start | bytes 196612
  99.2 1.3 collective-permute-start
  100.6 4.9 %collective-permute-start.1 = (f32[128,128]{0,1:T(8,128)S(1)}, f32[128,128]{0,1:T(8,128)S(1)}, u32[]{:S(2)}, u32[]{:S(2)}) collective-permute-start(f32[128,128]{0,1:T(8,128)S(1)} %add.61), channel_id=1, source_target_pairs={{0,2},{1,3},{2,0},{3,1},{4,6},{5,7},{6,4},{7,5},{8,10},{9,11},{10,... | collective-permute-start | bytes 196616 | tf_op jit(solution)/shard_map/ppermute | solution.py:22
  105.5 5.8 %collective-permute-start.2 = (f32[128,128]{0,1:T(8,128)S(1)}, f32[128,128]{0,1:T(8,128)S(1)}, u32[]{:S(2)}, u32[]{:S(2)}) collective-permute-start(f32[128,128]{0,1:T(8,128)S(1)} %add.62), channel_id=1, source_target_pairs={{0,4},{1,5},{2,6},{3,7},{4,0},{5,1},{6,2},{7,3},{8,12},{9,13},{10,... | collective-permute-start | bytes 196616 | tf_op jit(solution)/shard_map/ppermute | solution.py:22
  111.3 16.4 %collective-permute-start.3 = (f32[128,128]{0,1:T(8,128)S(1)}, f32[128,128]{0,1:T(8,128)S(1)}, u32[]{:S(2)}, u32[]{:S(2)}) collective-permute-start(f32[128,128]{0,1:T(8,128)S(1)} %add.63), channel_id=1, source_target_pairs={{0,8},{1,9},{2,10},{3,11},{4,12},{5,13},{6,14},{7,15},{8,0},{9,1},... | collective-permute-start | bytes 196616 | tf_op jit(solution)/shard_map/ppermute | solution.py:22
  127.8 5.8 %collective-permute-start.4 = (f32[128,128]{0,1:T(8,128)S(1)}, f32[128,128]{0,1:T(8,128)S(1)}, u32[]{:S(2)}, u32[]{:S(2)}) collective-permute-start(f32[128,128]{0,1:T(8,128)S(1)} %add.64), channel_id=1, source_target_pairs={{0,16},{1,17},{2,18},{3,19},{4,20},{5,21},{6,22},{7,23},{8,24},{9,... | collective-permute-start | bytes 196616 | tf_op jit(solution)/shard_map/ppermute | solution.py:22
  134.9 5.5 %collective-permute-start.5 = (f32[128,128]{0,1:T(8,128)S(1)}, f32[128,128]{0,1:T(8,128)S(1)}, u32[]{:S(2)}, u32[]{:S(2)}) collective-permute-start(f32[128,128]{0,1:T(8,128)S(1)} %multiply_divide_fusion), channel_id=1, source_target_pairs={{0,32},{32,64},{64,96},{96,0},{1,33},{33,65},{65,97},{97,1},{2,34}... | collective-permute-start | bytes 196616 | tf_op jit(solution)/shard_map/ppermute | solution.py:33
  135.0 6.4 %collective-permute-start.6 = (f32[128,128]{0,1:T(8,128)S(1)}, f32[128,128]{0,1:T(8,128)S(1)}, u32[]{:S(2)}, u32[]{:S(2)}) collective-permute-start(f32[128,128]{0,1:T(8,128)S(1)} %multiply_divide_fusion), channel_id=1, source_target_pairs={{0,64},{32,96},{64,0},{96,32},{1,65},{33,97},{65,1},{97,33},{2,66}... | collective-permute-start | bytes 196616 | tf_op jit(solution)/shard_map/ppermute | solution.py:33
  138.5 4.3 %collective-permute-start.7 = (f32[128,128]{0,1:T(8,128)S(1)}, f32[128,128]{0,1:T(8,128)S(1)}, u32[]{:S(2)}, u32[]{:S(2)}) collective-permute-start(f32[128,128]{0,1:T(8,128)S(1)} %multiply_divide_fusion), channel_id=1, source_target_pairs={{0,96},{32,0},{64,32},{96,64},{1,97},{33,1},{65,33},{97,65},{2,98}... | collective-permute-start | bytes 196616 | tf_op jit(solution)/shard_map/ppermute | solution.py:33
Sparse Core Ops, SparseCore 0:
  10.2 75.1 all-gather.2

commit v13 on v12

--- a/solution.py
+++ b/solution.py
@@ -14,13 +14,19 @@
     return jnp.dot(first, second, precision=lax.Precision.HIGH)
 
 
-def butterfly_sum(value, axis):
+def grouped_sum(value, axis, sizes):
     peers = lax.axis_size(axis)
-    step = 1
-    while step < peers:
-        pairs = [(i, i ^ step) for i in range(peers)]
-        value = value + lax.ppermute(value, axis, pairs)
-        step *= 2
+    stride = 1
+    for size in sizes:
+        total = value
+        for shift in range(1, size):
+            pairs = []
+            for i in range(peers):
+                digit = (i // stride) % size
+                pairs.append((i, i + ((digit + shift) % size - digit) * stride))
+            total = total + lax.ppermute(value, axis, pairs)
+        value = total
+        stride *= size
     return value
 
 
@@ -111,7 +117,8 @@
     partial_intersection = jnp.einsum(
         "ipc,ipd->cd", theta_f, acted, precision=lax.Precision.HIGH
     )
-    intersection = butterfly_sum(partial_intersection, "blk")
+    blk_peers = lax.axis_size("blk")
+    intersection = grouped_sum(partial_intersection, "blk", (2, 4, blk_peers // 8))
     transfer = (
         intersection
         * jnp.sqrt(jnp.float32(cols))

time: 155 us -> 150 us (0.968)
  waiting for transfers between devices: 74.3 us -> 67.1 us
  starting transfers between devices: 26 us -> 30.4 us
    ppermute x5 -> x7, waiting for transfers between devices: 13 us -> 5.73 us  [grouped_sum(): total = total + lax.ppermute(value, axis, pairs)]
    ppermute x5 -> x7, starting transfers between devices: 21.2 us -> 23.9 us  [grouped_sum(): total = total + lax.ppermute(value, axis, pairs)]
    ppermute x3, starting transfers between devices: 4.8 us -> 6.47 us  [gather_all(): parts.append(lax.ppermute(value, axis, pairs))]
  transfers between devices with their start and end apart: 9 -> 11, of which waited for: 9 -> 10; matrix products, arithmetic and copies ran while one was open for 11% -> 11% of each run, Pallas kernels for 0% -> 0%
where the time goes in v13:
time: 150 us
  waiting for transfers between devices  67.1 us (45%)
  starting transfers between devices  30.4 us (20%)
  between operations  18.1 us (12%)
  local copies, waits for them, and re-layouts  16.5 us (11%)
  Pallas kernels  7.17 us (5%)
  matrix products  7.12 us (5%)
  other arithmetic  3.51 us (2%)
    all_gather x1, waiting for transfers between devices, per_device(): theta_all = lax.all_gather(theta_loc, 'blk', axis=0, tiled=True)  57.8 us
    ppermute x7, starting transfers between devices, grouped_sum(): total = total + lax.ppermute(value, axis, pairs)  23.9 us
    transpose x1, local copies, waits for them, and re-layouts, masked_apply(): jnp.transpose(env_loc, (1, 0, 2))  11.3 us
    pallas_call x1, Pallas kernels, masked_apply(): pl.pallas_call(masked_apply_kernel, grid_spec=grid_spec, out_shape=jax.Sh...  7.17 us
    ppermute x3, starting transfers between devices, gather_all(): parts.append(lax.ppermute(value, axis, pairs))  6.47 us
    ppermute x7, waiting for transfers between devices, grouped_sum(): total = total + lax.ppermute(value, axis, pairs)  5.73 us
    dot_general x1, matrix products, per_device(): jnp.einsum('wpq,iwqc->ipc', ops_loc, applied, precision=lax.Precision.HIGH)  4.59 us
  transfers between devices with their start and end apart: 11, of which 10 were waited for; matrix products, arithmetic and copies ran while one was open for 11% of the time, Pallas kernels for 0%

profile of v13, /device:TPU:0, one launch (start us, length us, event | category | flops | bytes accessed | tf_op | source)
XLA Modules:
  0.0 149.8 jit_solution(8975795095501818236)
XLA Ops:
  7.2 0.7 all-gather.3.cloned.1.call-update
  9.1 2.7 %fusion.12 = (s32[]{:T(128)}, s32[]{:T(128)}) fusion(s32[1,4096]{1,0:T(1,128)} %sec_j_ref.1, s32[]{:T(128)} %bitcast, s32[]{:T(128)} %bitcast.2), kind=kLoop, calls=%fused_computation.29 | loop fusion | flops 24574 | bytes 16400 | tf_op jit(solution)/shard_map/reduce_sum | solution.py:68
  16.0 11.3 %copy.18 = bf16[128,8,4096]{2,1,0:T(8,128)(2,1)} copy(bf16[128,8,4096]{2,0,1:T(8,128)(2,1)} %bitcast.79) | data formatting | bytes 16777216 | tf_op jit(solution)/shard_map/transpose | solution.py:72
  27.6 57.8 %all-gather.3.cloned.1.call-done = bf16[1,4096,2048]{2,1,0:T(8,128)(2,1)} async-done(((bf16[1,128,2048]{2,1,0:T(8,128)(2,1)}), bf16[1,4096,2048]{2,1,0:T(8,128)(2,1)}) %all-gather.3.cloned.1.call-update) | async-done | bytes 16777232 | tf_op jit(solution)/shard_map/all_gather | solution.py:112
  85.4 7.2 %shard_map.68 = f32[1024,2048]{1,0:T(8,128)} custom-call(s32[2]{0:T(128)S(1)} %pad_add_fusion.span_ref, bf16[64,16,4096]{2,1,0:T(8,128)(2,1)} %bitcast.77, bf16[4096,2048]{1,0:T(8,128)(2,1)} %bitcast.78, s32[1,4096]{1,0:T(1,128)S(1)} %copy-done, s32[1024,1]{1,0:T(8,128)S(1)} %reshape_reshape.4.sec_i_ref), custom_call_target="tpu_custom_call" | custom-call | tf_op jit(solution)/shard_map/pallas_call | solution.py:89
  92.6 4.6 %fusion.2 = f32[128,16,128]{2,1,0:T(8,128)S(1)} fusion(f32[8,16,16,1]{1,0,2,3:T(8,128)S(1)} %copy.32, f32[1024,2048]{1,0:T(8,128)} %shard_map.68), kind=kOutput, calls=%fused_computation.3 | convolution fusion | flops 201326592 | bytes 9445376 | tf_op jit(solution)/shard_map/wpq,iwqc->ipc/dot_general | solution.py:115
  97.2 0.7 convolution_bitcast_fusion
  98.0 13.5 %collective-permute-start = (f32[128,128]{0,1:T(8,128)S(1)}, f32[128,128]{0,1:T(8,128)S(1)}, u32[]{:S(2)}, u32[]{:S(2)}) collective-permute-start(f32[128,128]{0,1:T(8,128)S(1)} %convolution_bitcast_fusion), channel_id=1, source_target_pairs={{0,1},{1,0},{2,3},{3,2},{4,5},{5,4},{6,7},{7,6},{8,9},{9,8},{10,11... | collective-permute-start | bytes 196616 | tf_op jit(solution)/shard_map/ppermute | solution.py:27
  111.5 0.8 collective-permute-done
  112.3 1.1 collective-permute-start.1
  113.4 2.9 %collective-permute-start.2 = (f32[128,128]{0,1:T(8,128)S(1)}, f32[128,128]{0,1:T(8,128)S(1)}, u32[]{:S(2)}, u32[]{:S(2)}) collective-permute-start(f32[128,128]{0,1:T(8,128)S(1)} %add.67), channel_id=1, source_target_pairs={{0,4},{1,5},{2,6},{3,7},{4,0},{5,1},{6,2},{7,3},{8,12},{9,13},{10,... | collective-permute-start | bytes 196616 | tf_op jit(solution)/shard_map/ppermute | solution.py:27
  116.3 1.4 collective-permute-start.3
  118.1 1.8 %collective-permute-done.2 = f32[128,128]{0,1:T(8,128)S(1)} collective-permute-done((f32[128,128]{0,1:T(8,128)S(1)}, f32[128,128]{0,1:T(8,128)S(1)}, u32[]{:S(2)}, u32[]{:S(2)}) %collective-permute-start.2) | collective-permute-done | bytes 65568 | tf_op jit(solution)/shard_map/ppermute | solution.py:27
  120.6 0.9 collective-permute-start.4
  121.5 1.6 %collective-permute-start.5 = (f32[128,128]{0,1:T(8,128)S(1)}, f32[128,128]{0,1:T(8,128)S(1)}, u32[]{:S(2)}, u32[]{:S(2)}) collective-permute-start(f32[128,128]{0,1:T(8,128)S(1)} %add_add_fusion.1), channel_id=1, source_target_pairs={{0,16},{1,17},{2,18},{3,19},{4,20},{5,21},{6,22},{7,23},{8,24},{9,... | collective-permute-start | bytes 196616 | tf_op jit(solution)/shard_map/ppermute | solution.py:27
  123.1 2.5 %collective-permute-start.6 = (f32[128,128]{0,1:T(8,128)S(1)}, f32[128,128]{0,1:T(8,128)S(1)}, u32[]{:S(2)}, u32[]{:S(2)}) collective-permute-start(f32[128,128]{0,1:T(8,128)S(1)} %add_add_fusion.1), channel_id=1, source_target_pairs={{0,24},{1,25},{2,26},{3,27},{4,28},{5,29},{6,30},{7,31},{8,0},{9,1... | collective-permute-start | bytes 196616 | tf_op jit(solution)/shard_map/ppermute | solution.py:27
  126.3 1.0 collective-permute-done.5
  129.3 4.8 %collective-permute-start.8 = (f32[128,128]{0,1:T(8,128)S(1)}, f32[128,128]{0,1:T(8,128)S(1)}, u32[]{:S(2)}, u32[]{:S(2)}) collective-permute-start(f32[128,128]{0,1:T(8,128)S(1)} %multiply_divide_fusion), channel_id=1, source_target_pairs={{0,64},{32,96},{64,0},{96,32},{1,65},{33,97},{65,1},{97,33},{2,66}... | collective-permute-start | bytes 196616 | tf_op jit(solution)/shard_map/ppermute | solution.py:39
  134.1 1.4 collective-permute-start.9
  135.5 1.5 collective-permute-done.8
  137.0 1.3 collective-permute-done.9
  140.3 0.9 convolution_convert_fusion
  141.2 1.0 copy.29
  142.2 0.7 copy.30
  (44 shorter events, 7.6 us)
Async XLA Ops:
  7.2 78.3 %all-gather.3.cloned.1.call-start = ((), (), s32[]{:S(2)}) async-start(), calls=%async_computation | async-start | bytes 17301504 | tf_op jit(solution)/shard_map/all_gather | solution.py:112
  16.0 11.3 %copy-start.3 = (f32[1,8,16,16]{3,2,1,0:T(8,128)S(1)}, f32[1,8,16,16]{3,2,1,0:T(8,128)}, u32[]{:S(2)}) copy-start(f32[1,8,16,16]{3,2,1,0:T(8,128)} %param.8) | copy-start | bytes 24580
  16.0 11.4 %copy-start.1 = (bf16[1,128,2048]{2,1,0:T(8,128)(2,1)S(1)}, bf16[1,128,2048]{2,1,0:T(8,128)(2,1)}, u32[]{:S(2)}) copy-start(bf16[1,128,2048]{2,1,0:T(8,128)(2,1)} %param.5) | copy-start | bytes 1572868
  16.0 69.4 %copy-start = (s32[1,4096]{1,0:T(1,128)S(1)}, s32[1,4096]{1,0:T(1,128)}, u32[]{:S(2)}) copy-start(s32[1,4096]{1,0:T(1,128)} %sec_j_ref.1) | copy-start | bytes 49156
  92.6 18.8 %copy-start.2 = (f32[128,128]{1,0:T(8,128)S(1)}, f32[128,128]{1,0:T(8,128)}, u32[]{:S(2)}) copy-start(f32[128,128]{1,0:T(8,128)} %param.9) | copy-start | bytes 196612
  98.0 14.4 %collective-permute-start = (f32[128,128]{0,1:T(8,128)S(1)}, f32[128,128]{0,1:T(8,128)S(1)}, u32[]{:S(2)}, u32[]{:S(2)}) collective-permute-start(f32[128,128]{0,1:T(8,128)S(1)} %convolution_bitcast_fusion), channel_id=1, source_target_pairs={{0,1},{1,0},{2,3},{3,2},{4,5},{5,4},{6,7},{7,6},{8,9},{9,8},{10,11... | collective-permute-start | bytes 196616 | tf_op jit(solution)/shard_map/ppermute | solution.py:27
  112.3 5.8 %collective-permute-start.1 = (f32[128,128]{0,1:T(8,128)S(1)}, f32[128,128]{0,1:T(8,128)S(1)}, u32[]{:S(2)}, u32[]{:S(2)}) collective-permute-start(f32[128,128]{0,1:T(8,128)S(1)} %add.67), channel_id=1, source_target_pairs={{0,2},{1,3},{2,4},{3,5},{4,6},{5,7},{6,0},{7,1},{8,10},{9,11},{10,... | collective-permute-start | bytes 196616 | tf_op jit(solution)/shard_map/ppermute | solution.py:27
  113.4 6.5 %collective-permute-start.2 = (f32[128,128]{0,1:T(8,128)S(1)}, f32[128,128]{0,1:T(8,128)S(1)}, u32[]{:S(2)}, u32[]{:S(2)}) collective-permute-start(f32[128,128]{0,1:T(8,128)S(1)} %add.67), channel_id=1, source_target_pairs={{0,4},{1,5},{2,6},{3,7},{4,0},{5,1},{6,2},{7,3},{8,12},{9,13},{10,... | collective-permute-start | bytes 196616 | tf_op jit(solution)/shard_map/ppermute | solution.py:27
  116.3 4.3 %collective-permute-start.3 = (f32[128,128]{0,1:T(8,128)S(1)}, f32[128,128]{0,1:T(8,128)S(1)}, u32[]{:S(2)}, u32[]{:S(2)}) collective-permute-start(f32[128,128]{0,1:T(8,128)S(1)} %add.67), channel_id=1, source_target_pairs={{0,6},{1,7},{2,0},{3,1},{4,2},{5,3},{6,4},{7,5},{8,14},{9,15},{10,... | collective-permute-start | bytes 196616 | tf_op jit(solution)/shard_map/ppermute | solution.py:27
  120.6 5.7 %collective-permute-start.4 = (f32[128,128]{0,1:T(8,128)S(1)}, f32[128,128]{0,1:T(8,128)S(1)}, u32[]{:S(2)}, u32[]{:S(2)}) collective-permute-start(f32[128,128]{0,1:T(8,128)S(1)} %add_add_fusion.1), channel_id=1, source_target_pairs={{0,8},{1,9},{2,10},{3,11},{4,12},{5,13},{6,14},{7,15},{8,16},{9,17... | collective-permute-start | bytes 196616 | tf_op jit(solution)/shard_map/ppermute | solution.py:27
  121.5 5.8 %collective-permute-start.5 = (f32[128,128]{0,1:T(8,128)S(1)}, f32[128,128]{0,1:T(8,128)S(1)}, u32[]{:S(2)}, u32[]{:S(2)}) collective-permute-start(f32[128,128]{0,1:T(8,128)S(1)} %add_add_fusion.1), channel_id=1, source_target_pairs={{0,16},{1,17},{2,18},{3,19},{4,20},{5,21},{6,22},{7,23},{8,24},{9,... | collective-permute-start | bytes 196616 | tf_op jit(solution)/shard_map/ppermute | solution.py:27
  123.1 4.6 %collective-permute-start.6 = (f32[128,128]{0,1:T(8,128)S(1)}, f32[128,128]{0,1:T(8,128)S(1)}, u32[]{:S(2)}, u32[]{:S(2)}) collective-permute-start(f32[128,128]{0,1:T(8,128)S(1)} %add_add_fusion.1), channel_id=1, source_target_pairs={{0,24},{1,25},{2,26},{3,27},{4,28},{5,29},{6,30},{7,31},{8,0},{9,1... | collective-permute-start | bytes 196616 | tf_op jit(solution)/shard_map/ppermute | solution.py:27
  129.0 6.5 %collective-permute-start.7 = (f32[128,128]{0,1:T(8,128)S(1)}, f32[128,128]{0,1:T(8,128)S(1)}, u32[]{:S(2)}, u32[]{:S(2)}) collective-permute-start(f32[128,128]{0,1:T(8,128)S(1)} %multiply_divide_fusion), channel_id=1, source_target_pairs={{0,32},{32,64},{64,96},{96,0},{1,33},{33,65},{65,97},{97,1},{2,34}... | collective-permute-start | bytes 196616 | tf_op jit(solution)/shard_map/ppermute | solution.py:39
  129.3 7.7 %collective-permute-start.8 = (f32[128,128]{0,1:T(8,128)S(1)}, f32[128,128]{0,1:T(8,128)S(1)}, u32[]{:S(2)}, u32[]{:S(2)}) collective-permute-start(f32[128,128]{0,1:T(8,128)S(1)} %multiply_divide_fusion), channel_id=1, source_target_pairs={{0,64},{32,96},{64,0},{96,32},{1,65},{33,97},{65,1},{97,33},{2,66}... | collective-permute-start | bytes 196616 | tf_op jit(solution)/shard_map/ppermute | solution.py:39
  134.1 4.3 %collective-permute-start.9 = (f32[128,128]{0,1:T(8,128)S(1)}, f32[128,128]{0,1:T(8,128)S(1)}, u32[]{:S(2)}, u32[]{:S(2)}) collective-permute-start(f32[128,128]{0,1:T(8,128)S(1)} %multiply_divide_fusion), channel_id=1, source_target_pairs={{0,96},{32,0},{64,32},{96,64},{1,97},{33,1},{65,33},{97,65},{2,98}... | collective-permute-start | bytes 196616 | tf_op jit(solution)/shard_map/ppermute | solution.py:39
Sparse Core Ops, SparseCore 0:
  10.2 75.1 all-gather.2

commit v14 on v13

--- a/solution.py
+++ b/solution.py
@@ -118,7 +118,7 @@
         "ipc,ipd->cd", theta_f, acted, precision=lax.Precision.HIGH
     )
     blk_peers = lax.axis_size("blk")
-    intersection = grouped_sum(partial_intersection, "blk", (2, 4, blk_peers // 8))
+    intersection = grouped_sum(partial_intersection, "blk", (8, blk_peers // 8))
     transfer = (
         intersection
         * jnp.sqrt(jnp.float32(cols))

time: 150 us -> 153 us (1.020)
  starting transfers between devices: 30.4 us -> 33.3 us
    ppermute x7 -> x10, starting transfers between devices: 23.9 us -> 27.2 us  [grouped_sum(): total = total + lax.ppermute(value, axis, pairs)]
    ppermute x7 -> x10, waiting for transfers between devices: 5.73 us -> 5.25 us  [grouped_sum(): total = total + lax.ppermute(value, axis, pairs)]
  transfers between devices with their start and end apart: 11 -> 14, of which waited for: 10 -> 8; matrix products, arithmetic and copies ran while one was open for 11% -> 11% of each run, Pallas kernels for 0% -> 0%
where the time goes in v14:
time: 153 us; the launch traced here: 152 us
  waiting for transfers between devices  66.5 us (43%)
  starting transfers between devices  33.3 us (22%)
  between operations  18 us (12%)
  local copies, waits for them, and re-layouts  16.5 us (11%)
  Pallas kernels  7.17 us (5%)
  matrix products  7.13 us (5%)
  other arithmetic  3.51 us (2%)
    all_gather x1, waiting for transfers between devices, per_device(): theta_all = lax.all_gather(theta_loc, 'blk', axis=0, tiled=True)  57.9 us
    ppermute x10, starting transfers between devices, grouped_sum(): total = total + lax.ppermute(value, axis, pairs)  27.2 us
    transpose x1, local copies, waits for them, and re-layouts, masked_apply(): jnp.transpose(env_loc, (1, 0, 2))  11.3 us
    pallas_call x1, Pallas kernels, masked_apply(): pl.pallas_call(masked_apply_kernel, grid_spec=grid_spec, out_shape=jax.Sh...  7.17 us
    ppermute x3, starting transfers between devices, gather_all(): parts.append(lax.ppermute(value, axis, pairs))  6.07 us
    ppermute x10, waiting for transfers between devices, grouped_sum(): total = total + lax.ppermute(value, axis, pairs)  5.25 us
    dot_general x1, matrix products, per_device(): jnp.einsum('wpq,iwqc->ipc', ops_loc, applied, precision=lax.Precision.HIGH)  4.59 us
  transfers between devices with their start and end apart: 14, of which 8 were waited for; matrix products, arithmetic and copies ran while one was open for 11% of the time, Pallas kernels for 0%

profile of v14, /device:TPU:0, one launch (start us, length us, event | category | flops | bytes accessed | tf_op | source)
XLA Modules:
  0.0 152.1 jit_solution(633515327126640850)
XLA Ops:
  9.1 2.7 %fusion.12 = (s32[]{:T(128)}, s32[]{:T(128)}) fusion(s32[1,4096]{1,0:T(1,128)} %sec_j_ref.1, s32[]{:T(128)} %bitcast, s32[]{:T(128)} %bitcast.2), kind=kLoop, calls=%fused_computation.29 | loop fusion | flops 24574 | bytes 16400 | tf_op jit(solution)/shard_map/reduce_sum | solution.py:68
  15.9 11.3 %copy.18 = bf16[128,8,4096]{2,1,0:T(8,128)(2,1)} copy(bf16[128,8,4096]{2,0,1:T(8,128)(2,1)} %bitcast.79) | data formatting | bytes 16777216 | tf_op jit(solution)/shard_map/transpose | solution.py:72
  27.5 57.9 %all-gather.3.cloned.1.call-done = bf16[1,4096,2048]{2,1,0:T(8,128)(2,1)} async-done(((bf16[1,128,2048]{2,1,0:T(8,128)(2,1)}), bf16[1,4096,2048]{2,1,0:T(8,128)(2,1)}) %all-gather.3.cloned.1.call-update) | async-done | bytes 16777232 | tf_op jit(solution)/shard_map/all_gather | solution.py:112
  85.4 7.2 %shard_map.68 = f32[1024,2048]{1,0:T(8,128)} custom-call(s32[2]{0:T(128)S(1)} %pad_add_fusion.span_ref, bf16[64,16,4096]{2,1,0:T(8,128)(2,1)} %bitcast.77, bf16[4096,2048]{1,0:T(8,128)(2,1)} %bitcast.78, s32[1,4096]{1,0:T(1,128)S(1)} %copy-done, s32[1024,1]{1,0:T(8,128)S(1)} %reshape_reshape.4.sec_i_ref), custom_call_target="tpu_custom_call" | custom-call | tf_op jit(solution)/shard_map/pallas_call | solution.py:89
  92.6 4.6 %fusion.2 = f32[128,16,128]{2,1,0:T(8,128)S(1)} fusion(f32[8,16,16,1]{1,0,2,3:T(8,128)S(1)} %copy.32, f32[1024,2048]{1,0:T(8,128)} %shard_map.68), kind=kOutput, calls=%fused_computation.3 | convolution fusion | flops 201326592 | bytes 9445376 | tf_op jit(solution)/shard_map/wpq,iwqc->ipc/dot_general | solution.py:115
  98.0 1.6 %collective-permute-start = (f32[128,128]{0,1:T(8,128)S(1)}, f32[128,128]{0,1:T(8,128)S(1)}, u32[]{:S(2)}, u32[]{:S(2)}) collective-permute-start(f32[128,128]{0,1:T(8,128)S(1)} %convolution_bitcast_fusion), channel_id=1, source_target_pairs={{0,1},{1,2},{2,3},{3,4},{4,5},{5,6},{6,7},{7,0},{8,9},{9,10},{10,1... | collective-permute-start | bytes 196616 | tf_op jit(solution)/shard_map/ppermute | solution.py:27
  99.5 12.8 %collective-permute-start.1 = (f32[128,128]{0,1:T(8,128)S(1)}, f32[128,128]{0,1:T(8,128)S(1)}, u32[]{:S(2)}, u32[]{:S(2)}) collective-permute-start(f32[128,128]{0,1:T(8,128)S(1)} %convolution_bitcast_fusion), channel_id=1, source_target_pairs={{0,2},{1,3},{2,4},{3,5},{4,6},{5,7},{6,0},{7,1},{8,10},{9,11},{10,... | collective-permute-start | bytes 196616 | tf_op jit(solution)/shard_map/ppermute | solution.py:27
  112.4 2.1 %collective-permute-start.2 = (f32[128,128]{0,1:T(8,128)S(1)}, f32[128,128]{0,1:T(8,128)S(1)}, u32[]{:S(2)}, u32[]{:S(2)}) collective-permute-start(f32[128,128]{0,1:T(8,128)S(1)} %convolution_bitcast_fusion), channel_id=1, source_target_pairs={{0,3},{1,4},{2,5},{3,6},{4,7},{5,0},{6,1},{7,2},{8,11},{9,12},{10,... | collective-permute-start | bytes 196616 | tf_op jit(solution)/shard_map/ppermute | solution.py:27
  114.5 0.9 collective-permute-start.3
  115.4 2.9 %collective-permute-start.4 = (f32[128,128]{0,1:T(8,128)S(1)}, f32[128,128]{0,1:T(8,128)S(1)}, u32[]{:S(2)}, u32[]{:S(2)}) collective-permute-start(f32[128,128]{0,1:T(8,128)S(1)} %convolution_bitcast_fusion), channel_id=1, source_target_pairs={{0,5},{1,6},{2,7},{3,0},{4,1},{5,2},{6,3},{7,4},{8,13},{9,14},{10,... | collective-permute-start | bytes 196616 | tf_op jit(solution)/shard_map/ppermute | solution.py:27
  118.3 1.4 collective-permute-start.5
  119.7 1.2 collective-permute-done.3
  120.9 1.6 %collective-permute-done.5 = f32[128,128]{0,1:T(8,128)S(1)} collective-permute-done((f32[128,128]{0,1:T(8,128)S(1)}, f32[128,128]{0,1:T(8,128)S(1)}, u32[]{:S(2)}, u32[]{:S(2)}) %collective-permute-start.5) | collective-permute-done | bytes 65568 | tf_op jit(solution)/shard_map/ppermute | solution.py:27
  122.6 1.4 collective-permute-start.7
  124.0 1.7 %collective-permute-start.8 = (f32[128,128]{0,1:T(8,128)S(1)}, f32[128,128]{0,1:T(8,128)S(1)}, u32[]{:S(2)}, u32[]{:S(2)}) collective-permute-start(f32[128,128]{0,1:T(8,128)S(1)} %add_add_fusion.1), channel_id=1, source_target_pairs={{0,16},{1,17},{2,18},{3,19},{4,20},{5,21},{6,22},{7,23},{8,24},{9,... | collective-permute-start | bytes 196616 | tf_op jit(solution)/shard_map/ppermute | solution.py:27
  125.7 2.5 %collective-permute-start.9 = (f32[128,128]{0,1:T(8,128)S(1)}, f32[128,128]{0,1:T(8,128)S(1)}, u32[]{:S(2)}, u32[]{:S(2)}) collective-permute-start(f32[128,128]{0,1:T(8,128)S(1)} %add_add_fusion.1), channel_id=1, source_target_pairs={{0,24},{1,25},{2,26},{3,27},{4,28},{5,29},{6,30},{7,31},{8,0},{9,1... | collective-permute-start | bytes 196616 | tf_op jit(solution)/shard_map/ppermute | solution.py:27
  128.2 1.8 %collective-permute-done.7 = f32[128,128]{0,1:T(8,128)S(1)} collective-permute-done((f32[128,128]{0,1:T(8,128)S(1)}, f32[128,128]{0,1:T(8,128)S(1)}, u32[]{:S(2)}, u32[]{:S(2)}) %collective-permute-start.7) | collective-permute-done | bytes 65568 | tf_op jit(solution)/shard_map/ppermute | solution.py:27
  131.9 1.9 %collective-permute-start.10 = (f32[128,128]{0,1:T(8,128)S(1)}, f32[128,128]{0,1:T(8,128)S(1)}, u32[]{:S(2)}, u32[]{:S(2)}) collective-permute-start(f32[128,128]{0,1:T(8,128)S(1)} %multiply_divide_fusion), channel_id=1, source_target_pairs={{0,32},{32,64},{64,96},{96,0},{1,33},{33,65},{65,97},{97,1},{2,34}... | collective-permute-start | bytes 196616 | tf_op jit(solution)/shard_map/ppermute | solution.py:39
  133.8 2.5 %collective-permute-start.11 = (f32[128,128]{0,1:T(8,128)S(1)}, f32[128,128]{0,1:T(8,128)S(1)}, u32[]{:S(2)}, u32[]{:S(2)}) collective-permute-start(f32[128,128]{0,1:T(8,128)S(1)} %multiply_divide_fusion), channel_id=1, source_target_pairs={{0,64},{32,96},{64,0},{96,32},{1,65},{33,97},{65,1},{97,33},{2,66}... | collective-permute-start | bytes 196616 | tf_op jit(solution)/shard_map/ppermute | solution.py:39
  136.4 1.6 %collective-permute-start.12 = (f32[128,128]{0,1:T(8,128)S(1)}, f32[128,128]{0,1:T(8,128)S(1)}, u32[]{:S(2)}, u32[]{:S(2)}) collective-permute-start(f32[128,128]{0,1:T(8,128)S(1)} %multiply_divide_fusion), channel_id=1, source_target_pairs={{0,96},{32,0},{64,32},{96,64},{1,97},{33,1},{65,33},{97,65},{2,98}... | collective-permute-start | bytes 196616 | tf_op jit(solution)/shard_map/ppermute | solution.py:39
  138.2 1.4 collective-permute-done.11
  139.6 1.0 collective-permute-done.12
  142.6 0.9 convolution_convert_fusion
  143.5 1.0 copy.29
  (49 shorter events, 8.2 us)
Async XLA Ops:
  7.2 78.3 %all-gather.3.cloned.1.call-start = ((), (), s32[]{:S(2)}) async-start(), calls=%async_computation | async-start | bytes 17301504 | tf_op jit(solution)/shard_map/all_gather | solution.py:112
  15.9 11.3 %copy-start.3 = (f32[1,8,16,16]{3,2,1,0:T(8,128)S(1)}, f32[1,8,16,16]{3,2,1,0:T(8,128)}, u32[]{:S(2)}) copy-start(f32[1,8,16,16]{3,2,1,0:T(8,128)} %param.8) | copy-start | bytes 24580
  15.9 11.4 %copy-start.1 = (bf16[1,128,2048]{2,1,0:T(8,128)(2,1)S(1)}, bf16[1,128,2048]{2,1,0:T(8,128)(2,1)}, u32[]{:S(2)}) copy-start(bf16[1,128,2048]{2,1,0:T(8,128)(2,1)} %param.5) | copy-start | bytes 1572868
  15.9 69.5 %copy-start = (s32[1,4096]{1,0:T(1,128)S(1)}, s32[1,4096]{1,0:T(1,128)}, u32[]{:S(2)}) copy-start(s32[1,4096]{1,0:T(1,128)} %sec_j_ref.1) | copy-start | bytes 49156
  92.6 19.7 %copy-start.2 = (f32[128,128]{1,0:T(8,128)S(1)}, f32[128,128]{1,0:T(8,128)}, u32[]{:S(2)}) copy-start(f32[128,128]{1,0:T(8,128)} %param.9) | copy-start | bytes 196612
  98.0 20.3 %collective-permute-start = (f32[128,128]{0,1:T(8,128)S(1)}, f32[128,128]{0,1:T(8,128)S(1)}, u32[]{:S(2)}, u32[]{:S(2)}) collective-permute-start(f32[128,128]{0,1:T(8,128)S(1)} %convolution_bitcast_fusion), channel_id=1, source_target_pairs={{0,1},{1,2},{2,3},{3,4},{4,5},{5,6},{6,7},{7,0},{8,9},{9,10},{10,1... | collective-permute-start | bytes 196616 | tf_op jit(solution)/shard_map/ppermute | solution.py:27
  99.5 20.2 %collective-permute-start.1 = (f32[128,128]{0,1:T(8,128)S(1)}, f32[128,128]{0,1:T(8,128)S(1)}, u32[]{:S(2)}, u32[]{:S(2)}) collective-permute-start(f32[128,128]{0,1:T(8,128)S(1)} %convolution_bitcast_fusion), channel_id=1, source_target_pairs={{0,2},{1,3},{2,4},{3,5},{4,6},{5,7},{6,0},{7,1},{8,10},{9,11},{10,... | collective-permute-start | bytes 196616 | tf_op jit(solution)/shard_map/ppermute | solution.py:27
  112.4 7.3 %collective-permute-start.2 = (f32[128,128]{0,1:T(8,128)S(1)}, f32[128,128]{0,1:T(8,128)S(1)}, u32[]{:S(2)}, u32[]{:S(2)}) collective-permute-start(f32[128,128]{0,1:T(8,128)S(1)} %convolution_bitcast_fusion), channel_id=1, source_target_pairs={{0,3},{1,4},{2,5},{3,6},{4,7},{5,0},{6,1},{7,2},{8,11},{9,12},{10,... | collective-permute-start | bytes 196616 | tf_op jit(solution)/shard_map/ppermute | solution.py:27
  114.5 6.5 %collective-permute-start.3 = (f32[128,128]{0,1:T(8,128)S(1)}, f32[128,128]{0,1:T(8,128)S(1)}, u32[]{:S(2)}, u32[]{:S(2)}) collective-permute-start(f32[128,128]{0,1:T(8,128)S(1)} %convolution_bitcast_fusion), channel_id=1, source_target_pairs={{0,4},{1,5},{2,6},{3,7},{4,0},{5,1},{6,2},{7,3},{8,12},{9,13},{10,... | collective-permute-start | bytes 196616 | tf_op jit(solution)/shard_map/ppermute | solution.py:27
  115.4 5.5 %collective-permute-start.4 = (f32[128,128]{0,1:T(8,128)S(1)}, f32[128,128]{0,1:T(8,128)S(1)}, u32[]{:S(2)}, u32[]{:S(2)}) collective-permute-start(f32[128,128]{0,1:T(8,128)S(1)} %convolution_bitcast_fusion), channel_id=1, source_target_pairs={{0,5},{1,6},{2,7},{3,0},{4,1},{5,2},{6,3},{7,4},{8,13},{9,14},{10,... | collective-permute-start | bytes 196616 | tf_op jit(solution)/shard_map/ppermute | solution.py:27
  118.3 4.3 %collective-permute-start.5 = (f32[128,128]{0,1:T(8,128)S(1)}, f32[128,128]{0,1:T(8,128)S(1)}, u32[]{:S(2)}, u32[]{:S(2)}) collective-permute-start(f32[128,128]{0,1:T(8,128)S(1)} %convolution_bitcast_fusion), channel_id=1, source_target_pairs={{0,6},{1,7},{2,0},{3,1},{4,2},{5,3},{6,4},{7,5},{8,14},{9,15},{10,... | collective-permute-start | bytes 196616 | tf_op jit(solution)/shard_map/ppermute | solution.py:27
  119.7 2.9 %collective-permute-start.6 = (f32[128,128]{0,1:T(8,128)S(1)}, f32[128,128]{0,1:T(8,128)S(1)}, u32[]{:S(2)}, u32[]{:S(2)}) collective-permute-start(f32[128,128]{0,1:T(8,128)S(1)} %convolution_bitcast_fusion), channel_id=1, source_target_pairs={{0,7},{1,0},{2,1},{3,2},{4,3},{5,4},{6,5},{7,6},{8,15},{9,8},{10,9... | collective-permute-start | bytes 196616 | tf_op jit(solution)/shard_map/ppermute | solution.py:27
  122.6 7.4 %collective-permute-start.7 = (f32[128,128]{0,1:T(8,128)S(1)}, f32[128,128]{0,1:T(8,128)S(1)}, u32[]{:S(2)}, u32[]{:S(2)}) collective-permute-start(f32[128,128]{0,1:T(8,128)S(1)} %add_add_fusion.1), channel_id=1, source_target_pairs={{0,8},{1,9},{2,10},{3,11},{4,12},{5,13},{6,14},{7,15},{8,16},{9,17... | collective-permute-start | bytes 196616 | tf_op jit(solution)/shard_map/ppermute | solution.py:27
  124.0 6.0 %collective-permute-start.8 = (f32[128,128]{0,1:T(8,128)S(1)}, f32[128,128]{0,1:T(8,128)S(1)}, u32[]{:S(2)}, u32[]{:S(2)}) collective-permute-start(f32[128,128]{0,1:T(8,128)S(1)} %add_add_fusion.1), channel_id=1, source_target_pairs={{0,16},{1,17},{2,18},{3,19},{4,20},{5,21},{6,22},{7,23},{8,24},{9,... | collective-permute-start | bytes 196616 | tf_op jit(solution)/shard_map/ppermute | solution.py:27
  125.7 4.9 %collective-permute-start.9 = (f32[128,128]{0,1:T(8,128)S(1)}, f32[128,128]{0,1:T(8,128)S(1)}, u32[]{:S(2)}, u32[]{:S(2)}) collective-permute-start(f32[128,128]{0,1:T(8,128)S(1)} %add_add_fusion.1), channel_id=1, source_target_pairs={{0,24},{1,25},{2,26},{3,27},{4,28},{5,29},{6,30},{7,31},{8,0},{9,1... | collective-permute-start | bytes 196616 | tf_op jit(solution)/shard_map/ppermute | solution.py:27
  131.9 6.2 %collective-permute-start.10 = (f32[128,128]{0,1:T(8,128)S(1)}, f32[128,128]{0,1:T(8,128)S(1)}, u32[]{:S(2)}, u32[]{:S(2)}) collective-permute-start(f32[128,128]{0,1:T(8,128)S(1)} %multiply_divide_fusion), channel_id=1, source_target_pairs={{0,32},{32,64},{64,96},{96,0},{1,33},{33,65},{65,97},{97,1},{2,34}... | collective-permute-start | bytes 196616 | tf_op jit(solution)/shard_map/ppermute | solution.py:39
  133.8 5.8 %collective-permute-start.11 = (f32[128,128]{0,1:T(8,128)S(1)}, f32[128,128]{0,1:T(8,128)S(1)}, u32[]{:S(2)}, u32[]{:S(2)}) collective-permute-start(f32[128,128]{0,1:T(8,128)S(1)} %multiply_divide_fusion), channel_id=1, source_target_pairs={{0,64},{32,96},{64,0},{96,32},{1,65},{33,97},{65,1},{97,33},{2,66}... | collective-permute-start | bytes 196616 | tf_op jit(solution)/shard_map/ppermute | solution.py:39
  136.4 4.3 %collective-permute-start.12 = (f32[128,128]{0,1:T(8,128)S(1)}, f32[128,128]{0,1:T(8,128)S(1)}, u32[]{:S(2)}, u32[]{:S(2)}) collective-permute-start(f32[128,128]{0,1:T(8,128)S(1)} %multiply_divide_fusion), channel_id=1, source_target_pairs={{0,96},{32,0},{64,32},{96,64},{1,97},{33,1},{65,33},{97,65},{2,98}... | collective-permute-start | bytes 196616 | tf_op jit(solution)/shard_map/ppermute | solution.py:39
Sparse Core Ops, SparseCore 0:
  10.2 75.1 all-gather.2

commit v15 on v13

--- a/solution.py
+++ b/solution.py
@@ -35,7 +35,7 @@
     me = lax.axis_index(axis)
     parts = [value]
     for shift in range(1, peers):
-        pairs = [(i, (i + shift) % peers) for i in range(peers)]
+        pairs = [(i, i + shift) for i in range(peers - shift)]
         parts.append(lax.ppermute(value, axis, pairs))
     stacked = jnp.stack(parts)
     order = (me - jnp.arange(peers)) % peers

time: 150 us -> 154 us (1.027)
  starting transfers between devices: 30.4 us -> 33.2 us
    ppermute x3, starting transfers between devices: 6.47 us -> 9.27 us  [gather_all(): parts.append(lax.ppermute(value, axis, pairs))]
  transfers between devices with their start and end apart: 11 -> 11, of which waited for: 10 -> 7; matrix products, arithmetic and copies ran while one was open for 11% -> 11% of each run, Pallas kernels for 0% -> 0%
where the time goes in v15:
time: 154 us; the launch traced here: 152 us
  waiting for transfers between devices  66.9 us (43%)
  starting transfers between devices  33.2 us (22%)
  between operations  18.1 us (12%)
  local copies, waits for them, and re-layouts  16.5 us (11%)
  Pallas kernels  7.17 us (5%)
  matrix products  7.12 us (5%)
  other arithmetic  3.51 us (2%)
    all_gather x1, waiting for transfers between devices, per_device(): theta_all = lax.all_gather(theta_loc, 'blk', axis=0, tiled=True)  57.8 us
    ppermute x7, starting transfers between devices, grouped_sum(): total = total + lax.ppermute(value, axis, pairs)  23.9 us
    transpose x1, local copies, waits for them, and re-layouts, masked_apply(): jnp.transpose(env_loc, (1, 0, 2))  11.3 us
    ppermute x3, starting transfers between devices, gather_all(): parts.append(lax.ppermute(value, axis, pairs))  9.27 us
    pallas_call x1, Pallas kernels, masked_apply(): pl.pallas_call(masked_apply_kernel, grid_spec=grid_spec, out_shape=jax.Sh...  7.17 us
    ppermute x7, waiting for transfers between devices, grouped_sum(): total = total + lax.ppermute(value, axis, pairs)  6.52 us
    dot_general x1, matrix products, per_device(): jnp.einsum('wpq,iwqc->ipc', ops_loc, applied, precision=lax.Precision.HIGH)  4.59 us
  transfers between devices with their start and end apart: 11, of which 7 were waited for; matrix products, arithmetic and copies ran while one was open for 11% of the time, Pallas kernels for 0%

profile of v15, /device:TPU:0, one launch (start us, length us, event | category | flops | bytes accessed | tf_op | source)
XLA Modules:
  0.0 152.5 jit_solution(5170402617842391865)
XLA Ops:
  9.1 2.7 %fusion.12 = (s32[]{:T(128)}, s32[]{:T(128)}) fusion(s32[1,4096]{1,0:T(1,128)} %sec_j_ref.1, s32[]{:T(128)} %bitcast, s32[]{:T(128)} %bitcast.2), kind=kLoop, calls=%fused_computation.29 | loop fusion | flops 24574 | bytes 16400 | tf_op jit(solution)/shard_map/reduce_sum | solution.py:68
  16.0 11.3 %copy.18 = bf16[128,8,4096]{2,1,0:T(8,128)(2,1)} copy(bf16[128,8,4096]{2,0,1:T(8,128)(2,1)} %bitcast.79) | data formatting | bytes 16777216 | tf_op jit(solution)/shard_map/transpose | solution.py:72
  27.6 57.8 %all-gather.3.cloned.1.call-done = bf16[1,4096,2048]{2,1,0:T(8,128)(2,1)} async-done(((bf16[1,128,2048]{2,1,0:T(8,128)(2,1)}), bf16[1,4096,2048]{2,1,0:T(8,128)(2,1)}) %all-gather.3.cloned.1.call-update) | async-done | bytes 16777232 | tf_op jit(solution)/shard_map/all_gather | solution.py:112
  85.4 7.2 %shard_map.68 = f32[1024,2048]{1,0:T(8,128)} custom-call(s32[2]{0:T(128)S(1)} %pad_add_fusion.span_ref, bf16[64,16,4096]{2,1,0:T(8,128)(2,1)} %bitcast.77, bf16[4096,2048]{1,0:T(8,128)(2,1)} %bitcast.78, s32[1,4096]{1,0:T(1,128)S(1)} %copy-done, s32[1024,1]{1,0:T(8,128)S(1)} %reshape_reshape.4.sec_i_ref), custom_call_target="tpu_custom_call" | custom-call | tf_op jit(solution)/shard_map/pallas_call | solution.py:89
  92.6 4.6 %fusion.2 = f32[128,16,128]{2,1,0:T(8,128)S(1)} fusion(f32[8,16,16,1]{1,0,2,3:T(8,128)S(1)} %copy.32, f32[1024,2048]{1,0:T(8,128)} %shard_map.68), kind=kOutput, calls=%fused_computation.3 | convolution fusion | flops 201326592 | bytes 9445376 | tf_op jit(solution)/shard_map/wpq,iwqc->ipc/dot_general | solution.py:115
  97.2 0.7 convolution_bitcast_fusion
  98.0 1.6 %collective-permute-start = (f32[128,128]{0,1:T(8,128)S(1)}, f32[128,128]{0,1:T(8,128)S(1)}, u32[]{:S(2)}, u32[]{:S(2)}) collective-permute-start(f32[128,128]{0,1:T(8,128)S(1)} %convolution_bitcast_fusion), channel_id=1, source_target_pairs={{0,1},{1,0},{2,3},{3,2},{4,5},{5,4},{6,7},{7,6},{8,9},{9,8},{10,11... | collective-permute-start | bytes 196616 | tf_op jit(solution)/shard_map/ppermute | solution.py:27
  99.7 0.8 collective-permute-done
  100.5 1.1 collective-permute-start.1
  101.6 4.2 %collective-permute-start.2 = (f32[128,128]{0,1:T(8,128)S(1)}, f32[128,128]{0,1:T(8,128)S(1)}, u32[]{:S(2)}, u32[]{:S(2)}) collective-permute-start(f32[128,128]{0,1:T(8,128)S(1)} %add.67), channel_id=1, source_target_pairs={{0,4},{1,5},{2,6},{3,7},{4,0},{5,1},{6,2},{7,3},{8,12},{9,13},{10,... | collective-permute-start | bytes 196616 | tf_op jit(solution)/shard_map/ppermute | solution.py:27
  105.8 1.4 collective-permute-start.3
  107.2 2.1 %collective-permute-done.2 = f32[128,128]{0,1:T(8,128)S(1)} collective-permute-done((f32[128,128]{0,1:T(8,128)S(1)}, f32[128,128]{0,1:T(8,128)S(1)}, u32[]{:S(2)}, u32[]{:S(2)}) %collective-permute-start.2) | collective-permute-done | bytes 65568 | tf_op jit(solution)/shard_map/ppermute | solution.py:27
  109.3 0.7 collective-permute-done.3
  110.1 12.6 %collective-permute-start.4 = (f32[128,128]{0,1:T(8,128)S(1)}, f32[128,128]{0,1:T(8,128)S(1)}, u32[]{:S(2)}, u32[]{:S(2)}) collective-permute-start(f32[128,128]{0,1:T(8,128)S(1)} %add_add_fusion.1), channel_id=1, source_target_pairs={{0,8},{1,9},{2,10},{3,11},{4,12},{5,13},{6,14},{7,15},{8,16},{9,17... | collective-permute-start | bytes 196616 | tf_op jit(solution)/shard_map/ppermute | solution.py:27
  122.7 1.5 collective-permute-start.5
  124.2 1.5 collective-permute-start.6
  125.7 2.8 %collective-permute-done.5 = f32[128,128]{0,1:T(8,128)S(1)} collective-permute-done((f32[128,128]{0,1:T(8,128)S(1)}, f32[128,128]{0,1:T(8,128)S(1)}, u32[]{:S(2)}, u32[]{:S(2)}) %collective-permute-start.5) | collective-permute-done | bytes 65568 | tf_op jit(solution)/shard_map/ppermute | solution.py:27
  129.8 2.6 %collective-permute-start.7 = (f32[128,128]{0,1:T(8,128)S(1)}, f32[128,128]{0,1:T(8,128)S(1)}, u32[]{:S(2)}, u32[]{:S(2)}) collective-permute-start(f32[128,128]{0,1:T(8,128)S(1)} %multiply_divide_fusion), channel_id=1, source_target_pairs={{0,32},{32,64},{64,96},{1,33},{33,65},{65,97},{2,34},{34,66},{66,9... | collective-permute-start | bytes 196616 | tf_op jit(solution)/shard_map/ppermute | solution.py:39
  132.4 5.4 %collective-permute-start.8 = (f32[128,128]{0,1:T(8,128)S(1)}, f32[128,128]{0,1:T(8,128)S(1)}, u32[]{:S(2)}, u32[]{:S(2)}) collective-permute-start(f32[128,128]{0,1:T(8,128)S(1)} %multiply_divide_fusion), channel_id=1, source_target_pairs={{0,64},{32,96},{1,65},{33,97},{2,66},{34,98},{3,67},{35,99},{4,68}... | collective-permute-start | bytes 196616 | tf_op jit(solution)/shard_map/ppermute | solution.py:39
  137.8 1.3 collective-permute-start.9
  139.7 1.3 collective-permute-done.9
  143.0 0.9 convolution_convert_fusion
  143.9 1.0 copy.29
  144.9 0.7 copy.30
  (44 shorter events, 6.5 us)
Async XLA Ops:
  7.2 78.3 %all-gather.3.cloned.1.call-start = ((), (), s32[]{:S(2)}) async-start(), calls=%async_computation | async-start | bytes 17301504 | tf_op jit(solution)/shard_map/all_gather | solution.py:112
  16.0 11.3 %copy-start.3 = (f32[1,8,16,16]{3,2,1,0:T(8,128)S(1)}, f32[1,8,16,16]{3,2,1,0:T(8,128)}, u32[]{:S(2)}) copy-start(f32[1,8,16,16]{3,2,1,0:T(8,128)} %param.8) | copy-start | bytes 24580
  16.0 11.4 %copy-start.1 = (bf16[1,128,2048]{2,1,0:T(8,128)(2,1)S(1)}, bf16[1,128,2048]{2,1,0:T(8,128)(2,1)}, u32[]{:S(2)}) copy-start(bf16[1,128,2048]{2,1,0:T(8,128)(2,1)} %param.5) | copy-start | bytes 1572868
  16.0 69.4 %copy-start = (s32[1,4096]{1,0:T(1,128)S(1)}, s32[1,4096]{1,0:T(1,128)}, u32[]{:S(2)}) copy-start(s32[1,4096]{1,0:T(1,128)} %sec_j_ref.1) | copy-start | bytes 49156
  92.6 7.0 %copy-start.2 = (f32[128,128]{1,0:T(8,128)S(1)}, f32[128,128]{1,0:T(8,128)}, u32[]{:S(2)}) copy-start(f32[128,128]{1,0:T(8,128)} %param.9) | copy-start | bytes 196612
  98.0 2.5 %collective-permute-start = (f32[128,128]{0,1:T(8,128)S(1)}, f32[128,128]{0,1:T(8,128)S(1)}, u32[]{:S(2)}, u32[]{:S(2)}) collective-permute-start(f32[128,128]{0,1:T(8,128)S(1)} %convolution_bitcast_fusion), channel_id=1, source_target_pairs={{0,1},{1,0},{2,3},{3,2},{4,5},{5,4},{6,7},{7,6},{8,9},{9,8},{10,11... | collective-permute-start | bytes 196616 | tf_op jit(solution)/shard_map/ppermute | solution.py:27
  100.5 6.7 %collective-permute-start.1 = (f32[128,128]{0,1:T(8,128)S(1)}, f32[128,128]{0,1:T(8,128)S(1)}, u32[]{:S(2)}, u32[]{:S(2)}) collective-permute-start(f32[128,128]{0,1:T(8,128)S(1)} %add.67), channel_id=1, source_target_pairs={{0,2},{1,3},{2,4},{3,5},{4,6},{5,7},{6,0},{7,1},{8,10},{9,11},{10,... | collective-permute-start | bytes 196616 | tf_op jit(solution)/shard_map/ppermute | solution.py:27
  101.6 7.7 %collective-permute-start.2 = (f32[128,128]{0,1:T(8,128)S(1)}, f32[128,128]{0,1:T(8,128)S(1)}, u32[]{:S(2)}, u32[]{:S(2)}) collective-permute-start(f32[128,128]{0,1:T(8,128)S(1)} %add.67), channel_id=1, source_target_pairs={{0,4},{1,5},{2,6},{3,7},{4,0},{5,1},{6,2},{7,3},{8,12},{9,13},{10,... | collective-permute-start | bytes 196616 | tf_op jit(solution)/shard_map/ppermute | solution.py:27
  105.8 4.3 %collective-permute-start.3 = (f32[128,128]{0,1:T(8,128)S(1)}, f32[128,128]{0,1:T(8,128)S(1)}, u32[]{:S(2)}, u32[]{:S(2)}) collective-permute-start(f32[128,128]{0,1:T(8,128)S(1)} %add.67), channel_id=1, source_target_pairs={{0,6},{1,7},{2,0},{3,1},{4,2},{5,3},{6,4},{7,5},{8,14},{9,15},{10,... | collective-permute-start | bytes 196616 | tf_op jit(solution)/shard_map/ppermute | solution.py:27
  110.1 15.6 %collective-permute-start.4 = (f32[128,128]{0,1:T(8,128)S(1)}, f32[128,128]{0,1:T(8,128)S(1)}, u32[]{:S(2)}, u32[]{:S(2)}) collective-permute-start(f32[128,128]{0,1:T(8,128)S(1)} %add_add_fusion.1), channel_id=1, source_target_pairs={{0,8},{1,9},{2,10},{3,11},{4,12},{5,13},{6,14},{7,15},{8,16},{9,17... | collective-permute-start | bytes 196616 | tf_op jit(solution)/shard_map/ppermute | solution.py:27
  122.7 5.8 %collective-permute-start.5 = (f32[128,128]{0,1:T(8,128)S(1)}, f32[128,128]{0,1:T(8,128)S(1)}, u32[]{:S(2)}, u32[]{:S(2)}) collective-permute-start(f32[128,128]{0,1:T(8,128)S(1)} %add_add_fusion.1), channel_id=1, source_target_pairs={{0,16},{1,17},{2,18},{3,19},{4,20},{5,21},{6,22},{7,23},{8,24},{9,... | collective-permute-start | bytes 196616 | tf_op jit(solution)/shard_map/ppermute | solution.py:27
  124.2 4.3 %collective-permute-start.6 = (f32[128,128]{0,1:T(8,128)S(1)}, f32[128,128]{0,1:T(8,128)S(1)}, u32[]{:S(2)}, u32[]{:S(2)}) collective-permute-start(f32[128,128]{0,1:T(8,128)S(1)} %add_add_fusion.1), channel_id=1, source_target_pairs={{0,24},{1,25},{2,26},{3,27},{4,28},{5,29},{6,30},{7,31},{8,0},{9,1... | collective-permute-start | bytes 196616 | tf_op jit(solution)/shard_map/ppermute | solution.py:27
  129.8 9.3 %collective-permute-start.7 = (f32[128,128]{0,1:T(8,128)S(1)}, f32[128,128]{0,1:T(8,128)S(1)}, u32[]{:S(2)}, u32[]{:S(2)}) collective-permute-start(f32[128,128]{0,1:T(8,128)S(1)} %multiply_divide_fusion), channel_id=1, source_target_pairs={{0,32},{32,64},{64,96},{1,33},{33,65},{65,97},{2,34},{34,66},{66,9... | collective-permute-start | bytes 196616 | tf_op jit(solution)/shard_map/ppermute | solution.py:39
  132.4 7.3 %collective-permute-start.8 = (f32[128,128]{0,1:T(8,128)S(1)}, f32[128,128]{0,1:T(8,128)S(1)}, u32[]{:S(2)}, u32[]{:S(2)}) collective-permute-start(f32[128,128]{0,1:T(8,128)S(1)} %multiply_divide_fusion), channel_id=1, source_target_pairs={{0,64},{32,96},{1,65},{33,97},{2,66},{34,98},{3,67},{35,99},{4,68}... | collective-permute-start | bytes 196616 | tf_op jit(solution)/shard_map/ppermute | solution.py:39
  137.8 3.2 %collective-permute-start.9 = (f32[128,128]{0,1:T(8,128)S(1)}, f32[128,128]{0,1:T(8,128)S(1)}, u32[]{:S(2)}, u32[]{:S(2)}) collective-permute-start(f32[128,128]{0,1:T(8,128)S(1)} %multiply_divide_fusion), channel_id=1, source_target_pairs={{0,96},{1,97},{2,98},{3,99},{4,100},{5,101},{6,102},{7,103},{8,104... | collective-permute-start | bytes 196616 | tf_op jit(solution)/shard_map/ppermute | solution.py:39
Sparse Core Ops, SparseCore 0:
  10.2 75.1 all-gather.2

commit v16 on v13

--- a/solution.py
+++ b/solution.py
@@ -42,15 +42,13 @@
     return jnp.zeros_like(stacked).at[order].set(stacked)
 
 
-def masked_apply_kernel(span_ref, env_ref, theta_ref, sec_j_ref, sec_i_ref, out_ref):
+def masked_apply_kernel(span_ref, env_ref, theta_ref, out_ref):
     step = pl.program_id(0)
 
     def product():
         env = env_ref[...]
         env = env.reshape(env.shape[0] * env.shape[1], env.shape[2])
-        same = sec_i_ref[...] == sec_j_ref[...]
-        masked = jnp.where(same, env, jnp.zeros_like(env))
-        return jnp.dot(masked, theta_ref[...], preferred_element_type=jnp.float32)
+        return jnp.dot(env, theta_ref[...], preferred_element_type=jnp.float32)
 
     @pl.when(step == 0)
     def _():
@@ -69,8 +67,9 @@
     last = jnp.sum((sec_all <= my_sec[-1]).astype(jnp.int32)) - 1
     span = jnp.stack([first // K_TILE, last // K_TILE]).astype(jnp.int32)
     group = 16
-    env_rows = jnp.transpose(env_loc, (1, 0, 2)).reshape(chain_w * rows_dev // group, group, depth)
-    sec_rows = jnp.repeat(my_sec, chain_w).reshape(chain_w * rows_dev, 1)
+    same = my_sec[:, None] == sec_all[None, :]
+    masked = jnp.where(same[None], env_loc, jnp.zeros_like(env_loc))
+    env_rows = jnp.transpose(masked, (1, 0, 2)).reshape(chain_w * rows_dev // group, group, depth)
 
     def tile_of(step, span_ref):
         return jnp.minimum(span_ref[0] + step, span_ref[1])
@@ -81,8 +80,6 @@
         in_specs=[
             pl.BlockSpec((chain_w * rows_dev // group, group, K_TILE), lambda k, s: (0, 0, tile_of(k, s))),
             pl.BlockSpec((K_TILE, width), lambda k, s: (tile_of(k, s), 0)),
-            pl.BlockSpec((1, K_TILE), lambda k, s: (0, tile_of(k, s))),
-            pl.BlockSpec((chain_w * rows_dev, 1), lambda k, s: (0, 0)),
         ],
         out_specs=pl.BlockSpec((chain_w * rows_dev, width), lambda k, s: (0, 0)),
     )
@@ -93,7 +90,7 @@
         compiler_params=pltpu.CompilerParams(
             dimension_semantics=("arbitrary",), vmem_limit_bytes=48 * 1024 * 1024
         ),
-    )(span, env_rows, theta_all, sec_all.reshape(1, depth), sec_rows)
+    )(span, env_rows, theta_all)
 
 
 def per_device(theta, left_env, sector_ids, local_ops, edge_env):

time: 150 us -> 151 us (level)
  other arithmetic: 3.51 us -> 13.4 us
  waiting for transfers between devices: 67.1 us -> 57.4 us
    all_gather x1, waiting for transfers between devices: 57.8 us -> 48.3 us  [per_device(): theta_all = lax.all_gather(theta_loc, 'blk', axis=0, tiled=True)]
    transpose x0 -> x1, other arithmetic: none -> 8.83 us  [masked_apply(): jnp.transpose(masked, (1, 0, 2))]
  transfers between devices with their start and end apart: 11 -> 11, of which waited for: 10 -> 10; matrix products, arithmetic and copies ran while one was open for 11% -> 17% of each run, Pallas kernels for 0% -> 0%
where the time goes in v16:
time: 151 us; the launch traced here: 150 us
  waiting for transfers between devices  57.4 us (38%)
  starting transfers between devices  30.3 us (20%)
  between operations  18.1 us (12%)
  local copies, waits for them, and re-layouts  16.2 us (11%)
  other arithmetic  13.4 us (9%)
  matrix products  7.1 us (5%)
  Pallas kernels  7.07 us (5%)
    all_gather x1, waiting for transfers between devices, per_device(): theta_all = lax.all_gather(theta_loc, 'blk', axis=0, tiled=True)  48.3 us
    ppermute x7, starting transfers between devices, grouped_sum(): total = total + lax.ppermute(value, axis, pairs)  23.8 us
    transpose x1, local copies, waits for them, and re-layouts, masked_apply(): jnp.transpose(masked, (1, 0, 2))  11.3 us
    transpose x1, other arithmetic, masked_apply(): jnp.transpose(masked, (1, 0, 2))  8.83 us
    pallas_call x1, Pallas kernels, masked_apply(): pl.pallas_call(masked_apply_kernel, grid_spec=grid_spec, out_shape=jax.Sh...  7.07 us
    ppermute x3, starting transfers between devices, gather_all(): parts.append(lax.ppermute(value, axis, pairs))  6.47 us
    ppermute x7, waiting for transfers between devices, grouped_sum(): total = total + lax.ppermute(value, axis, pairs)  5.73 us
    dot_general x1, matrix products, per_device(): jnp.einsum('wpq,iwqc->ipc', ops_loc, applied, precision=lax.Precision.HIGH)  4.59 us
  transfers between devices with their start and end apart: 11, of which 10 were waited for; matrix products, arithmetic and copies ran while one was open for 17% of the time, Pallas kernels for 0%

profile of v16, /device:TPU:0, one launch (start us, length us, event | category | flops | bytes accessed | tf_op | source)
XLA Modules:
  0.0 149.6 jit_solution(4749455981008976854)
XLA Ops:
  9.1 2.7 %convert_reduce_fusion.1 = (s32[]{:T(128)}, s32[]{:T(128)}) fusion(s32[4096]{0:T(1024)} %bitcast.86, s32[]{:T(128)} %bitcast.1, s32[]{:T(128)} %bitcast.3), kind=kLoop, calls=%fused_computation.31 | loop fusion | flops 24574 | bytes 16400 | tf_op jit(solution)/shard_map/reduce_sum | solution.py:66
  15.7 1.1 broadcast_compare_fusion
  16.7 8.8 %fusion.2 = bf16[128,8,4096]{2,0,1:T(8,128)(2,1)} fusion(bf16[1,8,128,4096]{3,2,1,0:T(8,128)(2,1)} %param.6, pred[128,4096]{1,0:T(8,128)(4,1)S(1)} %broadcast_compare_fusion), kind=kLoop, calls=%fused_computation.4 | loop fusion | flops 4194304 | bytes 17301504 | tf_op jit(solution)/shard_map/transpose | solution.py:72
  25.6 11.3 %copy.18 = bf16[128,8,4096]{2,1,0:T(8,128)(2,1)} copy(bf16[128,8,4096]{2,0,1:T(8,128)(2,1)} %fusion.2) | data formatting | bytes 16777216 | tf_op jit(solution)/shard_map/transpose | solution.py:72
  37.2 48.3 %all-gather.3.cloned.1.call-done = bf16[1,4096,2048]{2,1,0:T(8,128)(2,1)} async-done(((bf16[1,128,2048]{2,1,0:T(8,128)(2,1)}), bf16[1,4096,2048]{2,1,0:T(8,128)(2,1)}) %all-gather.3.cloned.1.call-update) | async-done | bytes 16777232 | tf_op jit(solution)/shard_map/all_gather | solution.py:109
  85.4 7.1 %shard_map.68 = f32[1024,2048]{1,0:T(8,128)} custom-call(s32[2]{0:T(128)S(1)} %pad_add_fusion.span_ref, bf16[64,16,4096]{2,1,0:T(8,128)(2,1)} %bitcast.81, bf16[4096,2048]{1,0:T(8,128)(2,1)} %bitcast.82), custom_call_target="tpu_custom_call" | custom-call | tf_op jit(solution)/shard_map/pallas_call | solution.py:86
  92.5 4.6 %fusion.3 = f32[128,16,128]{2,1,0:T(8,128)S(1)} fusion(f32[8,16,16,1]{1,0,2,3:T(8,128)S(1)} %copy.31, f32[1024,2048]{1,0:T(8,128)} %shard_map.68), kind=kOutput, calls=%fused_computation.5 | convolution fusion | flops 201326592 | bytes 9445376 | tf_op jit(solution)/shard_map/wpq,iwqc->ipc/dot_general | solution.py:112
  97.8 13.4 %collective-permute-start = (f32[128,128]{0,1:T(8,128)S(1)}, f32[128,128]{0,1:T(8,128)S(1)}, u32[]{:S(2)}, u32[]{:S(2)}) collective-permute-start(f32[128,128]{0,1:T(8,128)S(1)} %convolution_bitcast_fusion), channel_id=1, source_target_pairs={{0,1},{1,0},{2,3},{3,2},{4,5},{5,4},{6,7},{7,6},{8,9},{9,8},{10,11... | collective-permute-start | bytes 196616 | tf_op jit(solution)/shard_map/ppermute | solution.py:27
  111.4 0.8 collective-permute-done
  112.2 1.1 collective-permute-start.1
  113.3 2.9 %collective-permute-start.2 = (f32[128,128]{0,1:T(8,128)S(1)}, f32[128,128]{0,1:T(8,128)S(1)}, u32[]{:S(2)}, u32[]{:S(2)}) collective-permute-start(f32[128,128]{0,1:T(8,128)S(1)} %add.67), channel_id=1, source_target_pairs={{0,4},{1,5},{2,6},{3,7},{4,0},{5,1},{6,2},{7,3},{8,12},{9,13},{10,... | collective-permute-start | bytes 196616 | tf_op jit(solution)/shard_map/ppermute | solution.py:27
  116.2 1.4 collective-permute-start.3
  118.0 1.8 %collective-permute-done.2 = f32[128,128]{0,1:T(8,128)S(1)} collective-permute-done((f32[128,128]{0,1:T(8,128)S(1)}, f32[128,128]{0,1:T(8,128)S(1)}, u32[]{:S(2)}, u32[]{:S(2)}) %collective-permute-start.2) | collective-permute-done | bytes 65568 | tf_op jit(solution)/shard_map/ppermute | solution.py:27
  120.4 0.9 collective-permute-start.4
  121.4 1.6 %collective-permute-start.5 = (f32[128,128]{0,1:T(8,128)S(1)}, f32[128,128]{0,1:T(8,128)S(1)}, u32[]{:S(2)}, u32[]{:S(2)}) collective-permute-start(f32[128,128]{0,1:T(8,128)S(1)} %add_add_fusion.1), channel_id=1, source_target_pairs={{0,16},{1,17},{2,18},{3,19},{4,20},{5,21},{6,22},{7,23},{8,24},{9,... | collective-permute-start | bytes 196616 | tf_op jit(solution)/shard_map/ppermute | solution.py:27
  123.0 2.5 %collective-permute-start.6 = (f32[128,128]{0,1:T(8,128)S(1)}, f32[128,128]{0,1:T(8,128)S(1)}, u32[]{:S(2)}, u32[]{:S(2)}) collective-permute-start(f32[128,128]{0,1:T(8,128)S(1)} %add_add_fusion.1), channel_id=1, source_target_pairs={{0,24},{1,25},{2,26},{3,27},{4,28},{5,29},{6,30},{7,31},{8,0},{9,1... | collective-permute-start | bytes 196616 | tf_op jit(solution)/shard_map/ppermute | solution.py:27
  126.1 1.0 collective-permute-done.5
  128.9 2.8 %collective-permute-start.7 = (f32[128,128]{0,1:T(8,128)S(1)}, f32[128,128]{0,1:T(8,128)S(1)}, u32[]{:S(2)}, u32[]{:S(2)}) collective-permute-start(f32[128,128]{0,1:T(8,128)S(1)} %multiply_divide_fusion), channel_id=1, source_target_pairs={{0,32},{32,64},{64,96},{96,0},{1,33},{33,65},{65,97},{97,1},{2,34}... | collective-permute-start | bytes 196616 | tf_op jit(solution)/shard_map/ppermute | solution.py:39
  131.7 2.1 %collective-permute-start.8 = (f32[128,128]{0,1:T(8,128)S(1)}, f32[128,128]{0,1:T(8,128)S(1)}, u32[]{:S(2)}, u32[]{:S(2)}) collective-permute-start(f32[128,128]{0,1:T(8,128)S(1)} %multiply_divide_fusion), channel_id=1, source_target_pairs={{0,64},{32,96},{64,0},{96,32},{1,65},{33,97},{65,1},{97,33},{2,66}... | collective-permute-start | bytes 196616 | tf_op jit(solution)/shard_map/ppermute | solution.py:39
  133.8 1.5 %collective-permute-start.9 = (f32[128,128]{0,1:T(8,128)S(1)}, f32[128,128]{0,1:T(8,128)S(1)}, u32[]{:S(2)}, u32[]{:S(2)}) collective-permute-start(f32[128,128]{0,1:T(8,128)S(1)} %multiply_divide_fusion), channel_id=1, source_target_pairs={{0,96},{32,0},{64,32},{96,64},{1,97},{33,1},{65,33},{97,65},{2,98}... | collective-permute-start | bytes 196616 | tf_op jit(solution)/shard_map/ppermute | solution.py:39
  135.4 2.1 %collective-permute-done.8 = f32[128,128]{0,1:T(8,128)S(1)} collective-permute-done((f32[128,128]{0,1:T(8,128)S(1)}, f32[128,128]{0,1:T(8,128)S(1)}, u32[]{:S(2)}, u32[]{:S(2)}) %collective-permute-start.8) | collective-permute-done | bytes 65568 | tf_op jit(solution)/shard_map/ppermute | solution.py:39
  140.1 0.9 convolution_convert_fusion
  141.0 1.0 copy.28
  142.0 0.7 copy.29
  (42 shorter events, 9.1 us)
Async XLA Ops:
  7.2 78.3 %all-gather.3.cloned.1.call-start = ((), (), s32[]{:S(2)}) async-start(), calls=%async_computation | async-start | bytes 17301504 | tf_op jit(solution)/shard_map/all_gather | solution.py:109
  25.6 11.3 %copy-start.2 = (f32[1,8,16,16]{3,2,1,0:T(8,128)S(1)}, f32[1,8,16,16]{3,2,1,0:T(8,128)}, u32[]{:S(2)}) copy-start(f32[1,8,16,16]{3,2,1,0:T(8,128)} %param.8) | copy-start | bytes 24580
  25.6 11.4 %copy-start = (bf16[1,128,2048]{2,1,0:T(8,128)(2,1)S(1)}, bf16[1,128,2048]{2,1,0:T(8,128)(2,1)}, u32[]{:S(2)}) copy-start(bf16[1,128,2048]{2,1,0:T(8,128)(2,1)} %param.5) | copy-start | bytes 1572868
  92.5 18.8 %copy-start.1 = (f32[128,128]{1,0:T(8,128)S(1)}, f32[128,128]{1,0:T(8,128)}, u32[]{:S(2)}) copy-start(f32[128,128]{1,0:T(8,128)} %param.9) | copy-start | bytes 196612
  97.8 14.3 %collective-permute-start = (f32[128,128]{0,1:T(8,128)S(1)}, f32[128,128]{0,1:T(8,128)S(1)}, u32[]{:S(2)}, u32[]{:S(2)}) collective-permute-start(f32[128,128]{0,1:T(8,128)S(1)} %convolution_bitcast_fusion), channel_id=1, source_target_pairs={{0,1},{1,0},{2,3},{3,2},{4,5},{5,4},{6,7},{7,6},{8,9},{9,8},{10,11... | collective-permute-start | bytes 196616 | tf_op jit(solution)/shard_map/ppermute | solution.py:27
  112.2 5.8 %collective-permute-start.1 = (f32[128,128]{0,1:T(8,128)S(1)}, f32[128,128]{0,1:T(8,128)S(1)}, u32[]{:S(2)}, u32[]{:S(2)}) collective-permute-start(f32[128,128]{0,1:T(8,128)S(1)} %add.67), channel_id=1, source_target_pairs={{0,2},{1,3},{2,4},{3,5},{4,6},{5,7},{6,0},{7,1},{8,10},{9,11},{10,... | collective-permute-start | bytes 196616 | tf_op jit(solution)/shard_map/ppermute | solution.py:27
  113.3 6.5 %collective-permute-start.2 = (f32[128,128]{0,1:T(8,128)S(1)}, f32[128,128]{0,1:T(8,128)S(1)}, u32[]{:S(2)}, u32[]{:S(2)}) collective-permute-start(f32[128,128]{0,1:T(8,128)S(1)} %add.67), channel_id=1, source_target_pairs={{0,4},{1,5},{2,6},{3,7},{4,0},{5,1},{6,2},{7,3},{8,12},{9,13},{10,... | collective-permute-start | bytes 196616 | tf_op jit(solution)/shard_map/ppermute | solution.py:27
  116.2 4.3 %collective-permute-start.3 = (f32[128,128]{0,1:T(8,128)S(1)}, f32[128,128]{0,1:T(8,128)S(1)}, u32[]{:S(2)}, u32[]{:S(2)}) collective-permute-start(f32[128,128]{0,1:T(8,128)S(1)} %add.67), channel_id=1, source_target_pairs={{0,6},{1,7},{2,0},{3,1},{4,2},{5,3},{6,4},{7,5},{8,14},{9,15},{10,... | collective-permute-start | bytes 196616 | tf_op jit(solution)/shard_map/ppermute | solution.py:27
  120.4 5.7 %collective-permute-start.4 = (f32[128,128]{0,1:T(8,128)S(1)}, f32[128,128]{0,1:T(8,128)S(1)}, u32[]{:S(2)}, u32[]{:S(2)}) collective-permute-start(f32[128,128]{0,1:T(8,128)S(1)} %add_add_fusion.1), channel_id=1, source_target_pairs={{0,8},{1,9},{2,10},{3,11},{4,12},{5,13},{6,14},{7,15},{8,16},{9,17... | collective-permute-start | bytes 196616 | tf_op jit(solution)/shard_map/ppermute | solution.py:27
  121.4 5.8 %collective-permute-start.5 = (f32[128,128]{0,1:T(8,128)S(1)}, f32[128,128]{0,1:T(8,128)S(1)}, u32[]{:S(2)}, u32[]{:S(2)}) collective-permute-start(f32[128,128]{0,1:T(8,128)S(1)} %add_add_fusion.1), channel_id=1, source_target_pairs={{0,16},{1,17},{2,18},{3,19},{4,20},{5,21},{6,22},{7,23},{8,24},{9,... | collective-permute-start | bytes 196616 | tf_op jit(solution)/shard_map/ppermute | solution.py:27
  123.0 4.6 %collective-permute-start.6 = (f32[128,128]{0,1:T(8,128)S(1)}, f32[128,128]{0,1:T(8,128)S(1)}, u32[]{:S(2)}, u32[]{:S(2)}) collective-permute-start(f32[128,128]{0,1:T(8,128)S(1)} %add_add_fusion.1), channel_id=1, source_target_pairs={{0,24},{1,25},{2,26},{3,27},{4,28},{5,29},{6,30},{7,31},{8,0},{9,1... | collective-permute-start | bytes 196616 | tf_op jit(solution)/shard_map/ppermute | solution.py:27
  128.9 6.5 %collective-permute-start.7 = (f32[128,128]{0,1:T(8,128)S(1)}, f32[128,128]{0,1:T(8,128)S(1)}, u32[]{:S(2)}, u32[]{:S(2)}) collective-permute-start(f32[128,128]{0,1:T(8,128)S(1)} %multiply_divide_fusion), channel_id=1, source_target_pairs={{0,32},{32,64},{64,96},{96,0},{1,33},{33,65},{65,97},{97,1},{2,34}... | collective-permute-start | bytes 196616 | tf_op jit(solution)/shard_map/ppermute | solution.py:39
  131.7 5.8 %collective-permute-start.8 = (f32[128,128]{0,1:T(8,128)S(1)}, f32[128,128]{0,1:T(8,128)S(1)}, u32[]{:S(2)}, u32[]{:S(2)}) collective-permute-start(f32[128,128]{0,1:T(8,128)S(1)} %multiply_divide_fusion), channel_id=1, source_target_pairs={{0,64},{32,96},{64,0},{96,32},{1,65},{33,97},{65,1},{97,33},{2,66}... | collective-permute-start | bytes 196616 | tf_op jit(solution)/shard_map/ppermute | solution.py:39
  133.8 4.3 %collective-permute-start.9 = (f32[128,128]{0,1:T(8,128)S(1)}, f32[128,128]{0,1:T(8,128)S(1)}, u32[]{:S(2)}, u32[]{:S(2)}) collective-permute-start(f32[128,128]{0,1:T(8,128)S(1)} %multiply_divide_fusion), channel_id=1, source_target_pairs={{0,96},{32,0},{64,32},{96,64},{1,97},{33,1},{65,33},{97,65},{2,98}... | collective-permute-start | bytes 196616 | tf_op jit(solution)/shard_map/ppermute | solution.py:39
Sparse Core Ops, SparseCore 0:
  10.2 75.1 all-gather.2

commit v17 on v13

--- a/solution.py
+++ b/solution.py
@@ -32,14 +32,11 @@
 
 def gather_all(value, axis):
     peers = lax.axis_size(axis)
-    me = lax.axis_index(axis)
     parts = [value]
     for shift in range(1, peers):
         pairs = [(i, (i + shift) % peers) for i in range(peers)]
         parts.append(lax.ppermute(value, axis, pairs))
-    stacked = jnp.stack(parts)
-    order = (me - jnp.arange(peers)) % peers
-    return jnp.zeros_like(stacked).at[order].set(stacked)
+    return jnp.stack(parts)
 
 
 def masked_apply_kernel(span_ref, env_ref, theta_ref, sec_j_ref, sec_i_ref, out_ref):
@@ -124,14 +121,15 @@
         * jnp.sqrt(jnp.float32(cols))
         / jnp.sqrt(jnp.sum(intersection * intersection) + 1e-06)
     )
-    transfers = gather_all(transfer, "sect")
+    received = gather_all(transfer, "sect")
     sect_no = lax.axis_index("sect")
-    prefix = [edge_env]
-    for step_no in range(lax.axis_size("sect")):
-        prefix.append(matprod(prefix[-1], transfers[step_no]))
-    prefix = jnp.stack(prefix)
-    incoming = prefix[sect_no]
-    outgoing = prefix[sect_no + 1]
+    peers = lax.axis_size("sect")
+    incoming = edge_env
+    for step_no in range(peers - 1):
+        factor = received[(sect_no - step_no) % peers]
+        extended = matprod(incoming, factor)
+        incoming = jnp.where(step_no < sect_no, extended, incoming)
+    outgoing = matprod(incoming, transfer)
     result = jnp.einsum("ipc,cd->ipd", acted, incoming, precision=lax.Precision.HIGH)
     updated = result.reshape(1, rows_dev, width).astype(jnp.bfloat16)
     return (updated, outgoing[None])

time: 150 us -> 150 us (level)
  starting transfers between devices: 30.4 us -> 26.2 us
  waiting for transfers between devices: 67.1 us -> 70 us
  local copies, waits for them, and re-layouts: 16.5 us -> 14.7 us
    ppermute x7, starting transfers between devices: 23.9 us -> 21.1 us  [grouped_sum(): total = total + lax.ppermute(value, axis, pairs)]
    ppermute x7, waiting for transfers between devices: 5.73 us -> 8.5 us  [grouped_sum(): total = total + lax.ppermute(value, axis, pairs)]
  transfers between devices with their start and end apart: 11 -> 11, of which waited for: 10 -> 9; matrix products, arithmetic and copies ran while one was open for 11% -> 11% of each run, Pallas kernels for 0% -> 0%
where the time goes in v17:
time: 150 us; the launch traced here: 149 us
  waiting for transfers between devices  70 us (47%)
  starting transfers between devices  26.2 us (17%)
  between operations  18.1 us (12%)
  local copies, waits for them, and re-layouts  14.7 us (10%)
  Pallas kernels  8.46 us (6%)
  matrix products  7.64 us (5%)
  other arithmetic  3.51 us (2%)
    all_gather x1, waiting for transfers between devices, per_device(): theta_all = lax.all_gather(theta_loc, 'blk', axis=0, tiled=True)  57.8 us
    ppermute x7, starting transfers between devices, grouped_sum(): total = total + lax.ppermute(value, axis, pairs)  21.1 us
    transpose x1, local copies, waits for them, and re-layouts, masked_apply(): jnp.transpose(env_loc, (1, 0, 2))  11.2 us
    ppermute x7, waiting for transfers between devices, grouped_sum(): total = total + lax.ppermute(value, axis, pairs)  8.5 us
    pallas_call x1, Pallas kernels, masked_apply(): pl.pallas_call(masked_apply_kernel, grid_spec=grid_spec, out_shape=jax.Sh...  8.46 us
    ppermute x3, starting transfers between devices, gather_all(): parts.append(lax.ppermute(value, axis, pairs))  5.08 us
    dot_general x1, matrix products, per_device(): jnp.einsum('wpq,iwqc->ipc', ops_loc, applied, precision=lax.Precision.HIGH)  4.59 us
  transfers between devices with their start and end apart: 11, of which 9 were waited for; matrix products, arithmetic and copies ran while one was open for 11% of the time, Pallas kernels for 0%

profile of v17, /device:TPU:0, one launch (start us, length us, event | category | flops | bytes accessed | tf_op | source)
XLA Modules:
  0.0 148.6 jit_solution(10957563698674561549)
XLA Ops:
  7.2 0.7 all-gather.3.cloned.1.call-update
  9.1 2.7 %fusion.14 = (s32[]{:T(128)}, s32[]{:T(128)}) fusion(s32[1,4096]{1,0:T(1,128)} %sec_j_ref.1, s32[]{:T(128)} %bitcast, s32[]{:T(128)} %bitcast.2), kind=kLoop, calls=%fused_computation.25 | loop fusion | flops 24574 | bytes 16400 | tf_op jit(solution)/shard_map/reduce_sum | solution.py:65
  16.1 11.2 %copy.16 = bf16[128,8,4096]{2,1,0:T(8,128)(2,1)} copy(bf16[128,8,4096]{2,0,1:T(8,128)(2,1)} %bitcast.64) | data formatting | bytes 16777216 | tf_op jit(solution)/shard_map/transpose | solution.py:69
  27.6 57.8 %all-gather.3.cloned.1.call-done = bf16[1,4096,2048]{2,1,0:T(8,128)(2,1)} async-done(((bf16[1,128,2048]{2,1,0:T(8,128)(2,1)}), bf16[1,4096,2048]{2,1,0:T(8,128)(2,1)}) %all-gather.3.cloned.1.call-update) | async-done | bytes 16777232 | tf_op jit(solution)/shard_map/all_gather | solution.py:109
  85.4 8.5 %shard_map.68 = f32[1024,2048]{1,0:T(8,128)} custom-call(s32[2]{0:T(128)S(1)} %pad_add_fusion.span_ref, bf16[64,16,4096]{2,1,0:T(8,128)(2,1)} %bitcast.62, bf16[4096,2048]{1,0:T(8,128)(2,1)} %bitcast.63, s32[1,4096]{1,0:T(1,128)S(1)} %copy-done, s32[1024,1]{1,0:T(8,128)S(1)} %reshape_reshape.4.sec_i_ref), custom_call_target="tpu_custom_call" | custom-call | tf_op jit(solution)/shard_map/pallas_call | solution.py:86
  93.9 4.6 %fusion.2 = f32[128,16,128]{2,1,0:T(8,128)S(1)} fusion(f32[8,16,16,1]{1,0,2,3:T(8,128)S(1)} %copy.27, f32[1024,2048]{1,0:T(8,128)} %shard_map.68), kind=kOutput, calls=%fused_computation.2 | convolution fusion | flops 201326592 | bytes 9445376 | tf_op jit(solution)/shard_map/wpq,iwqc->ipc/dot_general | solution.py:112
  98.5 0.7 convolution_bitcast_fusion
  99.6 1.0 collective-permute-done
  100.6 1.0 collective-permute-start.1
  101.6 16.0 %collective-permute-start.2 = (f32[128,128]{0,1:T(8,128)S(1)}, f32[128,128]{0,1:T(8,128)S(1)}, u32[]{:S(2)}, u32[]{:S(2)}) collective-permute-start(f32[128,128]{0,1:T(8,128)S(1)} %add.52), channel_id=1, source_target_pairs={{0,4},{1,5},{2,6},{3,7},{4,0},{5,1},{6,2},{7,3},{8,12},{9,13},{10,... | collective-permute-start | bytes 196616 | tf_op jit(solution)/shard_map/ppermute | solution.py:27
  117.6 0.9 collective-permute-done.1
  118.6 2.6 %collective-permute-done.2 = f32[128,128]{0,1:T(8,128)S(1)} collective-permute-done((f32[128,128]{0,1:T(8,128)S(1)}, f32[128,128]{0,1:T(8,128)S(1)}, u32[]{:S(2)}, u32[]{:S(2)}) %collective-permute-start.2) | collective-permute-done | bytes 65568 | tf_op jit(solution)/shard_map/ppermute | solution.py:27
  121.1 0.7 collective-permute-done.3
  122.0 2.2 %collective-permute-start.5 = (f32[128,128]{0,1:T(8,128)S(1)}, f32[128,128]{0,1:T(8,128)S(1)}, u32[]{:S(2)}, u32[]{:S(2)}) collective-permute-start(f32[128,128]{0,1:T(8,128)S(1)} %add_add_fusion.1), channel_id=1, source_target_pairs={{0,16},{1,17},{2,18},{3,19},{4,20},{5,21},{6,22},{7,23},{8,24},{9,... | collective-permute-start | bytes 196616 | tf_op jit(solution)/shard_map/ppermute | solution.py:27
  124.2 1.5 collective-permute-start.6
  125.8 2.4 %collective-permute-done.4 = f32[128,128]{0,1:T(8,128)S(1)} collective-permute-done((f32[128,128]{0,1:T(8,128)S(1)}, f32[128,128]{0,1:T(8,128)S(1)}, u32[]{:S(2)}, u32[]{:S(2)}) %collective-permute-start.4) | collective-permute-done | bytes 65568 | tf_op jit(solution)/shard_map/ppermute | solution.py:27
  128.1 0.9 collective-permute-done.6
  130.3 2.3 %collective-permute-start.7 = (f32[128,128]{0,1:T(8,128)S(1)}, f32[128,128]{0,1:T(8,128)S(1)}, u32[]{:S(2)}, u32[]{:S(2)}) collective-permute-start(f32[128,128]{0,1:T(8,128)S(1)} %multiply_divide_fusion), channel_id=1, source_target_pairs={{0,32},{32,64},{64,96},{96,0},{1,33},{33,65},{65,97},{97,1},{2,34}... | collective-permute-start | bytes 196616 | tf_op jit(solution)/shard_map/ppermute | solution.py:38
  132.6 2.8 %collective-permute-start.9 = (f32[128,128]{0,1:T(8,128)S(1)}, f32[128,128]{0,1:T(8,128)S(1)}, u32[]{:S(2)}, u32[]{:S(2)}) collective-permute-start(f32[128,128]{0,1:T(8,128)S(1)} %multiply_divide_fusion), channel_id=1, source_target_pairs={{0,96},{32,0},{64,32},{96,64},{1,97},{33,1},{65,33},{97,65},{2,98}... | collective-permute-start | bytes 196616 | tf_op jit(solution)/shard_map/ppermute | solution.py:38
  135.4 0.7 collective-permute-done.7
  136.1 2.3 %collective-permute-done.8 = f32[128,128]{0,1:T(8,128)S(1)} collective-permute-done((f32[128,128]{0,1:T(8,128)S(1)}, f32[128,128]{0,1:T(8,128)S(1)}, u32[]{:S(2)}, u32[]{:S(2)}) %collective-permute-start.8) | collective-permute-done | bytes 65568 | tf_op jit(solution)/shard_map/ppermute | solution.py:38
  139.0 0.9 convolution_bitcast_fusion.1
  139.9 0.9 convolution_convert_fusion
  140.8 1.0 copy.25
  (33 shorter events, 4.3 us)
Async XLA Ops:
  7.2 78.3 %all-gather.3.cloned.1.call-start = ((), (), s32[]{:S(2)}) async-start(), calls=%async_computation | async-start | bytes 17301504 | tf_op jit(solution)/shard_map/all_gather | solution.py:109
  16.0 11.3 %copy-start.3 = (f32[1,8,16,16]{3,2,1,0:T(8,128)S(1)}, f32[1,8,16,16]{3,2,1,0:T(8,128)}, u32[]{:S(2)}) copy-start(f32[1,8,16,16]{3,2,1,0:T(8,128)} %param.8) | copy-start | bytes 24580
  16.1 11.4 %copy-start.1 = (bf16[1,128,2048]{2,1,0:T(8,128)(2,1)S(1)}, bf16[1,128,2048]{2,1,0:T(8,128)(2,1)}, u32[]{:S(2)}) copy-start(bf16[1,128,2048]{2,1,0:T(8,128)(2,1)} %param.5) | copy-start | bytes 1572868
  16.1 69.4 %copy-start = (s32[1,4096]{1,0:T(1,128)S(1)}, s32[1,4096]{1,0:T(1,128)}, u32[]{:S(2)}) copy-start(s32[1,4096]{1,0:T(1,128)} %sec_j_ref.1) | copy-start | bytes 49156
  93.9 31.8 %copy-start.2 = (f32[128,128]{1,0:T(8,128)S(1)}, f32[128,128]{1,0:T(8,128)}, u32[]{:S(2)}) copy-start(f32[128,128]{1,0:T(8,128)} %param.9) | copy-start | bytes 196612
  99.2 1.3 collective-permute-start
  100.6 18.0 %collective-permute-start.1 = (f32[128,128]{0,1:T(8,128)S(1)}, f32[128,128]{0,1:T(8,128)S(1)}, u32[]{:S(2)}, u32[]{:S(2)}) collective-permute-start(f32[128,128]{0,1:T(8,128)S(1)} %add.52), channel_id=1, source_target_pairs={{0,2},{1,3},{2,4},{3,5},{4,6},{5,7},{6,0},{7,1},{8,10},{9,11},{10,... | collective-permute-start | bytes 196616 | tf_op jit(solution)/shard_map/ppermute | solution.py:27
  101.6 19.5 %collective-permute-start.2 = (f32[128,128]{0,1:T(8,128)S(1)}, f32[128,128]{0,1:T(8,128)S(1)}, u32[]{:S(2)}, u32[]{:S(2)}) collective-permute-start(f32[128,128]{0,1:T(8,128)S(1)} %add.52), channel_id=1, source_target_pairs={{0,4},{1,5},{2,6},{3,7},{4,0},{5,1},{6,2},{7,3},{8,12},{9,13},{10,... | collective-permute-start | bytes 196616 | tf_op jit(solution)/shard_map/ppermute | solution.py:27
  117.6 4.3 %collective-permute-start.3 = (f32[128,128]{0,1:T(8,128)S(1)}, f32[128,128]{0,1:T(8,128)S(1)}, u32[]{:S(2)}, u32[]{:S(2)}) collective-permute-start(f32[128,128]{0,1:T(8,128)S(1)} %add.52), channel_id=1, source_target_pairs={{0,6},{1,7},{2,0},{3,1},{4,2},{5,3},{6,4},{7,5},{8,14},{9,15},{10,... | collective-permute-start | bytes 196616 | tf_op jit(solution)/shard_map/ppermute | solution.py:27
  121.9 6.2 %collective-permute-start.4 = (f32[128,128]{0,1:T(8,128)S(1)}, f32[128,128]{0,1:T(8,128)S(1)}, u32[]{:S(2)}, u32[]{:S(2)}) collective-permute-start(f32[128,128]{0,1:T(8,128)S(1)} %add_add_fusion.1), channel_id=1, source_target_pairs={{0,8},{1,9},{2,10},{3,11},{4,12},{5,13},{6,14},{7,15},{8,16},{9,17... | collective-permute-start | bytes 196616 | tf_op jit(solution)/shard_map/ppermute | solution.py:27
  122.0 6.2 %collective-permute-start.5 = (f32[128,128]{0,1:T(8,128)S(1)}, f32[128,128]{0,1:T(8,128)S(1)}, u32[]{:S(2)}, u32[]{:S(2)}) collective-permute-start(f32[128,128]{0,1:T(8,128)S(1)} %add_add_fusion.1), channel_id=1, source_target_pairs={{0,16},{1,17},{2,18},{3,19},{4,20},{5,21},{6,22},{7,23},{8,24},{9,... | collective-permute-start | bytes 196616 | tf_op jit(solution)/shard_map/ppermute | solution.py:27
  124.2 4.8 %collective-permute-start.6 = (f32[128,128]{0,1:T(8,128)S(1)}, f32[128,128]{0,1:T(8,128)S(1)}, u32[]{:S(2)}, u32[]{:S(2)}) collective-permute-start(f32[128,128]{0,1:T(8,128)S(1)} %add_add_fusion.1), channel_id=1, source_target_pairs={{0,24},{1,25},{2,26},{3,27},{4,28},{5,29},{6,30},{7,31},{8,0},{9,1... | collective-permute-start | bytes 196616 | tf_op jit(solution)/shard_map/ppermute | solution.py:27
  130.3 5.8 %collective-permute-start.7 = (f32[128,128]{0,1:T(8,128)S(1)}, f32[128,128]{0,1:T(8,128)S(1)}, u32[]{:S(2)}, u32[]{:S(2)}) collective-permute-start(f32[128,128]{0,1:T(8,128)S(1)} %multiply_divide_fusion), channel_id=1, source_target_pairs={{0,32},{32,64},{64,96},{96,0},{1,33},{33,65},{65,97},{97,1},{2,34}... | collective-permute-start | bytes 196616 | tf_op jit(solution)/shard_map/ppermute | solution.py:38
  132.6 5.8 %collective-permute-start.8 = (f32[128,128]{0,1:T(8,128)S(1)}, f32[128,128]{0,1:T(8,128)S(1)}, u32[]{:S(2)}, u32[]{:S(2)}) collective-permute-start(f32[128,128]{0,1:T(8,128)S(1)} %multiply_divide_fusion), channel_id=1, source_target_pairs={{0,64},{32,96},{64,0},{96,32},{1,65},{33,97},{65,1},{97,33},{2,66}... | collective-permute-start | bytes 196616 | tf_op jit(solution)/shard_map/ppermute | solution.py:38
  132.6 5.8 %collective-permute-start.9 = (f32[128,128]{0,1:T(8,128)S(1)}, f32[128,128]{0,1:T(8,128)S(1)}, u32[]{:S(2)}, u32[]{:S(2)}) collective-permute-start(f32[128,128]{0,1:T(8,128)S(1)} %multiply_divide_fusion), channel_id=1, source_target_pairs={{0,96},{32,0},{64,32},{96,64},{1,97},{33,1},{65,33},{97,65},{2,98}... | collective-permute-start | bytes 196616 | tf_op jit(solution)/shard_map/ppermute | solution.py:38
Sparse Core Ops, SparseCore 0:
  10.2 75.1 all-gather.2

commit v18 on v17

--- a/solution.py
+++ b/solution.py
@@ -130,8 +130,8 @@
         extended = matprod(incoming, factor)
         incoming = jnp.where(step_no < sect_no, extended, incoming)
     outgoing = matprod(incoming, transfer)
-    result = jnp.einsum("ipc,cd->ipd", acted, incoming, precision=lax.Precision.HIGH)
-    updated = result.reshape(1, rows_dev, width).astype(jnp.bfloat16)
+    result = jnp.dot(acted.reshape(rows_dev * phys, cols), incoming, precision=lax.Precision.HIGH)
+    updated = result.astype(jnp.bfloat16).reshape(1, rows_dev, width)
     return (updated, outgoing[None])
 
 

time: 150 us -> 150 us (level)
  starting transfers between devices: 26.2 us -> 31.8 us
  waiting for transfers between devices: 70 us -> 65.9 us
    ppermute x7, starting transfers between devices: 21.1 us -> 24.2 us  [grouped_sum(): total = total + lax.ppermute(value, axis, pairs)]
    ppermute x7, waiting for transfers between devices: 8.5 us -> 5.58 us  [grouped_sum(): total = total + lax.ppermute(value, axis, pairs)]
    ppermute x3, starting transfers between devices: 5.08 us -> 7.62 us  [gather_all(): parts.append(lax.ppermute(value, axis, pairs))]
where the time goes in v18:
time: 150 us; the launch traced here: 149 us
  waiting for transfers between devices  65.9 us (44%)
  starting transfers between devices  31.8 us (21%)
  between operations  18.1 us (12%)
  local copies, waits for them, and re-layouts  14.7 us (10%)
  matrix products  7.38 us (5%)
  Pallas kernels  7.16 us (5%)
  other arithmetic  3.51 us (2%)
    all_gather x1, waiting for transfers between devices, per_device(): theta_all = lax.all_gather(theta_loc, 'blk', axis=0, tiled=True)  57.8 us
    ppermute x7, starting transfers between devices, grouped_sum(): total = total + lax.ppermute(value, axis, pairs)  24.2 us
    transpose x1, local copies, waits for them, and re-layouts, masked_apply(): jnp.transpose(env_loc, (1, 0, 2))  11.2 us
    ppermute x3, starting transfers between devices, gather_all(): parts.append(lax.ppermute(value, axis, pairs))  7.62 us
    pallas_call x1, Pallas kernels, masked_apply(): pl.pallas_call(masked_apply_kernel, grid_spec=grid_spec, out_shape=jax.Sh...  7.16 us
    ppermute x7, waiting for transfers between devices, grouped_sum(): total = total + lax.ppermute(value, axis, pairs)  5.58 us
    dot_general x1, matrix products, per_device(): jnp.einsum('wpq,iwqc->ipc', ops_loc, applied, precision=lax.Precision.HIGH)  4.59 us
  transfers between devices with their start and end apart: 11, of which 9 were waited for; matrix products, arithmetic and copies ran while one was open for 11% of the time, Pallas kernels for 0%

profile of v18, /device:TPU:0, one launch (start us, length us, event | category | flops | bytes accessed | tf_op | source)
XLA Modules:
  0.0 148.7 jit_solution(9650854357865838242)
XLA Ops:
  7.2 0.7 all-gather.3.cloned.1.call-update
  9.1 2.7 %fusion.10 = (s32[]{:T(128)}, s32[]{:T(128)}) fusion(s32[1,4096]{1,0:T(1,128)} %sec_j_ref.1, s32[]{:T(128)} %bitcast, s32[]{:T(128)} %bitcast.2), kind=kLoop, calls=%fused_computation.23 | loop fusion | flops 24574 | bytes 16400 | tf_op jit(solution)/shard_map/reduce_sum | solution.py:65
  15.1 0.7 fusion.26
  16.1 11.2 %copy.14 = bf16[128,8,4096]{2,1,0:T(8,128)(2,1)} copy(bf16[128,8,4096]{2,0,1:T(8,128)(2,1)} %bitcast.62) | data formatting | bytes 16777216 | tf_op jit(solution)/shard_map/transpose | solution.py:69
  27.6 57.8 %all-gather.3.cloned.1.call-done = bf16[1,4096,2048]{2,1,0:T(8,128)(2,1)} async-done(((bf16[1,128,2048]{2,1,0:T(8,128)(2,1)}), bf16[1,4096,2048]{2,1,0:T(8,128)(2,1)}) %all-gather.3.cloned.1.call-update) | async-done | bytes 16777232 | tf_op jit(solution)/shard_map/all_gather | solution.py:109
  85.4 7.2 %shard_map.68 = f32[1024,2048]{1,0:T(8,128)} custom-call(s32[2]{0:T(128)S(1)} %pad_add_fusion.span_ref, bf16[64,16,4096]{2,1,0:T(8,128)(2,1)} %bitcast.60, bf16[4096,2048]{1,0:T(8,128)(2,1)} %bitcast.61, s32[1,4096]{1,0:T(1,128)S(1)} %copy-done, s32[1024,1]{1,0:T(8,128)S(1)} %reshape_reshape.4.sec_i_ref), custom_call_target="tpu_custom_call" | custom-call | tf_op jit(solution)/shard_map/pallas_call | solution.py:86
  92.6 4.6 %fusion = f32[128,128,16,1]{1,2,3,0:T(8,128)S(1)} fusion(f32[8,16,16,1]{1,0,2,3:T(8,128)S(1)} %copy.23, f32[1024,2048]{1,0:T(8,128)} %shard_map.68), kind=kOutput, calls=%fused_computation | convolution fusion | flops 201326592 | bytes 9445376 | tf_op jit(solution)/shard_map/wpq,iwqc->ipc/dot_general | solution.py:112
  97.2 0.7 convolution_bitcast_fusion
  97.9 1.6 %collective-permute-start = (f32[128,128]{0,1:T(8,128)S(1)}, f32[128,128]{0,1:T(8,128)S(1)}, u32[]{:S(2)}, u32[]{:S(2)}) collective-permute-start(f32[128,128]{0,1:T(8,128)S(1)} %convolution_bitcast_fusion), channel_id=1, source_target_pairs={{0,1},{1,0},{2,3},{3,2},{4,5},{5,4},{6,7},{7,6},{8,9},{9,8},{10,11... | collective-permute-start | bytes 196616 | tf_op jit(solution)/shard_map/ppermute | solution.py:27
  99.6 0.9 collective-permute-done
  100.5 12.9 %collective-permute-start.1 = (f32[128,128]{0,1:T(8,128)S(1)}, f32[128,128]{0,1:T(8,128)S(1)}, u32[]{:S(2)}, u32[]{:S(2)}) collective-permute-start(f32[128,128]{0,1:T(8,128)S(1)} %add.52), channel_id=1, source_target_pairs={{0,2},{1,3},{2,4},{3,5},{4,6},{5,7},{6,0},{7,1},{8,10},{9,11},{10,... | collective-permute-start | bytes 196616 | tf_op jit(solution)/shard_map/ppermute | solution.py:27
  113.3 3.0 %collective-permute-start.2 = (f32[128,128]{0,1:T(8,128)S(1)}, f32[128,128]{0,1:T(8,128)S(1)}, u32[]{:S(2)}, u32[]{:S(2)}) collective-permute-start(f32[128,128]{0,1:T(8,128)S(1)} %add.52), channel_id=1, source_target_pairs={{0,4},{1,5},{2,6},{3,7},{4,0},{5,1},{6,2},{7,3},{8,12},{9,13},{10,... | collective-permute-start | bytes 196616 | tf_op jit(solution)/shard_map/ppermute | solution.py:27
  116.3 1.4 collective-permute-start.3
  117.7 2.2 %collective-permute-done.2 = f32[128,128]{0,1:T(8,128)S(1)} collective-permute-done((f32[128,128]{0,1:T(8,128)S(1)}, f32[128,128]{0,1:T(8,128)S(1)}, u32[]{:S(2)}, u32[]{:S(2)}) %collective-permute-start.2) | collective-permute-done | bytes 65568 | tf_op jit(solution)/shard_map/ppermute | solution.py:27
  120.6 0.9 collective-permute-start.4
  121.5 1.9 %collective-permute-start.5 = (f32[128,128]{0,1:T(8,128)S(1)}, f32[128,128]{0,1:T(8,128)S(1)}, u32[]{:S(2)}, u32[]{:S(2)}) collective-permute-start(f32[128,128]{0,1:T(8,128)S(1)} %add_add_fusion.1), channel_id=1, source_target_pairs={{0,16},{1,17},{2,18},{3,19},{4,20},{5,21},{6,22},{7,23},{8,24},{9,... | collective-permute-start | bytes 196616 | tf_op jit(solution)/shard_map/ppermute | solution.py:27
  123.4 2.5 %collective-permute-start.6 = (f32[128,128]{0,1:T(8,128)S(1)}, f32[128,128]{0,1:T(8,128)S(1)}, u32[]{:S(2)}, u32[]{:S(2)}) collective-permute-start(f32[128,128]{0,1:T(8,128)S(1)} %add_add_fusion.1), channel_id=1, source_target_pairs={{0,24},{1,25},{2,26},{3,27},{4,28},{5,29},{6,30},{7,31},{8,0},{9,1... | collective-permute-start | bytes 196616 | tf_op jit(solution)/shard_map/ppermute | solution.py:27
  126.1 1.1 collective-permute-done.5
  129.2 3.4 %collective-permute-start.7 = (f32[128,128]{0,1:T(8,128)S(1)}, f32[128,128]{0,1:T(8,128)S(1)}, u32[]{:S(2)}, u32[]{:S(2)}) collective-permute-start(f32[128,128]{0,1:T(8,128)S(1)} %multiply_divide_fusion), channel_id=1, source_target_pairs={{0,32},{32,64},{64,96},{96,0},{1,33},{33,65},{65,97},{97,1},{2,34}... | collective-permute-start | bytes 196616 | tf_op jit(solution)/shard_map/ppermute | solution.py:38
  132.6 1.7 %collective-permute-start.8 = (f32[128,128]{0,1:T(8,128)S(1)}, f32[128,128]{0,1:T(8,128)S(1)}, u32[]{:S(2)}, u32[]{:S(2)}) collective-permute-start(f32[128,128]{0,1:T(8,128)S(1)} %multiply_divide_fusion), channel_id=1, source_target_pairs={{0,64},{32,96},{64,0},{96,32},{1,65},{33,97},{65,1},{97,33},{2,66}... | collective-permute-start | bytes 196616 | tf_op jit(solution)/shard_map/ppermute | solution.py:38
  134.3 2.5 %collective-permute-start.9 = (f32[128,128]{0,1:T(8,128)S(1)}, f32[128,128]{0,1:T(8,128)S(1)}, u32[]{:S(2)}, u32[]{:S(2)}) collective-permute-start(f32[128,128]{0,1:T(8,128)S(1)} %multiply_divide_fusion), channel_id=1, source_target_pairs={{0,96},{32,0},{64,32},{96,64},{1,97},{33,1},{65,33},{97,65},{2,98}... | collective-permute-start | bytes 196616 | tf_op jit(solution)/shard_map/ppermute | solution.py:38
  136.8 1.5 %collective-permute-done.8 = f32[128,128]{0,1:T(8,128)S(1)} collective-permute-done((f32[128,128]{0,1:T(8,128)S(1)}, f32[128,128]{0,1:T(8,128)S(1)}, u32[]{:S(2)}, u32[]{:S(2)}) %collective-permute-start.8) | collective-permute-done | bytes 65568 | tf_op jit(solution)/shard_map/ppermute | solution.py:38
  139.3 0.9 convolution_bitcast_fusion.1
  140.8 1.0 reshape.35
  (33 shorter events, 5.5 us)
Async XLA Ops:
  7.2 78.3 %all-gather.3.cloned.1.call-start = ((), (), s32[]{:S(2)}) async-start(), calls=%async_computation | async-start | bytes 17301504 | tf_op jit(solution)/shard_map/all_gather | solution.py:109
  16.0 11.3 %copy-start.3 = (f32[1,8,16,16]{3,2,1,0:T(8,128)S(1)}, f32[1,8,16,16]{3,2,1,0:T(8,128)}, u32[]{:S(2)}) copy-start(f32[1,8,16,16]{3,2,1,0:T(8,128)} %param.8) | copy-start | bytes 24580
  16.1 11.4 %copy-start.1 = (bf16[1,128,2048]{2,1,0:T(8,128)(2,1)S(1)}, bf16[1,128,2048]{2,1,0:T(8,128)(2,1)}, u32[]{:S(2)}) copy-start(bf16[1,128,2048]{2,1,0:T(8,128)(2,1)} %param.5) | copy-start | bytes 1572868
  16.1 69.4 %copy-start = (s32[1,4096]{1,0:T(1,128)S(1)}, s32[1,4096]{1,0:T(1,128)}, u32[]{:S(2)}) copy-start(s32[1,4096]{1,0:T(1,128)} %sec_j_ref.1) | copy-start | bytes 49156
  92.6 33.3 %copy-start.2 = (f32[128,128]{1,0:T(8,128)S(1)}, f32[128,128]{1,0:T(8,128)}, u32[]{:S(2)}) copy-start(f32[128,128]{1,0:T(8,128)} %param.9) | copy-start | bytes 196612
  97.9 2.5 %collective-permute-start = (f32[128,128]{0,1:T(8,128)S(1)}, f32[128,128]{0,1:T(8,128)S(1)}, u32[]{:S(2)}, u32[]{:S(2)}) collective-permute-start(f32[128,128]{0,1:T(8,128)S(1)} %convolution_bitcast_fusion), channel_id=1, source_target_pairs={{0,1},{1,0},{2,3},{3,2},{4,5},{5,4},{6,7},{7,6},{8,9},{9,8},{10,11... | collective-permute-start | bytes 196616 | tf_op jit(solution)/shard_map/ppermute | solution.py:27
  100.5 17.2 %collective-permute-start.1 = (f32[128,128]{0,1:T(8,128)S(1)}, f32[128,128]{0,1:T(8,128)S(1)}, u32[]{:S(2)}, u32[]{:S(2)}) collective-permute-start(f32[128,128]{0,1:T(8,128)S(1)} %add.52), channel_id=1, source_target_pairs={{0,2},{1,3},{2,4},{3,5},{4,6},{5,7},{6,0},{7,1},{8,10},{9,11},{10,... | collective-permute-start | bytes 196616 | tf_op jit(solution)/shard_map/ppermute | solution.py:27
  113.3 6.6 %collective-permute-start.2 = (f32[128,128]{0,1:T(8,128)S(1)}, f32[128,128]{0,1:T(8,128)S(1)}, u32[]{:S(2)}, u32[]{:S(2)}) collective-permute-start(f32[128,128]{0,1:T(8,128)S(1)} %add.52), channel_id=1, source_target_pairs={{0,4},{1,5},{2,6},{3,7},{4,0},{5,1},{6,2},{7,3},{8,12},{9,13},{10,... | collective-permute-start | bytes 196616 | tf_op jit(solution)/shard_map/ppermute | solution.py:27
  116.3 4.3 %collective-permute-start.3 = (f32[128,128]{0,1:T(8,128)S(1)}, f32[128,128]{0,1:T(8,128)S(1)}, u32[]{:S(2)}, u32[]{:S(2)}) collective-permute-start(f32[128,128]{0,1:T(8,128)S(1)} %add.52), channel_id=1, source_target_pairs={{0,6},{1,7},{2,0},{3,1},{4,2},{5,3},{6,4},{7,5},{8,14},{9,15},{10,... | collective-permute-start | bytes 196616 | tf_op jit(solution)/shard_map/ppermute | solution.py:27
  120.6 5.5 %collective-permute-start.4 = (f32[128,128]{0,1:T(8,128)S(1)}, f32[128,128]{0,1:T(8,128)S(1)}, u32[]{:S(2)}, u32[]{:S(2)}) collective-permute-start(f32[128,128]{0,1:T(8,128)S(1)} %add_add_fusion.1), channel_id=1, source_target_pairs={{0,8},{1,9},{2,10},{3,11},{4,12},{5,13},{6,14},{7,15},{8,16},{9,17... | collective-permute-start | bytes 196616 | tf_op jit(solution)/shard_map/ppermute | solution.py:27
  121.5 5.8 %collective-permute-start.5 = (f32[128,128]{0,1:T(8,128)S(1)}, f32[128,128]{0,1:T(8,128)S(1)}, u32[]{:S(2)}, u32[]{:S(2)}) collective-permute-start(f32[128,128]{0,1:T(8,128)S(1)} %add_add_fusion.1), channel_id=1, source_target_pairs={{0,16},{1,17},{2,18},{3,19},{4,20},{5,21},{6,22},{7,23},{8,24},{9,... | collective-permute-start | bytes 196616 | tf_op jit(solution)/shard_map/ppermute | solution.py:27
  123.4 4.4 %collective-permute-start.6 = (f32[128,128]{0,1:T(8,128)S(1)}, f32[128,128]{0,1:T(8,128)S(1)}, u32[]{:S(2)}, u32[]{:S(2)}) collective-permute-start(f32[128,128]{0,1:T(8,128)S(1)} %add_add_fusion.1), channel_id=1, source_target_pairs={{0,24},{1,25},{2,26},{3,27},{4,28},{5,29},{6,30},{7,31},{8,0},{9,1... | collective-permute-start | bytes 196616 | tf_op jit(solution)/shard_map/ppermute | solution.py:27
  129.2 7.6 %collective-permute-start.7 = (f32[128,128]{0,1:T(8,128)S(1)}, f32[128,128]{0,1:T(8,128)S(1)}, u32[]{:S(2)}, u32[]{:S(2)}) collective-permute-start(f32[128,128]{0,1:T(8,128)S(1)} %multiply_divide_fusion), channel_id=1, source_target_pairs={{0,32},{32,64},{64,96},{96,0},{1,33},{33,65},{65,97},{97,1},{2,34}... | collective-permute-start | bytes 196616 | tf_op jit(solution)/shard_map/ppermute | solution.py:38
  132.6 5.8 %collective-permute-start.8 = (f32[128,128]{0,1:T(8,128)S(1)}, f32[128,128]{0,1:T(8,128)S(1)}, u32[]{:S(2)}, u32[]{:S(2)}) collective-permute-start(f32[128,128]{0,1:T(8,128)S(1)} %multiply_divide_fusion), channel_id=1, source_target_pairs={{0,64},{32,96},{64,0},{96,32},{1,65},{33,97},{65,1},{97,33},{2,66}... | collective-permute-start | bytes 196616 | tf_op jit(solution)/shard_map/ppermute | solution.py:38
  134.3 4.4 %collective-permute-start.9 = (f32[128,128]{0,1:T(8,128)S(1)}, f32[128,128]{0,1:T(8,128)S(1)}, u32[]{:S(2)}, u32[]{:S(2)}) collective-permute-start(f32[128,128]{0,1:T(8,128)S(1)} %multiply_divide_fusion), channel_id=1, source_target_pairs={{0,96},{32,0},{64,32},{96,64},{1,97},{33,1},{65,33},{97,65},{2,98}... | collective-permute-start | bytes 196616 | tf_op jit(solution)/shard_map/ppermute | solution.py:38
Sparse Core Ops, SparseCore 0:
  10.2 75.1 all-gather.2
